TPU v7x, 256 devices: a whole 4x4x8 slice. The times are simulated.
256 devices in a mesh: dp: 32 (over x, z_hi, y), mp: 8 (over z_lo, core).
Axes of the slice: x: 4, y: 4, z: 8 (z_hi: 2, z_lo: 4; z = z_hi * 4 + z_lo), core: 2. Of those that a mesh axis runs over, the one named last changes fastest.
Arguments:
- store_rows: bfloat16 [8192, 8192], P('dp', 'mp'), may hold values from -6 to 6
- source_shard: int32 [1024], replicated, may hold values from 0 to 31, as said below
- source_row: int32 [1024], replicated, may hold values from 0 to 255
- state_len: int32 [32], replicated, may hold values from 1 to 64, 1024 in all
- visits: int32 [32], replicated, may hold values from 1 to 4095
- gain: bfloat16 [8192], P('mp'), may hold values from 0.5 to 1.5
- w_gate: bfloat16 [8192, 22016], P('mp', 'dp'), may hold values from -0.0625 to 0.0625
- w_up: bfloat16 [8192, 22016], P('mp', 'dp'), may hold values from -0.0625 to 0.0625
- w_down: bfloat16 [22016, 8192], P('dp', 'mp'), may hold values from -0.0390625 to 0.0390625
- upstream: bfloat16 [1024, 8192], P(None, 'mp'), may hold values from -0.375 to 0.375
Outputs:
- layer_out: bfloat16 [1024, 8192], P('dp', 'mp')
- grad_gate: bfloat16 [8192, 22016], P('mp', 'dp')
- grad_up: bfloat16 [8192, 22016], P('mp', 'dp')
- grad_down: bfloat16 [22016, 8192], P('dp', 'mp')
Inputs may be any that keep to these rules, and one draw needn't show every extreme that they name: `source_shard`: block b holds training rows b * 32 to (b + 1) * 32 - 1. No shard is named more than 4 times in one block nor more than 128 times in all; one shard, drawn from the seed, is named exactly 4 times in every block. `state_len`: the lengths sum to 1024.
All inputs are finite; a program needn't handle non-finite values.
Results may differ from a plain program's by a relative error of at most 0.017.
Values may be sent and summed in bfloat16 or wider, within the bound.
No kernel may reach another device: no remote copies, remote signals or barrier semaphores. Data moves between devices by JAX's collectives and lax.ppermute only.
A program may use at most 64 MiB of HBM per device.

v0:
```python
import jax
import jax.numpy as jnp
from jax import lax
from jax.sharding import PartitionSpec as P

D = 8192


epsilon = 1e-05


def pick_rows(store_rows, source_row, target, row_ids, slots):
    picked = jnp.zeros((slots,), jnp.int32).at[target].set(row_ids, mode="drop")
    filled = jnp.zeros((slots,), jnp.bool_).at[target].set(True, mode="drop")
    chosen = store_rows[source_row[picked]]
    return jnp.where(filled[:, None], chosen, jnp.zeros_like(chosen))


def shards(
    store_rows, source_shard, source_row, state_len, visits, gain, w_gate, w_up, w_down, upstream
):
    count_dp = lax.axis_size("dp")
    count_mp = lax.axis_size("mp")
    index_dp = lax.axis_index("dp")
    index_mp = lax.axis_index("mp")
    total_rows = source_shard.shape[0]
    block_rows = total_rows // count_dp
    share_rows = total_rows // count_mp
    pair_cap = max(block_rows // 8, 1)
    shard_cap = count_dp * pair_cap
    row_ids = jnp.arange(total_rows, dtype=jnp.int32)
    owned = source_shard == index_dp
    one_hot = (source_shard[:, None] == jnp.arange(count_dp, dtype=jnp.int32)[None, :]).astype(
        jnp.int32
    )
    before = jnp.cumsum(one_hot, axis=0) - one_hot
    shard_rank = jnp.sum(before * one_hot, axis=1)
    target = jnp.where(owned, shard_rank, shard_cap)
    outgoing = pick_rows(store_rows, source_row, target, row_ids, shard_cap)
    arrived = lax.all_gather(outgoing, "dp", axis=0, tiled=True)
    train_rows = arrived[source_shard * shard_cap + shard_rank]
    rows_float = train_rows.astype(jnp.float32)
    squares = jnp.sum(rows_float * rows_float, axis=1)
    scaled = (rows_float * gain.astype(jnp.float32)[None, :]).astype(jnp.bfloat16)
    share_first = index_mp * share_rows
    gate_term = jnp.dot(scaled, w_gate, preferred_element_type=jnp.float32)
    up_term = jnp.dot(scaled, w_up, preferred_element_type=jnp.float32)
    gate_total, up_total, square_total = lax.psum((gate_term, up_term, squares), "mp")
    inverse = lax.rsqrt(square_total / D + epsilon)
    gate_all = inverse[:, None] * gate_total
    up_all = inverse[:, None] * up_total
    hidden_all = (jax.nn.silu(gate_all) * up_all).astype(jnp.bfloat16)
    inverse_share = lax.dynamic_slice_in_dim(inverse, share_first, share_rows, 0)
    gate_share = lax.dynamic_slice_in_dim(gate_all, share_first, share_rows, 0)
    up_share = lax.dynamic_slice_in_dim(up_all, share_first, share_rows, 0)
    block = hidden_all
    down_block = lax.psum_scatter(
        jnp.dot(block, w_down, preferred_element_type=jnp.float32).astype(jnp.bfloat16),
        "dp",
        scatter_dimension=0,
        tiled=True,
    ).astype(jnp.float32)
    own_rows = lax.dynamic_slice_in_dim(rows_float, index_dp * block_rows, block_rows, 0)
    layer_out = (own_rows + down_block).astype(jnp.bfloat16)
    ends = jnp.cumsum(state_len)
    starts = ends - state_len
    member = ((row_ids[:, None] >= starts[None, :]) & (row_ids[:, None] < ends[None, :])).astype(
        jnp.float32
    )
    importance = jnp.log1p(visits.astype(jnp.float32))
    per_state = total_rows * importance / (state_len.astype(jnp.float32) * jnp.sum(importance))
    row_weight = jnp.sum(member * per_state[None, :], axis=1)
    out_grad = (upstream.astype(jnp.float32) * row_weight[:, None]).astype(jnp.bfloat16)
    grad_down = lax.dot_general(
        hidden_all, out_grad, (((0,), (0,)), ((), ())), preferred_element_type=jnp.float32
    ).astype(jnp.bfloat16)
    block = out_grad
    grad_hidden = lax.psum_scatter(
        lax.dot_general(
            block, w_down, (((1,), (1,)), ((), ())), preferred_element_type=jnp.float32
        ).astype(jnp.bfloat16),
        "mp",
        scatter_dimension=0,
        tiled=True,
    ).astype(jnp.float32)
    sigmoid_gate = jax.nn.sigmoid(gate_share)
    gate_delta = (
        inverse_share[:, None]
        * grad_hidden
        * up_share
        * sigmoid_gate
        * (1.0 + gate_share * (1.0 - sigmoid_gate))
    ).astype(jnp.bfloat16)
    up_delta = (inverse_share[:, None] * grad_hidden * gate_share * sigmoid_gate).astype(
        jnp.bfloat16
    )
    block = scaled
    gate_add = lax.dot_general(
        block,
        lax.all_gather(gate_delta, "mp", axis=0, tiled=True),
        (((0,), (0,)), ((), ())),
        preferred_element_type=jnp.float32,
    )
    up_add = lax.dot_general(
        block,
        lax.all_gather(up_delta, "mp", axis=0, tiled=True),
        (((0,), (0,)), ((), ())),
        preferred_element_type=jnp.float32,
    )
    return (layer_out, gate_add.astype(jnp.bfloat16), up_add.astype(jnp.bfloat16), grad_down)


def solution(mesh):
    in_specs = (
        P("dp", "mp"),
        P(),
        P(),
        P(),
        P(),
        P("mp"),
        P("mp", "dp"),
        P("mp", "dp"),
        P("dp", "mp"),
        P(None, "mp"),
    )
    out_specs = (P("dp", "mp"), P("mp", "dp"), P("mp", "dp"), P("dp", "mp"))
    return jax.shard_map(shards, mesh=mesh, in_specs=in_specs, out_specs=out_specs, check_vma=False)
```

profile of v0, /device:TPU:32, one launch (start us, length us, event | category | flops | bytes accessed | tf_op | source)
XLA Modules:
  0.0 596.2 jit_solution(9465282977196284565)
XLA Ops:
  8.1 0.8 fusion.5
  8.9 9.0 %reduce-window.18 = s32[32,8,128]{2,1,0:T(8,128)S(1)} reduce-window(s32[32,8,128]{2,1,0:T(8,128)S(1)} %fusion.5, s32[]{:T(128)} %constant.20.clone.1), window={size=1x1x128 pad=0_0x0_0x127_0}, to_apply=%region_0.0 | reduce-window | flops 4161536 | bytes 262148 | tf_op jit(solution)/shard_map/reduce-window
  17.9 0.1 slice.14
  18.0 0.1 copy.21
  18.2 0.1 copy.22
  18.3 0.1 broadcast_add_fusion
  18.4 0.7 fusion.4
  19.1 0.7 fusion.7
  19.8 4.3 scatter_custom_fusion.1
  24.2 1.6 gather_fusion
  25.8 0.9 gather_fusion.1
  26.7 4.3 scatter_custom_fusion
  31.0 0.8 broadcast_select_fusion
  31.8 0.0 reduce-scatter.7.cloned.1.call-start
  31.9 0.1 copy.23
  32.0 0.1 reduce-window.20
  32.0 0.1 reduce
  32.2 0.6 fusion.11
  32.8 0.7 multiply_divide_fusion
  33.4 0.1 select_reduce_fusion
  33.6 3.3 convolution_convert_fusion.4
  36.9 1.6 copy.24
  38.5 0.2 all-reduce.3.cloned.1.call-start
  38.8 150.9 %all-gather.4.cloned.1.call-done = bf16[4096,1024]{1,0:T(8,128)(2,1)} async-done(((bf16[128,1024]{1,0:T(8,128)(2,1)}), bf16[4096,1024]{1,0:T(8,128)(2,1)}) %all-gather.4.cloned.1.call-update) | async-done | bytes 8388624 | tf_op jit(solution)/shard_map/all_gather | solution.py:40
  189.6 9.4 %gather_fusion.2 = bf16[1024,1024]{1,0:T(8,128)(2,1)S(1)} fusion(bf16[4096,1024]{1,0:T(8,128)(2,1)} %all-gather.4.cloned.1.call-done, s32[1024]{0:T(1024)S(1)} %get-tuple-element.11), kind=kCustom, calls=%fused_computation.2 | custom fusion | bytes 4198400 | tf_op jit(solution)/shard_map/gather | solution.py:41
  199.1 4.7 fusion.1
  203.8 3.2 fusion
  207.0 0.0 all-gather.8.cloned.1.call-start
  207.1 1.7 copy.25
  208.9 0.5 multiply_reduce_fusion
  209.3 11.4 %psum.21 = f32[1024]{0:T(1024)S(1)} all-reduce(f32[1024]{0:T(1024)S(1)} %multiply_reduce_fusion), channel_id=1, replica_groups=mesh['dp'=32,'mp'=8] {'mp'}, use_global_device_ids=true, to_apply=%region_6.7 | all-reduce | flops 1024 | bytes 8192 | tf_op jit(solution)/shard_map/psum | solution.py:48
  220.8 0.1 dynamic_slice.13
  220.9 114.4 %all-reduce.3.cloned.1.call-done = (f32[1024,688]{0,1:T(8,128)}, f32[1024,688]{0,1:T(8,128)}) async-done(((f32[1024,688]{0,1:T(8,128)}, f32[1024,688]{0,1:T(8,128)}), (f32[1024,688]{0,1:T(8,128)}, f32[1024,688]{0,1:T(8,128)})) %all-reduce.3.cloned.1.call-update) | async-done | bytes 5636112 | tf_op jit(solution)/shard_map/psum | solution.py:48
  335.2 4.8 multiply_convert_fusion.2
  340.0 0.9 multiply_convert_fusion.9
  341.0 0.0 all-gather.6.cloned.1.call-start
  341.0 0.7 all-gather.6.cloned.1.call-update
  341.7 0.3 reduce-scatter.5.cloned.1.call-start
  342.0 4.5 convolution_convert_fusion
  346.5 2.5 convert_element_type.64
  349.1 0.8 copy-done.7
  349.9 2.8 convolution_convert_fusion.3
  352.8 24.3 %all-gather.8.cloned.1.call-done = bf16[1024,688]{0,1:T(8,128)(2,1)} async-done(((bf16[128,688]{0,1:T(8,128)(2,1)}), bf16[1024,688]{0,1:T(8,128)(2,1)}) %all-gather.8.cloned.1.call-update) | async-done | bytes 1409040 | tf_op jit(solution)/shard_map/all_gather | solution.py:106
  377.0 4.1 convolution_convert_fusion.1
  381.1 34.0 %all-gather.6.cloned.1.call-done = bf16[1024,688]{0,1:T(8,128)(2,1)} async-done(((bf16[128,688]{0,1:T(8,128)(2,1)}), bf16[1024,688]{0,1:T(8,128)(2,1)}) %all-gather.6.cloned.1.call-update) | async-done | bytes 1409040 | tf_op jit(solution)/shard_map/all_gather | solution.py:100
  415.1 4.1 convolution_convert_fusion.2
  419.2 167.8 %reduce-scatter.5.cloned.1.call-done = bf16[32,1024]{1,0:T(8,128)(2,1)} async-done(((bf16[1024,1024]{1,0:T(8,128)(2,1)}), bf16[32,1024]{1,0:T(8,128)(2,1)}) %reduce-scatter.5.cloned.1.call-update) | async-done | bytes 65552 | tf_op jit(solution)/shard_map/reduce_scatter | solution.py:57
  587.0 1.6 add_convert_fusion
  (35 shorter events, 0.3 us)
Async XLA Ops:
  8.0 25.6 %copy-start = (bf16[688,1024]{1,0:T(8,128)(2,1)S(1)}, bf16[688,1024]{1,0:T(8,128)(2,1)}, u32[]{:S(2)}) copy-start(bf16[688,1024]{1,0:T(8,128)(2,1)} %param.18) | copy-start | bytes 4227076
  8.0 17.8 %copy-start.1 = (bf16[256,1024]{1,0:T(8,128)(2,1)S(1)}, bf16[256,1024]{1,0:T(8,128)(2,1)}, u32[]{:S(2)}) copy-start(bf16[256,1024]{1,0:T(8,128)(2,1)} %param.10) | copy-start | bytes 1572868
  8.0 181.6 %all-gather.4.cloned.1.call-start = ((), (), s32[]{:S(2)}) async-start(), calls=%async_computation.2 | async-start | bytes 8650752 | tf_op jit(solution)/shard_map/all_gather | solution.py:40
  18.2 13.7 %copy-start.5 = (s32[32]{0:T(128)S(1)}, s32[32]{0:T(128)}, u32[]{:S(2)}) copy-start(s32[32]{0:T(128)} %param.13) | copy-start | bytes 388
  18.3 13.9 %copy-start.6 = (s32[32]{0:T(128)S(1)}, s32[32]{0:T(128)}, u32[]{:S(2)}) copy-start(s32[32]{0:T(128)} %param.14) | copy-start | bytes 388
  31.8 175.3 %reduce-scatter.7.cloned.1.call-start = ((), (), s32[]{:S(2)}) async-start(), calls=%async_computation.6 | async-start | bytes 1769472
  36.9 1.8 copy-start.4
  38.5 296.7 %all-reduce.3.cloned.1.call-start = ((), (), s32[]{:S(2)}) async-start(), calls=%async_computation.7 | async-start | bytes 11272192 | tf_op jit(solution)/shard_map/psum | solution.py:48
  199.0 4.7 copy-start.8
  207.0 170.0 %all-gather.8.cloned.1.call-start = ((), (), s32[]{:S(2)}) async-start(), calls=%async_computation.5 | async-start | bytes 1585152 | tf_op jit(solution)/shard_map/all_gather | solution.py:106
  335.2 4.8 copy-start.3
  341.0 74.2 %all-gather.6.cloned.1.call-start = ((), (), s32[]{:S(2)}) async-start(), calls=%async_computation.4 | async-start | bytes 1585152 | tf_op jit(solution)/shard_map/all_gather | solution.py:100
  341.7 245.3 %reduce-scatter.5.cloned.1.call-start = ((), (), s32[]{:S(2)}) async-start(), calls=%async_computation.3 | async-start | bytes 2162688 | tf_op jit(solution)/shard_map/reduce_scatter | solution.py:57
  346.5 2.6 copy-start.2
  346.5 3.4 copy-start.7
Sparse Core Ops, SparseCore 0:
  32.0 157.5 all-gather.3
  346.6 240.3 reduce-scatter.4
Sparse Core Ops, SparseCore 1:
  38.6 53.0 reduce-scatter.6
  207.1 128.0 all-reduce.2
  341.0 35.9 all-gather.7
  379.3 35.7 all-gather.5
where the time goes:
time: 597 us; the launch traced here: 596 us
  waiting for transfers between devices  492 us (82%)
  matrix products  26.8 us (4%)
  local copies, waits for them, and re-layouts  25.2 us (4%)
  other arithmetic  24.1 us (4%)
  between operations  15.9 us (3%)
  blocking collectives  11.4 us (2%)
    reduce_scatter x1, waiting for transfers between devices, shards(): lax.psum_scatter(jnp.dot(block, w_down, preferred_element_type=jnp.float3...  168 us
    all_gather x1, waiting for transfers between devices, shards(): arrived = lax.all_gather(outgoing, 'dp', axis=0, tiled=True)  151 us
    psum x1, waiting for transfers between devices, shards(): lax.psum((gate_term, up_term, squares), 'mp')  114 us
    all_gather x1, waiting for transfers between devices, shards(): lax.all_gather(gate_delta, 'mp', axis=0, tiled=True)  34 us
    all_gather x1, waiting for transfers between devices, shards(): lax.all_gather(up_delta, 'mp', axis=0, tiled=True)  24.3 us
  transfers between devices with their start and end apart: 6, of which 5 were waited for; matrix products, arithmetic and copies ran while one was open for 7% of the time, Pallas kernels for 0%

commit v1 on v0

v1 whole, which is shorter than its diff:
```python
import jax
import jax.numpy as jnp
from jax import lax
from jax.sharding import Mesh
from jax.sharding import PartitionSpec as P

D = 8192

epsilon = 1e-05

DP = ("x", "zh", "y")
MP = ("zl", "c")


def shards(
    store_rows, source_shard, source_row, state_len, visits, gain, w_gate, w_up, w_down, upstream
):
    f32, bf16 = jnp.float32, jnp.bfloat16
    count_dp = 1
    for name in DP:
        count_dp *= lax.axis_size(name)
    index_dp = lax.axis_index(DP)
    total_rows = source_shard.shape[0]
    block_rows = total_rows // count_dp
    pair_cap = max(block_rows // 8, 1)
    store_dev = store_rows.shape[0]
    hidden_dev = w_gate.shape[1]

    shard = source_shard.reshape(count_dp, block_rows)
    srow = source_row.reshape(count_dp, block_rows)
    same = shard[:, :, None] == shard[:, None, :]
    t_ids = jnp.arange(block_rows, dtype=jnp.int32)
    earlier = t_ids[None, :] < t_ids[:, None]
    rank = jnp.sum((same & earlier[None]).astype(jnp.int32), axis=2)

    owned = shard == index_dp
    slots = jnp.arange(pair_cap, dtype=jnp.int32)
    hit = owned[:, :, None] & (rank[:, :, None] == slots[None, None, :])
    slot_row = jnp.sum(jnp.where(hit, srow[:, :, None] + 1, 0), axis=1) - 1
    pick_out = (
        slot_row.reshape(count_dp * pair_cap)[:, None]
        == jnp.arange(store_dev, dtype=jnp.int32)[None, :]
    ).astype(bf16)
    outgoing = jnp.dot(pick_out, store_rows, preferred_element_type=f32).astype(bf16)
    received = lax.all_to_all(outgoing, DP, 0, 0, tiled=True)

    my_shard = lax.dynamic_index_in_dim(shard, index_dp, 0, keepdims=False)
    my_rank = lax.dynamic_index_in_dim(rank, index_dp, 0, keepdims=False)
    pick_in = (
        (my_shard * pair_cap + my_rank)[:, None]
        == jnp.arange(count_dp * pair_cap, dtype=jnp.int32)[None, :]
    ).astype(bf16)
    own_rows = jnp.dot(pick_in, received, preferred_element_type=f32).astype(bf16)

    train_rows = own_rows
    for name in reversed(DP):
        train_rows = lax.all_gather(train_rows, name, axis=0, tiled=True)

    rows_float = train_rows.astype(f32)
    squares = jnp.sum(rows_float * rows_float, axis=1)
    scaled = (rows_float * gain.astype(f32)[None, :]).astype(bf16)
    gate_term = jnp.dot(scaled, w_gate, preferred_element_type=f32)
    up_term = jnp.dot(scaled, w_up, preferred_element_type=f32)
    packed = jnp.concatenate([gate_term, up_term, squares[:, None]], axis=1)
    total = lax.psum(packed, MP)
    gate_total = total[:, :hidden_dev]
    up_total = total[:, hidden_dev : 2 * hidden_dev]
    square_total = total[:, 2 * hidden_dev]
    inverse = lax.rsqrt(square_total / D + epsilon)
    gate_all = inverse[:, None] * gate_total
    up_all = inverse[:, None] * up_total
    hidden_all = (jax.nn.silu(gate_all) * up_all).astype(bf16)

    down_part = jnp.dot(hidden_all, w_down, preferred_element_type=f32).astype(bf16)
    down_in = lax.all_to_all(down_part, DP, 0, 0, tiled=True)
    down_block = jnp.sum(
        down_in.reshape(count_dp, block_rows, down_in.shape[1]).astype(f32), axis=0
    )
    layer_out = (own_rows.astype(f32) + down_block).astype(bf16)

    row_ids = jnp.arange(total_rows, dtype=jnp.int32)
    ends = jnp.cumsum(state_len)
    starts = ends - state_len
    member = ((row_ids[:, None] >= starts[None, :]) & (row_ids[:, None] < ends[None, :])).astype(
        f32
    )
    importance = jnp.log1p(visits.astype(f32))
    per_state = total_rows * importance / (state_len.astype(f32) * jnp.sum(importance))
    row_weight = jnp.sum(member * per_state[None, :], axis=1)
    out_grad = (upstream.astype(f32) * row_weight[:, None]).astype(bf16)
    grad_down = lax.dot_general(
        hidden_all, out_grad, (((0,), (0,)), ((), ())), preferred_element_type=f32
    ).astype(bf16)
    hidden_term = lax.dot_general(
        out_grad, w_down, (((1,), (1,)), ((), ())), preferred_element_type=f32
    ).astype(bf16)
    grad_hidden = lax.psum(hidden_term, MP).astype(f32)
    sigmoid_gate = jax.nn.sigmoid(gate_all)
    gate_delta = (
        inverse[:, None]
        * grad_hidden
        * up_all
        * sigmoid_gate
        * (1.0 + gate_all * (1.0 - sigmoid_gate))
    ).astype(bf16)
    up_delta = (inverse[:, None] * grad_hidden * gate_all * sigmoid_gate).astype(bf16)
    grad_gate = lax.dot_general(
        scaled, gate_delta, (((0,), (0,)), ((), ())), preferred_element_type=f32
    ).astype(bf16)
    grad_up = lax.dot_general(
        scaled, up_delta, (((0,), (0,)), ((), ())), preferred_element_type=f32
    ).astype(bf16)
    return (layer_out, grad_gate, grad_up, grad_down)


def solution(mesh):
    sizes = dict(zip(mesh.axis_names, mesh.devices.shape))
    count_mp = sizes["mp"]
    count_dp = sizes["dp"]
    zh = 2
    y = 4
    x = count_dp // (zh * y)
    c = 2
    zl = count_mp // c
    view = Mesh(mesh.devices.reshape(x, zh, y, zl, c), DP + MP)
    in_specs = (
        P(DP, MP),
        P(),
        P(),
        P(),
        P(),
        P(MP),
        P(MP, DP),
        P(MP, DP),
        P(DP, MP),
        P(None, MP),
    )
    out_specs = (P(DP, MP), P(MP, DP), P(MP, DP), P(DP, MP))
    return jax.shard_map(shards, mesh=view, in_specs=in_specs, out_specs=out_specs, check_vma=False)
```

time: 597 us -> 382 us (0.64)
  waiting for transfers between devices: 492 us -> 263 us
  starting transfers between devices: 0.66 us -> 26.5 us
  local copies, waits for them, and re-layouts: 25.2 us -> 3.4 us
  blocking collectives: 11.4 us -> 25 us
  other arithmetic: 24.1 us -> 14.4 us
    all_gather x3 -> x1, waiting for transfers between devices: 209 us -> 27.8 us  [shards(): train_rows = lax.all_gather(train_rows, name, axis=0, tiled=True)]
    reduce_scatter x1 -> x0, waiting for transfers between devices: 168 us -> none  [shards(): lax.psum_scatter(jnp.dot(block, w_down, preferred_element_type=jnp.float3...]
    psum x1 -> x2, waiting for transfers between devices: 114 us -> 220 us  [the longest x1 133 us: shards(): total = lax.psum(packed, MP)]
    all_to_all x0 -> x2, starting transfers between devices: none -> 26.2 us  [the longest x1 13.1 us: shards(): down_in = lax.all_to_all(down_part, DP, 0, 0, tiled=True)]
    all_gather x0 -> x2, blocking collectives: none -> 25 us  [shards(): train_rows = lax.all_gather(train_rows, name, axis=0, tiled=True)]
    all_to_all x0 -> x2, waiting for transfers between devices: none -> 15.8 us  [the longest x1 15.8 us: shards(): received = lax.all_to_all(outgoing, DP, 0, 0, tiled=True)]
    gather x3 -> x0, local copies, waits for them, and re-layouts: 11.9 us -> none  [the longest x1 9.43 us: shards(): train_rows = arrived[source_shard * shard_cap + shard_rank]]
    psum x1 -> x0, blocking collectives: 11.4 us -> none  [shards(): lax.psum((gate_term, up_term, squares), 'mp')]
  transfers between devices with their start and end apart: 6 -> 5, of which waited for: 5 -> 4; matrix products, arithmetic and copies ran while one was open for 7% -> 6% of each run, Pallas kernels for 0% -> 0%
where the time goes in v1:
time: 382 us; the launch traced here: 378 us
  waiting for transfers between devices  263 us (69%)
  matrix products  31.4 us (8%)
  starting transfers between devices  26.5 us (7%)
  blocking collectives  25 us (7%)
  other arithmetic  14.4 us (4%)
  between operations  14 us (4%)
    psum x1, waiting for transfers between devices, shards(): total = lax.psum(packed, MP)  133 us
    psum x1, waiting for transfers between devices, shards(): grad_hidden = lax.psum(hidden_term, MP).astype(f32)  87.1 us
    all_gather x1, waiting for transfers between devices, shards(): train_rows = lax.all_gather(train_rows, name, axis=0, tiled=True)  27.8 us
    all_gather x2, blocking collectives, shards(): train_rows = lax.all_gather(train_rows, name, axis=0, tiled=True)  25 us
    all_to_all x1, waiting for transfers between devices, shards(): received = lax.all_to_all(outgoing, DP, 0, 0, tiled=True)  15.8 us
    all_to_all x1, starting transfers between devices, shards(): down_in = lax.all_to_all(down_part, DP, 0, 0, tiled=True)  13.1 us
    all_to_all x1, starting transfers between devices, shards(): received = lax.all_to_all(outgoing, DP, 0, 0, tiled=True)  13 us
  transfers between devices with their start and end apart: 5, of which 4 were waited for; matrix products, arithmetic and copies ran while one was open for 6% of the time, Pallas kernels for 0%

profile of v1, /device:TPU:32, one launch (start us, length us, event | category | flops | bytes accessed | tf_op | source)
XLA Modules:
  0.0 378.0 jit_solution(1981180116354993840)
XLA Ops:
  7.2 0.0 copy-start
  7.2 0.9 reshape.93
  8.1 0.8 convert_reduce_fusion.1
  8.9 0.7 broadcast_add_fusion
  9.6 0.1 add.70
  9.6 0.1 select_reduce_fusion.1
  9.8 0.1 copy.16
  9.9 0.1 sub.13
  10.0 1.3 convolution_convert_fusion.5
  11.3 0.0 copy-start.8
  11.3 0.8 all_to_all.14
  12.1 13.0 %all-to-all-start = ((bf16[32,4,1024]{2,1,0:T(4,128)(2,1)}), bf16[32,4,1024]{2,1,0:T(4,128)(2,1)S(1)}, u32[]{:S(2)}, u32[]{:S(2)}) async-start(bf16[32,4,1024]{2,1,0:T(4,128)(2,1)} %all_to_all.14), calls=%async_computation | async-start | bytes 524288 | tf_op jit(solution)/shard_map/all_to_all | solution.py:45
  25.2 0.0 all-gather.2.cloned.1.call-start
  25.3 15.8 %all-to-all-done = bf16[32,4,1024]{2,1,0:T(4,128)(2,1)S(1)} async-done(((bf16[32,4,1024]{2,1,0:T(4,128)(2,1)}), bf16[32,4,1024]{2,1,0:T(4,128)(2,1)S(1)}, u32[]{:S(2)}, u32[]{:S(2)}) %all-to-all-start) | async-done | bytes 262176 | tf_op jit(solution)/shard_map/all_to_all | solution.py:45
  41.0 0.1 all_to_all.16
  41.1 0.2 convolution_convert_fusion.6
  41.3 0.6 copy-done.4
  42.0 12.2 %all_gather.9 = bf16[128,1024]{1,0:T(8,128)(2,1)S(1)} all-gather(bf16[32,1024]{1,0:T(8,128)(2,1)S(1)} %convolution_convert_fusion.6), channel_id=1, replica_groups=mesh['x'=4,'zh'=2,'y'=4,'zl'=4,'c'=2] {'y'}, dimensions={0}, use_global_device_ids=true | all-gather | bytes 327680 | tf_op jit(solution)/shard_map/all_gather | solution.py:57
  54.2 12.7 %all_gather.10 = bf16[256,1024]{1,0:T(8,128)(2,1)} all-gather(bf16[128,1024]{1,0:T(8,128)(2,1)S(1)} %all_gather.9), channel_id=1, replica_groups=mesh['x'=4,'zh'=2,'y'=4,'zl'=4,'c'=2] {'zh'}, dimensions={0}, use_global_device_ids=true | all-gather | bytes 786432 | tf_op jit(solution)/shard_map/all_gather | solution.py:57
  66.9 0.0 all-gather.2.cloned.1.call-update
  67.0 0.0 all-reduce.3.cloned.1.call-start
  67.0 27.8 %all-gather.2.cloned.1.call-done = bf16[1024,1024]{1,0:T(8,128)(2,1)} async-done(((bf16[256,1024]{1,0:T(8,128)(2,1)}), bf16[1024,1024]{1,0:T(8,128)(2,1)}) %all-gather.2.cloned.1.call-update) | async-done | bytes 2097168 | tf_op jit(solution)/shard_map/all_gather | solution.py:57
  94.9 2.1 fusion.1
  97.0 3.4 fusion.4
  100.4 1.7 fusion.6
  102.1 3.0 pad_maximum_fusion
  105.1 0.0 all-reduce.3.cloned.1.call-update
  105.1 0.6 copy-done.6
  105.8 0.1 copy.17
  105.8 0.1 reduce-window.8
  105.9 0.1 reduce
  106.0 132.6 %all-reduce.3.cloned.1.call-done = f32[1024,1377]{0,1:T(8,128)} async-done(((f32[1024,1377]{0,1:T(8,128)}), f32[1024,1377]{0,1:T(8,128)}) %all-reduce.3.cloned.1.call-update) | async-done | bytes 5640208 | tf_op jit(solution)/shard_map/psum | solution.py:65
  238.6 0.8 fusion.13
  239.4 3.5 multiply_convert_fusion.3
  242.9 3.2 convolution_convert_fusion
  246.1 13.1 %all-to-all-start.1 = ((bf16[32,32,1024]{2,1,0:T(8,128)(2,1)}), bf16[32,32,1024]{2,1,0:T(8,128)(2,1)S(1)}, u32[]{:S(2)}, u32[]{:S(2)}) async-start(bf16[32,32,1024]{2,1,0:T(8,128)(2,1)} %bitcast.14), calls=%async_computation.1 | async-start | bytes 4194304 | tf_op jit(solution)/shard_map/all_to_all | solution.py:75
  259.2 0.2 all-reduce.5.cloned.1.call-start
  259.5 0.6 fusion.14
  260.1 0.7 multiply_divide_fusion
  260.7 0.1 select_reduce_fusion
  260.8 4.4 %convolution_convert_fusion.4 = bf16[1024,688]{0,1:T(8,128)(2,1)} fusion(bf16[688,1024]{1,0:T(8,128)(2,1)S(1)} %copy-done, bf16[1024,1024]{1,0:T(8,128)(2,1)} %param.19, f32[1024]{0:T(1024)S(1)} %select_reduce_fusion), kind=kOutput, calls=%fused_computation.18 | convolution fusion | flops 1446690816 | bytes 4919296 | tf_op jit(solution)/shard_map/dot_general | solution.py:94
  265.2 0.0 all-reduce.5.cloned.1.call-update
  265.3 4.9 %convolution_convert_fusion.3 = bf16[688,1024]{1,0:T(8,128)(2,1)} fusion(bf16[1024,688]{0,1:T(8,128)(2,1)} %copy-done.3, bf16[1024,1024]{1,0:T(8,128)(2,1)} %param.19, f32[1024]{0:T(1024)S(1)} %select_reduce_fusion), kind=kOutput, calls=%fused_computation.17 | convolution fusion | flops 1446690816 | bytes 4919296 | tf_op jit(solution)/shard_map/dot_general | solution.py:91
  270.1 87.1 %all-reduce.5.cloned.1.call-done = bf16[1024,688]{0,1:T(8,128)(2,1)} async-done(((bf16[1024,688]{0,1:T(8,128)(2,1)}), bf16[1024,688]{0,1:T(8,128)(2,1)}) %all-reduce.5.cloned.1.call-update) | async-done | bytes 1409040 | tf_op jit(solution)/shard_map/psum | solution.py:97
  357.3 6.1 %convolution_convert_fusion.1 = bf16[1024,688]{0,1:T(8,128)(2,1)} fusion(bf16[1024,688]{0,1:T(8,128)(2,1)} %all-reduce.5.cloned.1.call-done, f32[1024,1377]{0,1:T(8,128)} %all-reduce.3.cloned.1.call-done, f32[1024]{0:T(1024)S(1)} %bitcast.17, bf16[1024,1024]{1,0:T(8,128)(2,1)} %all-gather.2.cloned.1.call-done, f32[1024]{0:T(1024)S(1)} %convert_element_type.74), kind=kOutput, calls=%fused_computation.15 | convolution fusion | flops 1453031424 | bytes 7741440 | tf_op jit(solution)/shard_map/dot_general | solution.py:110
  363.3 6.3 %convolution_convert_fusion.2 = bf16[1024,688]{0,1:T(8,128)(2,1)} fusion(bf16[1024,688]{0,1:T(8,128)(2,1)S(1)} %copy-done.10, f32[1024,1377]{0,1:T(8,128)} %all-reduce.3.cloned.1.call-done, f32[1024]{0:T(1024)S(1)} %bitcast.18, bf16[1024,1024]{1,0:T(8,128)(2,1)S(1)} %copy-done.2, f32[1024]{0:T(1024)S(1)} %convert_element_type.74), kind=kOutput, calls=%fused_computation.16 | convolution fusion | flops 1456553984 | bytes 10559488 | tf_op jit(solution)/shard_map/dot_general | solution.py:107
  369.6 0.4 convert_reduce_fusion
  370.0 1.5 add_convert_fusion
  (25 shorter events, 0.1 us)
Async XLA Ops:
  7.2 235.7 %copy-start = (bf16[688,1024]{1,0:T(8,128)(2,1)S(1)}, bf16[688,1024]{1,0:T(8,128)(2,1)}, u32[]{:S(2)}) copy-start(bf16[688,1024]{1,0:T(8,128)(2,1)} %param.18) | copy-start | bytes 4227076
  7.2 59.8 %copy-start.5 = (bf16[1024]{0:T(1024)(128)(2,1)S(1)}, bf16[1024]{0:T(1024)(128)(2,1)}, u32[]{:S(2)}) copy-start(bf16[1024]{0:T(1024)(128)(2,1)} %param.15) | copy-start | bytes 6148
  11.3 85.6 %copy-start.8 = (bf16[1024,688]{0,1:T(8,128)(2,1)S(1)}, bf16[1024,688]{0,1:T(8,128)(2,1)}, u32[]{:S(2)}) copy-start(bf16[1024,688]{0,1:T(8,128)(2,1)} %param.17) | copy-start | bytes 4227076
  12.1 28.9 %all-to-all-start = ((bf16[32,4,1024]{2,1,0:T(4,128)(2,1)}), bf16[32,4,1024]{2,1,0:T(4,128)(2,1)S(1)}, u32[]{:S(2)}, u32[]{:S(2)}) async-start(bf16[32,4,1024]{2,1,0:T(4,128)(2,1)} %all_to_all.14), calls=%async_computation | async-start | bytes 524288 | tf_op jit(solution)/shard_map/all_to_all | solution.py:45
  25.2 69.7 %all-gather.2.cloned.1.call-start = ((), (), s32[]{:S(2)}) async-start(), calls=%async_computation.2 | async-start | bytes 2621440 | tf_op jit(solution)/shard_map/all_gather | solution.py:57
  41.3 0.6 copy-start.4
  67.0 171.6 %all-reduce.3.cloned.1.call-start = ((), (), s32[]{:S(2)}) async-start(), calls=%async_computation.3 | async-start | bytes 11337728 | tf_op jit(solution)/shard_map/psum | solution.py:65
  96.9 3.4 copy-start.1
  97.0 3.4 copy-start.9
  105.1 0.7 copy-start.6
  242.9 3.2 copy-start.3
  246.1 13.4 %copy-start.7 = (s32[32]{0:T(128)S(1)}, s32[32]{0:T(128)}, u32[]{:S(2)}) copy-start(s32[32]{0:T(128)} %param.14) | copy-start | bytes 388
  246.1 123.6 %all-to-all-start.1 = ((bf16[32,32,1024]{2,1,0:T(8,128)(2,1)}), bf16[32,32,1024]{2,1,0:T(8,128)(2,1)S(1)}, u32[]{:S(2)}, u32[]{:S(2)}) async-start(bf16[32,32,1024]{2,1,0:T(8,128)(2,1)} %bitcast.14), calls=%async_computation.1 | async-start | bytes 4194304 | tf_op jit(solution)/shard_map/all_to_all | solution.py:75
  259.2 98.0 %all-reduce.5.cloned.1.call-start = ((), (), s32[]{:S(2)}) async-start(), calls=%async_computation.4 | async-start | bytes 2818048 | tf_op jit(solution)/shard_map/psum | solution.py:97
  357.3 6.1 %copy-start.2 = (bf16[1024,1024]{1,0:T(8,128)(2,1)S(1)}, bf16[1024,1024]{1,0:T(8,128)(2,1)}, u32[]{:S(2)}) copy-start(bf16[1024,1024]{1,0:T(8,128)(2,1)} %all-gather.2.cloned.1.call-done) | copy-start | bytes 6291460
  357.3 6.1 %copy-start.10 = (bf16[1024,688]{0,1:T(8,128)(2,1)S(1)}, bf16[1024,688]{0,1:T(8,128)(2,1)}, u32[]{:S(2)}) copy-start(bf16[1024,688]{0,1:T(8,128)(2,1)} %all-reduce.5.cloned.1.call-done) | copy-start | bytes 4227076
Sparse Core Ops, SparseCore 0:
  67.1 27.7 all-gather.1
  105.2 133.3 all-reduce.2
  265.4 91.8 all-reduce.4

commit v2 on v1

--- a/solution.py
+++ b/solution.py
@@ -12,7 +12,7 @@
 MP = ("zl", "c")
 
 
-def shards(
+def body(
     store_rows, source_shard, source_row, state_len, visits, gain, w_gate, w_up, w_down, upstream
 ):
     f32, bf16 = jnp.float32, jnp.bfloat16
@@ -61,8 +61,8 @@
     scaled = (rows_float * gain.astype(f32)[None, :]).astype(bf16)
     gate_term = jnp.dot(scaled, w_gate, preferred_element_type=f32)
     up_term = jnp.dot(scaled, w_up, preferred_element_type=f32)
-    packed = jnp.concatenate([gate_term, up_term, squares[:, None]], axis=1)
-    total = lax.psum(packed, MP)
+    packed = jnp.concatenate([gate_term, up_term, squares[:, None]], axis=1).astype(bf16)
+    total = lax.psum(packed, MP).astype(f32)
     gate_total = total[:, :hidden_dev]
     up_total = total[:, hidden_dev : 2 * hidden_dev]
     square_total = total[:, 2 * hidden_dev]
@@ -136,4 +136,4 @@
         P(None, MP),
     )
     out_specs = (P(DP, MP), P(MP, DP), P(MP, DP), P(DP, MP))
-    return jax.shard_map(shards, mesh=view, in_specs=in_specs, out_specs=out_specs, check_vma=False)
+    return jax.shard_map(body, mesh=view, in_specs=in_specs, out_specs=out_specs, check_vma=False)

time: 382 us -> 295 us (0.77)
  waiting for transfers between devices: 263 us -> 187 us
  matrix products: 31.4 us -> 26 us
    psum x2 -> x1, waiting for transfers between devices: 220 us -> 107 us  [body(): total = lax.psum(packed, MP).astype(f32)]
    all_to_all x2, waiting for transfers between devices: 15.8 us -> 57.8 us  [the longest x1 42.1 us: body(): down_in = lax.all_to_all(down_part, DP, 0, 0, tiled=True)]
    all_gather x1, waiting for transfers between devices: 27.8 us -> 21.6 us  [body(): train_rows = lax.all_gather(train_rows, name, axis=0, tiled=True)]
    dot_general x9, matrix products: 31.4 us -> 26 us  [the longest x1 4.98 us: body(): lax.dot_general(hidden_all, out_grad, (((0,), (0,)), ((), ())), preferred...]
  transfers between devices with their start and end apart: 5 -> 4, of which waited for: 4 -> 4; matrix products, arithmetic and copies ran while one was open for 6% -> 6% of each run, Pallas kernels for 0% -> 0%
where the time goes in v2:
time: 295 us
  waiting for transfers between devices  187 us (63%)
  matrix products  26 us (9%)
  starting transfers between devices  25.9 us (9%)
  blocking collectives  25 us (8%)
  between operations  14.3 us (5%)
  other arithmetic  12.4 us (4%)
  local copies, waits for them, and re-layouts  4.4 us (1%)
    psum x1, waiting for transfers between devices, body(): total = lax.psum(packed, MP).astype(f32)  107 us
    all_to_all x1, waiting for transfers between devices, body(): down_in = lax.all_to_all(down_part, DP, 0, 0, tiled=True)  42.1 us
    all_gather x2, blocking collectives, body(): train_rows = lax.all_gather(train_rows, name, axis=0, tiled=True)  25 us
    all_gather x1, waiting for transfers between devices, body(): train_rows = lax.all_gather(train_rows, name, axis=0, tiled=True)  21.6 us
    all_to_all x1, waiting for transfers between devices, body(): received = lax.all_to_all(outgoing, DP, 0, 0, tiled=True)  15.8 us
    all_to_all x1, starting transfers between devices, body(): received = lax.all_to_all(outgoing, DP, 0, 0, tiled=True)  13 us
    all_to_all x1, starting transfers between devices, body(): down_in = lax.all_to_all(down_part, DP, 0, 0, tiled=True)  12.8 us
  transfers between devices with their start and end apart: 4, of which 4 were waited for; matrix products, arithmetic and copies ran while one was open for 6% of the time, Pallas kernels for 0%

profile of v2, /device:TPU:32, one launch (start us, length us, event | category | flops | bytes accessed | tf_op | source)
XLA Modules:
  0.0 294.8 jit_solution(4128444985738762636)
XLA Ops:
  7.2 0.0 copy-start
  7.2 0.9 reshape.93
  8.1 0.8 convert_reduce_fusion.1
  8.9 0.7 broadcast_add_fusion
  9.6 0.1 add.70
  9.7 0.1 select_reduce_fusion.1
  9.8 0.1 copy.16
  9.9 0.1 sub.13
  10.0 1.3 convolution_convert_fusion.7
  11.3 0.8 all_to_all.14
  12.1 13.0 %all-to-all-start = ((bf16[32,4,1024]{2,1,0:T(4,128)(2,1)}), bf16[32,4,1024]{2,1,0:T(4,128)(2,1)S(1)}, u32[]{:S(2)}, u32[]{:S(2)}) async-start(bf16[32,4,1024]{2,1,0:T(4,128)(2,1)} %all_to_all.14), calls=%async_computation | async-start | bytes 524288 | tf_op jit(solution)/shard_map/all_to_all | solution.py:45
  25.2 0.0 all-gather.2.cloned.1.call-start
  25.3 15.8 %all-to-all-done = bf16[32,4,1024]{2,1,0:T(4,128)(2,1)S(1)} async-done(((bf16[32,4,1024]{2,1,0:T(4,128)(2,1)}), bf16[32,4,1024]{2,1,0:T(4,128)(2,1)S(1)}, u32[]{:S(2)}, u32[]{:S(2)}) %all-to-all-start) | async-done | bytes 262176 | tf_op jit(solution)/shard_map/all_to_all | solution.py:45
  41.0 0.1 all_to_all.16
  41.1 0.2 convolution_convert_fusion.8
  41.3 0.0 copy-start.6
  41.3 0.6 copy-done.6
  42.0 12.2 %all_gather.9 = bf16[128,1024]{1,0:T(8,128)(2,1)S(1)} all-gather(bf16[32,1024]{1,0:T(8,128)(2,1)S(1)} %convolution_convert_fusion.8), channel_id=1, replica_groups=mesh['x'=4,'zh'=2,'y'=4,'zl'=4,'c'=2] {'y'}, dimensions={0}, use_global_device_ids=true | all-gather | bytes 327680 | tf_op jit(solution)/shard_map/all_gather | solution.py:57
  54.2 12.7 %all_gather.10 = bf16[256,1024]{1,0:T(8,128)(2,1)} all-gather(bf16[128,1024]{1,0:T(8,128)(2,1)S(1)} %all_gather.9), channel_id=1, replica_groups=mesh['x'=4,'zh'=2,'y'=4,'zl'=4,'c'=2] {'zh'}, dimensions={0}, use_global_device_ids=true | all-gather | bytes 786432 | tf_op jit(solution)/shard_map/all_gather | solution.py:57
  67.0 0.0 all-gather.2.cloned.1.call-update
  67.0 0.0 all-reduce.3.cloned.1.call-start
  67.1 0.1 copy.17
  67.2 0.1 reduce-window.8
  67.2 0.1 reduce
  67.3 0.6 fusion.12
  68.0 0.7 multiply_divide_fusion
  68.6 0.1 select_reduce_fusion
  68.7 0.0 copy-start.10
  68.7 4.5 %convolution_convert_fusion.4 = bf16[1024,688]{0,1:T(8,128)(2,1)} fusion(bf16[688,1024]{1,0:T(8,128)(2,1)S(1)} %copy-done, bf16[1024,1024]{1,0:T(8,128)(2,1)} %param.19, f32[1024]{0:T(1024)S(1)} %select_reduce_fusion), kind=kOutput, calls=%fused_computation.18 | convolution fusion | flops 1446690816 | bytes 4919296 | tf_op jit(solution)/shard_map/dot_general | solution.py:94
  73.3 21.6 %all-gather.2.cloned.1.call-done = bf16[1024,1024]{1,0:T(8,128)(2,1)} async-done(((bf16[256,1024]{1,0:T(8,128)(2,1)}), bf16[1024,1024]{1,0:T(8,128)(2,1)}) %all-gather.2.cloned.1.call-update) | async-done | bytes 2097168 | tf_op jit(solution)/shard_map/all_gather | solution.py:57
  94.9 2.1 fusion.1
  97.0 0.0 copy-start.11
  97.0 3.4 %convolution_convert_fusion.5 = bf16[1024,688]{0,1:T(8,128)(2,1)S(1)} fusion(bf16[1024,688]{0,1:T(8,128)(2,1)S(1)} %copy-done.10, bf16[1024,1024]{1,0:T(8,128)(2,1)} %all-gather.2.cloned.1.call-done, f32[1024]{0:T(1024)S(1)} %convert_element_type.78), kind=kOutput, calls=%fused_computation.19 | convolution fusion | flops 1446690816 | bytes 4919296 | tf_op jit(solution)/shard_map/dot_general | solution.py:63
  100.4 1.7 convolution_convert_fusion.6
  102.1 1.9 pad_maximum_fusion
  104.0 0.0 all-reduce.3.cloned.1.call-update
  104.0 107.3 %all-reduce.3.cloned.1.call-done = (bf16[1024,1377]{0,1:T(8,128)(2,1)}, bf16[1024,688]{0,1:T(8,128)(2,1)}) async-done(((bf16[1024,1377]{0,1:T(8,128)(2,1)}, bf16[1024,688]{0,1:T(8,128)(2,1)}), (bf16[1024,1377]{0,1:T(8,128)(2,1)}, bf16[1024,688]{0,1:T(8,128)(2,1)})) %all-reduce.3.cloned.1.call-update) | async-done | bytes 4229136 | tf_op jit(solution)/shard_map/psum | solution.py:65
  211.3 2.5 convert_element_type.80
  213.9 0.8 multiply_convert_fusion.3
  214.7 1.6 copy-done.1
  216.3 3.3 %convolution_convert_fusion = bf16[1024,1024]{1,0:T(8,128)(2,1)} fusion(bf16[1024,688]{0,1:T(8,128)(2,1)S(1)} %multiply_convert_fusion.3, bf16[688,1024]{1,0:T(8,128)(2,1)S(1)} %copy-done), kind=kOutput, calls=%fused_computation.14 | convolution fusion | flops 1443889152 | bytes 4915200 | tf_op jit(solution)/shard_map/dot_general | solution.py:74
  219.6 12.8 %all-to-all-start.1 = ((bf16[32,32,1024]{2,1,0:T(8,128)(2,1)}), bf16[32,32,1024]{2,1,0:T(8,128)(2,1)S(1)}, u32[]{:S(2)}, u32[]{:S(2)}) async-start(bf16[32,32,1024]{2,1,0:T(8,128)(2,1)} %bitcast.13), calls=%async_computation.1 | async-start | bytes 4194304 | tf_op jit(solution)/shard_map/all_to_all | solution.py:75
  232.4 5.0 %convolution_convert_fusion.3 = bf16[688,1024]{1,0:T(8,128)(2,1)} fusion(bf16[1024,688]{0,1:T(8,128)(2,1)} %copy-done.5, bf16[1024,1024]{1,0:T(8,128)(2,1)} %param.19, f32[1024]{0:T(1024)S(1)} %select_reduce_fusion), kind=kOutput, calls=%fused_computation.17 | convolution fusion | flops 1446690816 | bytes 4919296 | tf_op jit(solution)/shard_map/dot_general | solution.py:91
  237.4 3.1 %convolution_convert_fusion.1 = bf16[1024,688]{0,1:T(8,128)(2,1)} fusion(bf16[1024,688]{0,1:T(8,128)(2,1)S(1)} %copy-done.12, f32[1024,1377]{0,1:T(8,128)S(1)} %copy-done.2, f32[1024]{0:T(1024)S(1)} %bitcast.15, bf16[1024,1024]{1,0:T(8,128)(2,1)S(1)} %copy-done.4, f32[1024]{0:T(1024)S(1)} %convert_element_type.78), kind=kOutput, calls=%fused_computation.15 | convolution fusion | flops 1453031424 | bytes 7741440 | tf_op jit(solution)/shard_map/dot_general | solution.py:110
  240.4 3.6 %convolution_convert_fusion.2 = bf16[1024,688]{0,1:T(8,128)(2,1)} fusion(bf16[1024,688]{0,1:T(8,128)(2,1)S(1)} %copy-done.12, f32[1024,1377]{0,1:T(8,128)S(1)} %copy-done.2, f32[1024]{0:T(1024)S(1)} %bitcast.16, bf16[1024,1024]{1,0:T(8,128)(2,1)S(1)} %copy-done.4, f32[1024]{0:T(1024)S(1)} %convert_element_type.78), kind=kOutput, calls=%fused_computation.16 | convolution fusion | flops 1456553984 | bytes 10559488 | tf_op jit(solution)/shard_map/dot_general | solution.py:107
  244.1 42.1 %all-to-all-done.1 = bf16[32,32,1024]{2,1,0:T(8,128)(2,1)S(1)} async-done(((bf16[32,32,1024]{2,1,0:T(8,128)(2,1)}), bf16[32,32,1024]{2,1,0:T(8,128)(2,1)S(1)}, u32[]{:S(2)}, u32[]{:S(2)}) %all-to-all-start.1) | async-done | bytes 2097184 | tf_op jit(solution)/shard_map/all_to_all | solution.py:75
  286.1 0.4 convert_reduce_fusion
  286.5 1.5 add_convert_fusion
  (28 shorter events, 0.1 us)
Async XLA Ops:
  7.2 61.6 %copy-start = (bf16[688,1024]{1,0:T(8,128)(2,1)S(1)}, bf16[688,1024]{1,0:T(8,128)(2,1)}, u32[]{:S(2)}) copy-start(bf16[688,1024]{1,0:T(8,128)(2,1)} %param.18) | copy-start | bytes 4227076
  7.2 59.9 %copy-start.7 = (bf16[1024]{0:T(1024)(128)(2,1)S(1)}, bf16[1024]{0:T(1024)(128)(2,1)}, u32[]{:S(2)}) copy-start(bf16[1024]{0:T(1024)(128)(2,1)} %param.15) | copy-start | bytes 6148
  7.2 59.9 %copy-start.8 = (s32[32]{0:T(128)S(1)}, s32[32]{0:T(128)}, u32[]{:S(2)}) copy-start(s32[32]{0:T(128)} %param.13) | copy-start | bytes 388
  7.2 60.1 %copy-start.9 = (s32[32]{0:T(128)S(1)}, s32[32]{0:T(128)}, u32[]{:S(2)}) copy-start(s32[32]{0:T(128)} %param.14) | copy-start | bytes 388
  12.1 28.9 %all-to-all-start = ((bf16[32,4,1024]{2,1,0:T(4,128)(2,1)}), bf16[32,4,1024]{2,1,0:T(4,128)(2,1)S(1)}, u32[]{:S(2)}, u32[]{:S(2)}) async-start(bf16[32,4,1024]{2,1,0:T(4,128)(2,1)} %all_to_all.14), calls=%async_computation | async-start | bytes 524288 | tf_op jit(solution)/shard_map/all_to_all | solution.py:45
  25.2 69.7 %all-gather.2.cloned.1.call-start = ((), (), s32[]{:S(2)}) async-start(), calls=%async_computation.2 | async-start | bytes 2621440 | tf_op jit(solution)/shard_map/all_gather | solution.py:57
  41.3 0.6 copy-start.6
  67.0 144.3 %all-reduce.3.cloned.1.call-start = ((), (), s32[]{:S(2)}) async-start(), calls=%async_computation.3 | async-start | bytes 8486912 | tf_op jit(solution)/shard_map/psum | solution.py:65
  68.7 28.2 %copy-start.10 = (bf16[1024,688]{0,1:T(8,128)(2,1)S(1)}, bf16[1024,688]{0,1:T(8,128)(2,1)}, u32[]{:S(2)}) copy-start(bf16[1024,688]{0,1:T(8,128)(2,1)} %param.17) | copy-start | bytes 4227076
  97.0 3.4 %copy-start.3 = (bf16[1024,1024]{1,0:T(8,128)(2,1)S(1)}, bf16[1024,1024]{1,0:T(8,128)(2,1)}, u32[]{:S(2)}) copy-start(bf16[1024,1024]{1,0:T(8,128)(2,1)} %all-gather.2.cloned.1.call-done) | copy-start | bytes 6291460
  97.0 3.4 %copy-start.11 = (bf16[1024,688]{0,1:T(8,128)(2,1)S(1)}, bf16[1024,688]{0,1:T(8,128)(2,1)}, u32[]{:S(2)}) copy-start(bf16[1024,688]{0,1:T(8,128)(2,1)} %param.16) | copy-start | bytes 4227076
  213.8 2.5 copy-start.1
  216.3 3.3 %copy-start.5 = (bf16[1024,688]{0,1:T(8,128)(2,1)}, bf16[1024,688]{0,1:T(8,128)(2,1)S(1)}, u32[]{:S(2)}) copy-start(bf16[1024,688]{0,1:T(8,128)(2,1)S(1)} %multiply_convert_fusion.3) | copy-start | bytes 4227076
  219.6 66.5 %all-to-all-start.1 = ((bf16[32,32,1024]{2,1,0:T(8,128)(2,1)}), bf16[32,32,1024]{2,1,0:T(8,128)(2,1)S(1)}, u32[]{:S(2)}, u32[]{:S(2)}) async-start(bf16[32,32,1024]{2,1,0:T(8,128)(2,1)} %bitcast.13), calls=%async_computation.1 | async-start | bytes 4194304 | tf_op jit(solution)/shard_map/all_to_all | solution.py:75
  232.4 5.0 %copy-start.2 = (f32[1024,1377]{0,1:T(8,128)S(1)}, f32[1024,1377]{0,1:T(8,128)}, u32[]{:S(2)}) copy-start(f32[1024,1377]{0,1:T(8,128)} %copy-done.1) | copy-start | bytes 16920580
  232.4 5.0 %copy-start.4 = (bf16[1024,1024]{1,0:T(8,128)(2,1)S(1)}, bf16[1024,1024]{1,0:T(8,128)(2,1)}, u32[]{:S(2)}) copy-start(bf16[1024,1024]{1,0:T(8,128)(2,1)} %all-gather.2.cloned.1.call-done) | copy-start | bytes 6291460
  232.4 5.0 %copy-start.12 = (bf16[1024,688]{0,1:T(8,128)(2,1)S(1)}, bf16[1024,688]{0,1:T(8,128)(2,1)}, u32[]{:S(2)}) copy-start(bf16[1024,688]{0,1:T(8,128)(2,1)} %get-tuple-element.5) | copy-start | bytes 4227076
Sparse Core Ops, SparseCore 0:
  67.1 27.7 all-gather.1
  104.1 107.1 all-reduce.2

commit v3 on v2

--- a/solution.py
+++ b/solution.py
@@ -3,6 +3,7 @@
 from jax import lax
 from jax.sharding import Mesh
 from jax.sharding import PartitionSpec as P
+
 
 D = 8192
 
@@ -10,6 +11,34 @@
 
 DP = ("x", "zh", "y")
 MP = ("zl", "c")
+
+
+def ring_gather(piece, name):
+    count = lax.axis_size(name)
+    here = lax.axis_index(name)
+    ahead = [(i, (i + 1) % count) for i in range(count)]
+    behind = [(i, (i - 1) % count) for i in range(count)]
+    parts = [piece]
+    from_left = piece
+    from_right = piece
+    for step in range(1, count // 2 + 1):
+        from_left = lax.ppermute(from_left, name, ahead)
+        parts.append(from_left)
+        if step < count - step:
+            from_right = lax.ppermute(from_right, name, behind)
+            parts.append(from_right)
+    order = [0] * count
+    order[0] = 0
+    k = 1
+    for step in range(1, count // 2 + 1):
+        order[(count - step) % count] = k
+        k += 1
+        if step < count - step:
+            order[step] = k
+            k += 1
+    stacked = jnp.stack([parts[order[j]] for j in range(count)])
+    gathered = jnp.roll(stacked, here, axis=0)
+    return gathered.reshape((count * piece.shape[0],) + piece.shape[1:])
 
 
 def body(
@@ -53,8 +82,26 @@
     own_rows = jnp.dot(pick_in, received, preferred_element_type=f32).astype(bf16)
 
     train_rows = own_rows
-    for name in reversed(DP):
+    for name in reversed(DP[1:]):
         train_rows = lax.all_gather(train_rows, name, axis=0, tiled=True)
+    train_rows = ring_gather(train_rows, DP[0])
+
+    row_ids = jnp.arange(total_rows, dtype=jnp.int32)
+    ends = jnp.cumsum(state_len)
+    starts = ends - state_len
+    member = ((row_ids[:, None] >= starts[None, :]) & (row_ids[:, None] < ends[None, :])).astype(
+        f32
+    )
+    importance = jnp.log1p(visits.astype(f32))
+    per_state = total_rows * importance / (state_len.astype(f32) * jnp.sum(importance))
+    row_weight = jnp.sum(member * per_state[None, :], axis=1)
+    out_grad = (upstream.astype(f32) * row_weight[:, None]).astype(bf16)
+    hidden_term = lax.dot_general(
+        out_grad, w_down, (((1,), (1,)), ((), ())), preferred_element_type=f32
+    ).astype(bf16)
+    hidden_sum = lax.psum(hidden_term, MP)
+    hidden_sum, train_rows = lax.optimization_barrier((hidden_sum, train_rows))
+    grad_hidden = hidden_sum.astype(f32)
 
     rows_float = train_rows.astype(f32)
     squares = jnp.sum(rows_float * rows_float, axis=1)
@@ -78,23 +125,9 @@
     )
     layer_out = (own_rows.astype(f32) + down_block).astype(bf16)
 
-    row_ids = jnp.arange(total_rows, dtype=jnp.int32)
-    ends = jnp.cumsum(state_len)
-    starts = ends - state_len
-    member = ((row_ids[:, None] >= starts[None, :]) & (row_ids[:, None] < ends[None, :])).astype(
-        f32
-    )
-    importance = jnp.log1p(visits.astype(f32))
-    per_state = total_rows * importance / (state_len.astype(f32) * jnp.sum(importance))
-    row_weight = jnp.sum(member * per_state[None, :], axis=1)
-    out_grad = (upstream.astype(f32) * row_weight[:, None]).astype(bf16)
     grad_down = lax.dot_general(
         hidden_all, out_grad, (((0,), (0,)), ((), ())), preferred_element_type=f32
     ).astype(bf16)
-    hidden_term = lax.dot_general(
-        out_grad, w_down, (((1,), (1,)), ((), ())), preferred_element_type=f32
-    ).astype(bf16)
-    grad_hidden = lax.psum(hidden_term, MP).astype(f32)
     sigmoid_gate = jax.nn.sigmoid(gate_all)
     gate_delta = (
         inverse[:, None]

time: 295 us -> 333 us (1.13)
  waiting for transfers between devices: 187 us -> 222 us
  starting transfers between devices: 25.9 us -> 29.4 us
    psum x0 -> x1, waiting for transfers between devices: none -> 64.6 us  [body(): hidden_sum = lax.psum(hidden_term, MP)]
    psum x1, waiting for transfers between devices: 107 us -> 85.5 us  [body(): total = lax.psum(packed, MP).astype(f32)]
    all_gather x1 -> x0, waiting for transfers between devices: 21.6 us -> none  [body(): train_rows = lax.all_gather(train_rows, name, axis=0, tiled=True)]
    ppermute x0 -> x3, waiting for transfers between devices: none -> 14.1 us  [the longest x2 14.1 us: ring_gather(): from_left = lax.ppermute(from_left, name, ahead)]
  transfers between devices with their start and end apart: 4 -> 7, of which waited for: 4 -> 6; matrix products, arithmetic and copies ran while one was open for 6% -> 5% of each run, Pallas kernels for 0% -> 0%
where the time goes in v3:
time: 333 us
  waiting for transfers between devices  222 us (67%)
  starting transfers between devices  29.4 us (9%)
  matrix products  25.6 us (8%)
  blocking collectives  24.9 us (7%)
  between operations  14.4 us (4%)
  other arithmetic  12.4 us (4%)
  local copies, waits for them, and re-layouts  4.22 us (1%)
    psum x1, waiting for transfers between devices, body(): total = lax.psum(packed, MP).astype(f32)  85.5 us
    psum x1, waiting for transfers between devices, body(): hidden_sum = lax.psum(hidden_term, MP)  64.6 us
    all_to_all x1, waiting for transfers between devices, body(): down_in = lax.all_to_all(down_part, DP, 0, 0, tiled=True)  41.9 us
    all_gather x2, blocking collectives, body(): train_rows = lax.all_gather(train_rows, name, axis=0, tiled=True)  24.9 us
    all_to_all x1, waiting for transfers between devices, body(): received = lax.all_to_all(outgoing, DP, 0, 0, tiled=True)  15.8 us
    ppermute x2, waiting for transfers between devices, ring_gather(): from_left = lax.ppermute(from_left, name, ahead)  14.1 us
    all_to_all x1, starting transfers between devices, body(): received = lax.all_to_all(outgoing, DP, 0, 0, tiled=True)  13 us
    all_to_all x1, starting transfers between devices, body(): down_in = lax.all_to_all(down_part, DP, 0, 0, tiled=True)  12.8 us
  transfers between devices with their start and end apart: 7, of which 6 were waited for; matrix products, arithmetic and copies ran while one was open for 5% of the time, Pallas kernels for 0%

profile of v3, /device:TPU:32, one launch (start us, length us, event | category | flops | bytes accessed | tf_op | source)
XLA Modules:
  0.0 332.9 jit_solution(10607805695998259767)
XLA Ops:
  7.2 0.9 reshape.96
  8.1 0.8 convert_reduce_fusion.1
  8.9 0.7 broadcast_add_fusion
  9.6 0.1 add.80
  9.7 0.1 select_reduce_fusion.1
  9.8 0.1 copy.16
  9.9 0.1 sub.17
  10.0 1.3 convolution_convert_fusion.7
  11.3 0.8 all_to_all.14
  12.1 13.0 %all-to-all-start = ((bf16[32,4,1024]{2,1,0:T(4,128)(2,1)}), bf16[32,4,1024]{2,1,0:T(4,128)(2,1)S(1)}, u32[]{:S(2)}, u32[]{:S(2)}) async-start(bf16[32,4,1024]{2,1,0:T(4,128)(2,1)} %all_to_all.14), calls=%async_computation | async-start | bytes 524288 | tf_op jit(solution)/shard_map/all_to_all | solution.py:74
  25.2 0.0 all-reduce.3.cloned.1.call-start
  25.3 15.8 %all-to-all-done = bf16[32,4,1024]{2,1,0:T(4,128)(2,1)S(1)} async-done(((bf16[32,4,1024]{2,1,0:T(4,128)(2,1)}), bf16[32,4,1024]{2,1,0:T(4,128)(2,1)S(1)}, u32[]{:S(2)}, u32[]{:S(2)}) %all-to-all-start) | async-done | bytes 262176 | tf_op jit(solution)/shard_map/all_to_all | solution.py:74
  41.0 0.1 all_to_all.16
  41.1 0.2 convolution_convert_fusion.8
  41.3 12.3 %all_gather.6 = bf16[128,1024]{1,0:T(8,128)(2,1)S(1)} all-gather(bf16[32,1024]{1,0:T(8,128)(2,1)S(1)} %convolution_convert_fusion.8), channel_id=1, replica_groups=mesh['x'=4,'zh'=2,'y'=4,'zl'=4,'c'=2] {'y'}, dimensions={0}, use_global_device_ids=true | all-gather | bytes 327680 | tf_op jit(solution)/shard_map/all_gather | solution.py:86
  53.6 12.6 %all_gather.7 = bf16[256,1024]{1,0:T(8,128)(2,1)S(1)} all-gather(bf16[128,1024]{1,0:T(8,128)(2,1)S(1)} %all_gather.6), channel_id=1, replica_groups=mesh['x'=4,'zh'=2,'y'=4,'zl'=4,'c'=2] {'zh'}, dimensions={0}, use_global_device_ids=true | all-gather | bytes 786432 | tf_op jit(solution)/shard_map/all_gather | solution.py:86
  66.2 0.6 collective-permute-start.1
  66.8 0.1 copy.17
  66.9 0.1 reduce-window.8
  67.0 0.1 reduce
  67.1 0.6 fusion.15
  67.7 0.7 multiply_divide_fusion
  68.4 0.1 select_reduce_fusion
  68.5 2.7 collective-permute-start
  71.2 7.4 %collective-permute-done.1 = bf16[256,1024]{1,0:T(8,128)(2,1)S(1)} collective-permute-done((bf16[256,1024]{1,0:T(8,128)(2,1)S(1)}, bf16[256,1024]{1,0:T(8,128)(2,1)S(1)}, u32[]{:S(2)}, u32[]{:S(2)}) %collective-permute-start.1) | collective-permute-done | bytes 524320 | tf_op jit(solution)/shard_map/ppermute | solution.py:25
  78.6 4.4 %convolution_convert_fusion.6 = bf16[1024,688]{0,1:T(8,128)(2,1)} fusion(bf16[688,1024]{1,0:T(8,128)(2,1)S(1)} %copy-done, bf16[1024,1024]{1,0:T(8,128)(2,1)} %param.19, f32[1024]{0:T(1024)S(1)} %select_reduce_fusion), kind=kOutput, calls=%fused_computation.20 | convolution fusion | flops 1446690816 | bytes 4919296 | tf_op jit(solution)/shard_map/dot_general | solution.py:99
  83.0 0.0 all-reduce.3.cloned.1.call-update
  83.0 0.2 all-reduce.5.cloned.1.call-start
  83.4 6.7 %collective-permute-done.2 = bf16[256,1024]{1,0:T(8,128)(2,1)S(1)} collective-permute-done((bf16[256,1024]{1,0:T(8,128)(2,1)S(1)}, bf16[256,1024]{1,0:T(8,128)(2,1)S(1)}, u32[]{:S(2)}, u32[]{:S(2)}) %collective-permute-start.2) | collective-permute-done | bytes 524320 | tf_op jit(solution)/shard_map/ppermute | solution.py:25
  90.4 0.2 constant_dynamic-slice_fusion
  90.6 64.6 %all-reduce.3.cloned.1.call-done = bf16[1024,688]{0,1:T(8,128)(2,1)} async-done(((bf16[1024,688]{0,1:T(8,128)(2,1)}), bf16[1024,688]{0,1:T(8,128)(2,1)}) %all-reduce.3.cloned.1.call-update) | async-done | bytes 1409040 | tf_op jit(solution)/shard_map/psum | solution.py:102
  155.2 0.5 fusion.1
  155.7 3.1 convolution_convert_fusion.4
  158.8 1.7 convolution_convert_fusion.5
  160.5 1.9 pad_maximum_fusion
  162.4 0.0 all-reduce.5.cloned.1.call-update
  162.4 85.5 %all-reduce.5.cloned.1.call-done = bf16[1024,1377]{0,1:T(8,128)(2,1)} async-done(((bf16[1024,1377]{0,1:T(8,128)(2,1)}), bf16[1024,1377]{0,1:T(8,128)(2,1)}) %all-reduce.5.cloned.1.call-update) | async-done | bytes 2820112 | tf_op jit(solution)/shard_map/psum | solution.py:112
  247.9 2.5 convert_element_type.85
  250.4 0.8 multiply_convert_fusion.3
  251.3 1.6 copy-done.1
  252.9 3.3 convolution_convert_fusion
  256.2 12.8 %all-to-all-start.1 = ((bf16[32,32,1024]{2,1,0:T(8,128)(2,1)}), bf16[32,32,1024]{2,1,0:T(8,128)(2,1)}, u32[]{:S(2)}, u32[]{:S(2)}) async-start(bf16[32,32,1024]{2,1,0:T(8,128)(2,1)} %bitcast.31), calls=%async_computation.1 | async-start | bytes 4194304 | tf_op jit(solution)/shard_map/all_to_all | solution.py:122
  269.0 5.0 %convolution_convert_fusion.3 = bf16[688,1024]{1,0:T(8,128)(2,1)} fusion(bf16[1024,688]{0,1:T(8,128)(2,1)} %copy-done.3, bf16[1024,1024]{1,0:T(8,128)(2,1)} %param.19, f32[1024]{0:T(1024)S(1)} %select_reduce_fusion), kind=kOutput, calls=%fused_computation.17 | convolution fusion | flops 1446690816 | bytes 4919296 | tf_op jit(solution)/shard_map/dot_general | solution.py:128
  274.0 3.1 convolution_convert_fusion.1
  277.0 3.6 %convolution_convert_fusion.2 = bf16[1024,688]{0,1:T(8,128)(2,1)} fusion(bf16[1024,688]{0,1:T(8,128)(2,1)S(1)} %copy-done.9, f32[1024,1377]{0,1:T(8,128)S(1)} %copy-done.2, f32[1024]{0:T(1024)S(1)} %bitcast.34, bf16[1024,1024]{1,0:T(8,128)(2,1)S(1)} %bitcast.30, f32[1024]{0:T(1024)S(1)} %convert_element_type.83), kind=kOutput, calls=%fused_computation.16 | convolution fusion | flops 1456553984 | bytes 10559488 | tf_op jit(solution)/shard_map/dot_general | solution.py:140
  280.6 41.9 %all-to-all-done.1 = bf16[32,32,1024]{2,1,0:T(8,128)(2,1)} async-done(((bf16[32,32,1024]{2,1,0:T(8,128)(2,1)}), bf16[32,32,1024]{2,1,0:T(8,128)(2,1)}, u32[]{:S(2)}, u32[]{:S(2)}) %all-to-all-start.1) | async-done | bytes 2097184 | tf_op jit(solution)/shard_map/all_to_all | solution.py:122
  322.6 2.0 convert_reduce_fusion
  324.5 1.5 add_convert_fusion
  (37 shorter events, 0.4 us)
Async XLA Ops:
  7.2 71.4 %copy-start = (bf16[688,1024]{1,0:T(8,128)(2,1)S(1)}, bf16[688,1024]{1,0:T(8,128)(2,1)}, u32[]{:S(2)}) copy-start(bf16[688,1024]{1,0:T(8,128)(2,1)} %param.18) | copy-start | bytes 4227076
  7.2 59.7 %copy-start.6 = (s32[32]{0:T(128)S(1)}, s32[32]{0:T(128)}, u32[]{:S(2)}) copy-start(s32[32]{0:T(128)} %param.13) | copy-start | bytes 388
  7.2 59.9 %copy-start.7 = (s32[32]{0:T(128)S(1)}, s32[32]{0:T(128)}, u32[]{:S(2)}) copy-start(s32[32]{0:T(128)} %param.14) | copy-start | bytes 388
  12.1 28.9 %all-to-all-start = ((bf16[32,4,1024]{2,1,0:T(4,128)(2,1)}), bf16[32,4,1024]{2,1,0:T(4,128)(2,1)S(1)}, u32[]{:S(2)}, u32[]{:S(2)}) async-start(bf16[32,4,1024]{2,1,0:T(4,128)(2,1)} %all_to_all.14), calls=%async_computation | async-start | bytes 524288 | tf_op jit(solution)/shard_map/all_to_all | solution.py:74
  25.2 130.0 %all-reduce.3.cloned.1.call-start = ((), (), s32[]{:S(2)}) async-start(), calls=%async_computation.2 | async-start | bytes 2818048 | tf_op jit(solution)/shard_map/psum | solution.py:102
  41.3 24.9 %copy-start.4 = (bf16[32,1024]{1,0:T(8,128)(2,1)}, bf16[32,1024]{1,0:T(8,128)(2,1)S(1)}, u32[]{:S(2)}) copy-start(bf16[32,1024]{1,0:T(8,128)(2,1)S(1)} %convolution_convert_fusion.8) | copy-start | bytes 196612
  66.2 12.4 %collective-permute-start.1 = (bf16[256,1024]{1,0:T(8,128)(2,1)S(1)}, bf16[256,1024]{1,0:T(8,128)(2,1)S(1)}, u32[]{:S(2)}, u32[]{:S(2)}) collective-permute-start(bf16[256,1024]{1,0:T(8,128)(2,1)S(1)} %all_gather.7), channel_id=1, source_target_pairs={{0,64},{64,128},{128,192},{192,0},{1,65},{65,129},{129,193},{193,1... | collective-permute-start | bytes 1572872 | tf_op jit(solution)/shard_map/ppermute | solution.py:25
  68.5 14.8 %copy-start.5 = (bf16[1024]{0:T(1024)(128)(2,1)S(1)}, bf16[1024]{0:T(1024)(128)(2,1)}, u32[]{:S(2)}) copy-start(bf16[1024]{0:T(1024)(128)(2,1)} %param.15) | copy-start | bytes 6148
  68.5 14.9 %collective-permute-start = (bf16[256,1024]{1,0:T(8,128)(2,1)S(1)}, bf16[256,1024]{1,0:T(8,128)(2,1)S(1)}, u32[]{:S(2)}, u32[]{:S(2)}) collective-permute-start(bf16[256,1024]{1,0:T(8,128)(2,1)S(1)} %all_gather.7), channel_id=1, source_target_pairs={{0,192},{64,0},{128,64},{192,128},{1,193},{65,1},{129,65},{193,129... | collective-permute-start | bytes 1572872 | tf_op jit(solution)/shard_map/ppermute | solution.py:28
  78.6 11.5 %collective-permute-start.2 = (bf16[256,1024]{1,0:T(8,128)(2,1)S(1)}, bf16[256,1024]{1,0:T(8,128)(2,1)S(1)}, u32[]{:S(2)}, u32[]{:S(2)}) collective-permute-start(bf16[256,1024]{1,0:T(8,128)(2,1)S(1)} %collective-permute-done.1), channel_id=1, source_target_pairs={{0,64},{64,128},{128,192},{192,0},{1,65},{65,129},{129,193},{193,1... | collective-permute-start | bytes 1572872 | tf_op jit(solution)/shard_map/ppermute | solution.py:25
  83.0 164.9 %all-reduce.5.cloned.1.call-start = ((), (), s32[]{:S(2)}) async-start(), calls=%async_computation.3 | async-start | bytes 5668864 | tf_op jit(solution)/shard_map/psum | solution.py:112
  155.7 3.1 copy-start.8
  250.4 2.5 copy-start.1
  252.9 3.3 copy-start.3
  256.2 66.4 %all-to-all-start.1 = ((bf16[32,32,1024]{2,1,0:T(8,128)(2,1)}), bf16[32,32,1024]{2,1,0:T(8,128)(2,1)}, u32[]{:S(2)}, u32[]{:S(2)}) async-start(bf16[32,32,1024]{2,1,0:T(8,128)(2,1)} %bitcast.31), calls=%async_computation.1 | async-start | bytes 4194304 | tf_op jit(solution)/shard_map/all_to_all | solution.py:122
  268.9 5.0 %copy-start.2 = (f32[1024,1377]{0,1:T(8,128)S(1)}, f32[1024,1377]{0,1:T(8,128)}, u32[]{:S(2)}) copy-start(f32[1024,1377]{0,1:T(8,128)} %copy-done.1) | copy-start | bytes 16920580
  269.0 5.0 %copy-start.9 = (bf16[1024,688]{0,1:T(8,128)(2,1)S(1)}, bf16[1024,688]{0,1:T(8,128)(2,1)}, u32[]{:S(2)}) copy-start(bf16[1024,688]{0,1:T(8,128)(2,1)} %all-reduce.3.cloned.1.call-done) | copy-start | bytes 4227076
Sparse Core Ops, SparseCore 0:
  83.2 71.9 all-reduce.2
  162.5 85.3 all-reduce.4

commit v4 on v3

--- a/solution.py
+++ b/solution.py
@@ -39,6 +39,19 @@
     stacked = jnp.stack([parts[order[j]] for j in range(count)])
     gathered = jnp.roll(stacked, here, axis=0)
     return gathered.reshape((count * piece.shape[0],) + piece.shape[1:])
+
+
+def staged_scatter(part, block_rows):
+    sizes = tuple(lax.axis_size(name) for name in DP)
+    features = part.shape[1]
+    held = part.reshape(sizes + (block_rows, features))
+    held = jnp.transpose(held, (2, 0, 1, 3, 4))
+    total = None
+    for name in (DP[2], DP[0], DP[1]):
+        arrived = lax.all_to_all(held, name, 0, 0, tiled=True)
+        total = jnp.sum(arrived.astype(jnp.float32), axis=0)
+        held = total.astype(part.dtype)
+    return total.reshape(block_rows, features)
 
 
 def body(
@@ -119,10 +132,7 @@
     hidden_all = (jax.nn.silu(gate_all) * up_all).astype(bf16)
 
     down_part = jnp.dot(hidden_all, w_down, preferred_element_type=f32).astype(bf16)
-    down_in = lax.all_to_all(down_part, DP, 0, 0, tiled=True)
-    down_block = jnp.sum(
-        down_in.reshape(count_dp, block_rows, down_in.shape[1]).astype(f32), axis=0
-    )
+    down_block = staged_scatter(down_part, block_rows)
     layer_out = (own_rows.astype(f32) + down_block).astype(bf16)
 
     grad_down = lax.dot_general(

time: 333 us -> 329 us (0.988)
  waiting for transfers between devices: 222 us -> 209 us
  matrix products: 25.6 us -> 29.4 us
    all_to_all x1 -> x3, waiting for transfers between devices: 41.9 us -> 28.9 us  [staged_scatter(): arrived = lax.all_to_all(held, name, 0, 0, tiled=True)]
    all_to_all x1 -> x3, starting transfers between devices: 12.8 us -> 14.1 us  [staged_scatter(): arrived = lax.all_to_all(held, name, 0, 0, tiled=True)]
  transfers between devices with their start and end apart: 7 -> 9, of which waited for: 6 -> 8; matrix products, arithmetic and copies ran while one was open for 5% -> 7% of each run, Pallas kernels for 0% -> 0%
where the time goes in v4:
time: 329 us
  waiting for transfers between devices  209 us (64%)
  starting transfers between devices  30.7 us (9%)
  matrix products  29.4 us (9%)
  blocking collectives  24.9 us (8%)
  between operations  14.4 us (4%)
  other arithmetic  14.3 us (4%)
  local copies, waits for them, and re-layouts  5.81 us (2%)
    psum x1, waiting for transfers between devices, body(): total = lax.psum(packed, MP).astype(f32)  85.4 us
    psum x1, waiting for transfers between devices, body(): hidden_sum = lax.psum(hidden_term, MP)  64.9 us
    all_to_all x3, waiting for transfers between devices, staged_scatter(): arrived = lax.all_to_all(held, name, 0, 0, tiled=True)  28.9 us
    all_gather x2, blocking collectives, body(): train_rows = lax.all_gather(train_rows, name, axis=0, tiled=True)  24.9 us
    all_to_all x1, waiting for transfers between devices, body(): received = lax.all_to_all(outgoing, DP, 0, 0, tiled=True)  15.8 us
    ppermute x2, waiting for transfers between devices, ring_gather(): from_left = lax.ppermute(from_left, name, ahead)  14.1 us
    all_to_all x3, starting transfers between devices, staged_scatter(): arrived = lax.all_to_all(held, name, 0, 0, tiled=True)  14.1 us
    all_to_all x1, starting transfers between devices, body(): received = lax.all_to_all(outgoing, DP, 0, 0, tiled=True)  13 us
  transfers between devices with their start and end apart: 9, of which 8 were waited for; matrix products, arithmetic and copies ran while one was open for 7% of the time, Pallas kernels for 0%

profile of v4, /device:TPU:32, one launch (start us, length us, event | category | flops | bytes accessed | tf_op | source)
XLA Modules:
  0.0 328.7 jit_solution(3125515606308021816)
XLA Ops:
  7.2 0.9 reshape.95
  8.1 0.8 convert_reduce_fusion
  8.9 0.7 broadcast_add_fusion
  9.7 0.1 select_reduce_fusion.1
  9.8 0.1 copy.18
  9.9 0.1 sub.17
  10.0 1.3 convolution_convert_fusion.7
  11.3 0.8 all_to_all.17
  12.1 13.0 %all-to-all-start = ((bf16[32,4,1024]{2,1,0:T(4,128)(2,1)}), bf16[32,4,1024]{2,1,0:T(4,128)(2,1)S(1)}, u32[]{:S(2)}, u32[]{:S(2)}) async-start(bf16[32,4,1024]{2,1,0:T(4,128)(2,1)} %all_to_all.17), calls=%async_computation | async-start | bytes 524288 | tf_op jit(solution)/shard_map/all_to_all | solution.py:87
  25.3 15.8 %all-to-all-done = bf16[32,4,1024]{2,1,0:T(4,128)(2,1)S(1)} async-done(((bf16[32,4,1024]{2,1,0:T(4,128)(2,1)}), bf16[32,4,1024]{2,1,0:T(4,128)(2,1)S(1)}, u32[]{:S(2)}, u32[]{:S(2)}) %all-to-all-start) | async-done | bytes 262176 | tf_op jit(solution)/shard_map/all_to_all | solution.py:87
  41.1 0.2 convolution_convert_fusion.8
  41.3 12.3 %all_gather.6 = bf16[128,1024]{1,0:T(8,128)(2,1)S(1)} all-gather(bf16[32,1024]{1,0:T(8,128)(2,1)S(1)} %convolution_convert_fusion.8), channel_id=1, replica_groups=mesh['x'=4,'zh'=2,'y'=4,'zl'=4,'c'=2] {'y'}, dimensions={0}, use_global_device_ids=true | all-gather | bytes 327680 | tf_op jit(solution)/shard_map/all_gather | solution.py:99
  53.6 12.6 %all_gather.7 = bf16[256,1024]{1,0:T(8,128)(2,1)S(1)} all-gather(bf16[128,1024]{1,0:T(8,128)(2,1)S(1)} %all_gather.6), channel_id=1, replica_groups=mesh['x'=4,'zh'=2,'y'=4,'zl'=4,'c'=2] {'zh'}, dimensions={0}, use_global_device_ids=true | all-gather | bytes 786432 | tf_op jit(solution)/shard_map/all_gather | solution.py:99
  66.2 0.6 collective-permute-start.1
  66.8 0.1 copy.19
  67.0 0.1 reduce.2
  67.1 0.6 fusion.15
  67.7 0.7 multiply_divide_fusion
  68.4 0.1 select_reduce_fusion
  68.5 2.7 collective-permute-start
  71.2 7.4 %collective-permute-done.1 = bf16[256,1024]{1,0:T(8,128)(2,1)S(1)} collective-permute-done((bf16[256,1024]{1,0:T(8,128)(2,1)S(1)}, bf16[256,1024]{1,0:T(8,128)(2,1)S(1)}, u32[]{:S(2)}, u32[]{:S(2)}) %collective-permute-start.1) | collective-permute-done | bytes 524320 | tf_op jit(solution)/shard_map/ppermute | solution.py:25
  78.6 4.4 %convolution_convert_fusion.6 = bf16[1024,688]{0,1:T(8,128)(2,1)} fusion(bf16[688,1024]{1,0:T(8,128)(2,1)S(1)} %copy-done, bf16[1024,1024]{1,0:T(8,128)(2,1)} %param.19, f32[1024]{0:T(1024)S(1)} %select_reduce_fusion), kind=kOutput, calls=%fused_computation.20 | convolution fusion | flops 1446690816 | bytes 4919296 | tf_op jit(solution)/shard_map/dot_general | solution.py:112
  83.1 0.2 all-reduce.5.cloned.1.call-start
  83.4 6.7 %collective-permute-done.2 = bf16[256,1024]{1,0:T(8,128)(2,1)S(1)} collective-permute-done((bf16[256,1024]{1,0:T(8,128)(2,1)S(1)}, bf16[256,1024]{1,0:T(8,128)(2,1)S(1)}, u32[]{:S(2)}, u32[]{:S(2)}) %collective-permute-start.2) | collective-permute-done | bytes 524320 | tf_op jit(solution)/shard_map/ppermute | solution.py:25
  90.4 0.2 constant_dynamic-slice_fusion
  90.6 64.9 %all-reduce.3.cloned.1.call-done = bf16[1024,688]{0,1:T(8,128)(2,1)} async-done(((bf16[1024,688]{0,1:T(8,128)(2,1)}), bf16[1024,688]{0,1:T(8,128)(2,1)}) %all-reduce.3.cloned.1.call-update) | async-done | bytes 1409040 | tf_op jit(solution)/shard_map/psum | solution.py:115
  155.5 0.5 fusion.1
  156.0 3.1 convolution_convert_fusion.4
  159.1 1.7 convolution_convert_fusion.5
  160.8 1.9 pad_maximum_fusion
  162.7 85.4 %all-reduce.5.cloned.1.call-done = bf16[1024,1377]{0,1:T(8,128)(2,1)} async-done(((bf16[1024,1377]{0,1:T(8,128)(2,1)}), bf16[1024,1377]{0,1:T(8,128)(2,1)}) %all-reduce.5.cloned.1.call-update) | async-done | bytes 2820112 | tf_op jit(solution)/shard_map/psum | solution.py:125
  248.1 2.5 convert_element_type.89
  250.7 0.8 multiply_convert_fusion.3
  251.5 1.6 copy-done.1
  253.1 1.8 convolution_convert_fusion
  255.0 1.6 copy.22
  256.6 4.4 %all-to-all-start.1 = ((bf16[4,4,2,32,1024]{4,3,2,1,0:T(8,128)(2,1)}), bf16[4,4,2,32,1024]{4,3,2,1,0:T(8,128)(2,1)}, u32[]{:S(2)}, u32[]{:S(2)}) async-start(bf16[4,4,2,32,1024]{4,3,2,1,0:T(8,128)(2,1)} %bitcast.34), calls=%async_computation.1 | async-start | bytes 4194304 | tf_op jit(solution)/shard_map/all_to_all | solution.py:51
  261.0 6.7 %convolution_convert_fusion.2 = bf16[1024,688]{0,1:T(8,128)(2,1)} fusion(bf16[1024,688]{0,1:T(8,128)(2,1)} %all-reduce.3.cloned.1.call-done, f32[1024,1377]{0,1:T(8,128)} %copy-done.1, f32[1024]{0:T(1024)S(1)} %bitcast.37, bf16[1024,1024]{1,0:T(8,128)(2,1)S(1)} %bitcast.32, f32[1024]{0:T(1024)S(1)} %convert_element_type.87), kind=kOutput, calls=%fused_computation.16 | convolution fusion | flops 1456553984 | bytes 10559488 | tf_op jit(solution)/shard_map/dot_general | solution.py:150
  267.7 20.6 %all-to-all-done.1 = bf16[4,4,2,32,1024]{4,3,2,1,0:T(8,128)(2,1)} async-done(((bf16[4,4,2,32,1024]{4,3,2,1,0:T(8,128)(2,1)}), bf16[4,4,2,32,1024]{4,3,2,1,0:T(8,128)(2,1)}, u32[]{:S(2)}, u32[]{:S(2)}) %all-to-all-start.1) | async-done | bytes 2097184 | tf_op jit(solution)/shard_map/all_to_all | solution.py:51
  288.3 2.9 reduce_sum.83
  291.2 4.4 %all-to-all-start.2 = ((bf16[4,2,32,1024]{3,2,1,0:T(8,128)(2,1)}), bf16[4,2,32,1024]{3,2,1,0:T(8,128)(2,1)}, u32[]{:S(2)}, u32[]{:S(2)}) async-start(bf16[4,2,32,1024]{3,2,1,0:T(8,128)(2,1)} %reduce_sum.83), calls=%async_computation.2 | async-start | bytes 1048576 | tf_op jit(solution)/shard_map/all_to_all | solution.py:51
  295.6 5.3 %convolution_convert_fusion.1 = bf16[1024,688]{0,1:T(8,128)(2,1)} fusion(bf16[1024,688]{0,1:T(8,128)(2,1)} %all-reduce.3.cloned.1.call-done, f32[1024,1377]{0,1:T(8,128)} %copy-done.1, f32[1024]{0:T(1024)S(1)} %bitcast.38, bf16[1024,1024]{1,0:T(8,128)(2,1)S(1)} %bitcast.33, f32[1024]{0:T(1024)S(1)} %convert_element_type.87), kind=kOutput, calls=%fused_computation.15 | convolution fusion | flops 1453031424 | bytes 7741440 | tf_op jit(solution)/shard_map/dot_general | solution.py:153
  300.9 4.8 %all-to-all-done.2 = bf16[4,2,32,1024]{3,2,1,0:T(8,128)(2,1)} async-done(((bf16[4,2,32,1024]{3,2,1,0:T(8,128)(2,1)}), bf16[4,2,32,1024]{3,2,1,0:T(8,128)(2,1)}, u32[]{:S(2)}, u32[]{:S(2)}) %all-to-all-start.2) | async-done | bytes 524320 | tf_op jit(solution)/shard_map/all_to_all | solution.py:51
  305.7 1.8 reduce_sum.84
  307.5 5.3 %all-to-all-start.3 = ((bf16[2,32,1024]{2,1,0:T(8,128)(2,1)}), bf16[2,32,1024]{2,1,0:T(8,128)(2,1)S(1)}, u32[]{:S(2)}, u32[]{:S(2)}) async-start(bf16[2,32,1024]{2,1,0:T(8,128)(2,1)} %reduce_sum.84), calls=%async_computation.3 | async-start | bytes 262144 | tf_op jit(solution)/shard_map/all_to_all | solution.py:51
  312.8 4.9 %convolution_convert_fusion.3 = bf16[688,1024]{1,0:T(8,128)(2,1)} fusion(bf16[1024,688]{0,1:T(8,128)(2,1)} %copy-done.2, bf16[1024,1024]{1,0:T(8,128)(2,1)} %param.19, f32[1024]{0:T(1024)S(1)} %select_reduce_fusion), kind=kOutput, calls=%fused_computation.17 | convolution fusion | flops 1446690816 | bytes 4919296 | tf_op jit(solution)/shard_map/dot_general | solution.py:138
  317.7 3.5 %all-to-all-done.3 = bf16[2,32,1024]{2,1,0:T(8,128)(2,1)S(1)} async-done(((bf16[2,32,1024]{2,1,0:T(8,128)(2,1)}), bf16[2,32,1024]{2,1,0:T(8,128)(2,1)S(1)}, u32[]{:S(2)}, u32[]{:S(2)}) %all-to-all-start.3) | async-done | bytes 131104 | tf_op jit(solution)/shard_map/all_to_all | solution.py:51
  321.2 0.7 add_convert_fusion
  (42 shorter events, 0.7 us)
Async XLA Ops:
  7.2 71.4 %copy-start = (bf16[688,1024]{1,0:T(8,128)(2,1)S(1)}, bf16[688,1024]{1,0:T(8,128)(2,1)}, u32[]{:S(2)}) copy-start(bf16[688,1024]{1,0:T(8,128)(2,1)} %param.18) | copy-start | bytes 4227076
  7.2 59.7 %copy-start.6 = (s32[32]{0:T(128)S(1)}, s32[32]{0:T(128)}, u32[]{:S(2)}) copy-start(s32[32]{0:T(128)} %param.13) | copy-start | bytes 388
  7.2 59.9 %copy-start.7 = (s32[32]{0:T(128)S(1)}, s32[32]{0:T(128)}, u32[]{:S(2)}) copy-start(s32[32]{0:T(128)} %param.14) | copy-start | bytes 388
  12.1 28.9 %all-to-all-start = ((bf16[32,4,1024]{2,1,0:T(4,128)(2,1)}), bf16[32,4,1024]{2,1,0:T(4,128)(2,1)S(1)}, u32[]{:S(2)}, u32[]{:S(2)}) async-start(bf16[32,4,1024]{2,1,0:T(4,128)(2,1)} %all_to_all.17), calls=%async_computation | async-start | bytes 524288 | tf_op jit(solution)/shard_map/all_to_all | solution.py:87
  25.2 130.3 %all-reduce.3.cloned.1.call-start = ((), (), s32[]{:S(2)}) async-start(), calls=%async_computation.4 | async-start | bytes 2818048 | tf_op jit(solution)/shard_map/psum | solution.py:115
  41.3 24.9 %copy-start.3 = (bf16[32,1024]{1,0:T(8,128)(2,1)}, bf16[32,1024]{1,0:T(8,128)(2,1)S(1)}, u32[]{:S(2)}) copy-start(bf16[32,1024]{1,0:T(8,128)(2,1)S(1)} %convolution_convert_fusion.8) | copy-start | bytes 196612
  66.2 12.4 %collective-permute-start.1 = (bf16[256,1024]{1,0:T(8,128)(2,1)S(1)}, bf16[256,1024]{1,0:T(8,128)(2,1)S(1)}, u32[]{:S(2)}, u32[]{:S(2)}) collective-permute-start(bf16[256,1024]{1,0:T(8,128)(2,1)S(1)} %all_gather.7), channel_id=1, source_target_pairs={{0,64},{64,128},{128,192},{192,0},{1,65},{65,129},{129,193},{193,1... | collective-permute-start | bytes 1572872 | tf_op jit(solution)/shard_map/ppermute | solution.py:25
  68.5 14.8 %copy-start.5 = (bf16[1024]{0:T(1024)(128)(2,1)S(1)}, bf16[1024]{0:T(1024)(128)(2,1)}, u32[]{:S(2)}) copy-start(bf16[1024]{0:T(1024)(128)(2,1)} %param.15) | copy-start | bytes 6148
  68.5 14.9 %collective-permute-start = (bf16[256,1024]{1,0:T(8,128)(2,1)S(1)}, bf16[256,1024]{1,0:T(8,128)(2,1)S(1)}, u32[]{:S(2)}, u32[]{:S(2)}) collective-permute-start(bf16[256,1024]{1,0:T(8,128)(2,1)S(1)} %all_gather.7), channel_id=1, source_target_pairs={{0,192},{64,0},{128,64},{192,128},{1,193},{65,1},{129,65},{193,129... | collective-permute-start | bytes 1572872 | tf_op jit(solution)/shard_map/ppermute | solution.py:28
  78.6 11.5 %collective-permute-start.2 = (bf16[256,1024]{1,0:T(8,128)(2,1)S(1)}, bf16[256,1024]{1,0:T(8,128)(2,1)S(1)}, u32[]{:S(2)}, u32[]{:S(2)}) collective-permute-start(bf16[256,1024]{1,0:T(8,128)(2,1)S(1)} %collective-permute-done.1), channel_id=1, source_target_pairs={{0,64},{64,128},{128,192},{192,0},{1,65},{65,129},{129,193},{193,1... | collective-permute-start | bytes 1572872 | tf_op jit(solution)/shard_map/ppermute | solution.py:25
  83.1 165.1 %all-reduce.5.cloned.1.call-start = ((), (), s32[]{:S(2)}) async-start(), calls=%async_computation.5 | async-start | bytes 5668864 | tf_op jit(solution)/shard_map/psum | solution.py:125
  156.0 3.1 copy-start.8
  250.6 2.5 copy-start.1
  253.1 1.8 copy-start.2
  256.6 31.7 %all-to-all-start.1 = ((bf16[4,4,2,32,1024]{4,3,2,1,0:T(8,128)(2,1)}), bf16[4,4,2,32,1024]{4,3,2,1,0:T(8,128)(2,1)}, u32[]{:S(2)}, u32[]{:S(2)}) async-start(bf16[4,4,2,32,1024]{4,3,2,1,0:T(8,128)(2,1)} %bitcast.34), calls=%async_computation.1 | async-start | bytes 4194304 | tf_op jit(solution)/shard_map/all_to_all | solution.py:51
  291.2 14.5 %all-to-all-start.2 = ((bf16[4,2,32,1024]{3,2,1,0:T(8,128)(2,1)}), bf16[4,2,32,1024]{3,2,1,0:T(8,128)(2,1)}, u32[]{:S(2)}, u32[]{:S(2)}) async-start(bf16[4,2,32,1024]{3,2,1,0:T(8,128)(2,1)} %reduce_sum.83), calls=%async_computation.2 | async-start | bytes 1048576 | tf_op jit(solution)/shard_map/all_to_all | solution.py:51
  307.5 13.7 %all-to-all-start.3 = ((bf16[2,32,1024]{2,1,0:T(8,128)(2,1)}), bf16[2,32,1024]{2,1,0:T(8,128)(2,1)S(1)}, u32[]{:S(2)}, u32[]{:S(2)}) async-start(bf16[2,32,1024]{2,1,0:T(8,128)(2,1)} %reduce_sum.84), calls=%async_computation.3 | async-start | bytes 262144 | tf_op jit(solution)/shard_map/all_to_all | solution.py:51
  312.8 8.4 %copy-start.4 = (bf16[32,1024]{1,0:T(8,128)(2,1)S(1)}, bf16[32,1024]{1,0:T(8,128)(2,1)}, u32[]{:S(2)}) copy-start(bf16[32,1024]{1,0:T(8,128)(2,1)} %copy-done.3) | copy-start | bytes 196612
Sparse Core Ops, SparseCore 0:
  83.2 72.2 all-reduce.2
  162.8 85.2 all-reduce.4

commit v5 on v4

--- a/solution.py
+++ b/solution.py
@@ -54,6 +54,34 @@
     return total.reshape(block_rows, features)
 
 
+def pair_allreduce(part, names):
+    steps = []
+    for name in reversed(names):
+        count = lax.axis_size(name)
+        bit = 1
+        while bit < count:
+            steps.append((name, bit))
+            bit *= 2
+    held = part.astype(jnp.float32)
+    for name, bit in steps:
+        pairs = [(i, i ^ bit) for i in range(lax.axis_size(name))]
+        upper = (lax.axis_index(name) & bit) != 0
+        low, high = jnp.split(held, 2, axis=0)
+        keep = jnp.where(upper, high, low)
+        give = jnp.where(upper, low, high)
+        got = lax.ppermute(give.astype(part.dtype), name, pairs)
+        held = keep + got.astype(jnp.float32)
+    held = held.astype(part.dtype)
+    for name, bit in reversed(steps):
+        pairs = [(i, i ^ bit) for i in range(lax.axis_size(name))]
+        upper = (lax.axis_index(name) & bit) != 0
+        got = lax.ppermute(held, name, pairs)
+        held = jnp.where(
+            upper, jnp.concatenate([got, held], axis=0), jnp.concatenate([held, got], axis=0)
+        )
+    return held
+
+
 def body(
     store_rows, source_shard, source_row, state_len, visits, gain, w_gate, w_up, w_down, upstream
 ):
@@ -95,9 +123,8 @@
     own_rows = jnp.dot(pick_in, received, preferred_element_type=f32).astype(bf16)
 
     train_rows = own_rows
-    for name in reversed(DP[1:]):
-        train_rows = lax.all_gather(train_rows, name, axis=0, tiled=True)
-    train_rows = ring_gather(train_rows, DP[0])
+    for name in reversed(DP):
+        train_rows = ring_gather(train_rows, name)
 
     row_ids = jnp.arange(total_rows, dtype=jnp.int32)
     ends = jnp.cumsum(state_len)
@@ -112,8 +139,7 @@
     hidden_term = lax.dot_general(
         out_grad, w_down, (((1,), (1,)), ((), ())), preferred_element_type=f32
     ).astype(bf16)
-    hidden_sum = lax.psum(hidden_term, MP)
-    hidden_sum, train_rows = lax.optimization_barrier((hidden_sum, train_rows))
+    hidden_sum = pair_allreduce(hidden_term, MP)
     grad_hidden = hidden_sum.astype(f32)
 
     rows_float = train_rows.astype(f32)

time: 329 us -> 264 us (0.80)
  waiting for transfers between devices: 209 us -> 151 us
  blocking collectives: 24.9 us -> 0 us
  starting transfers between devices: 30.7 us -> 41 us
  other arithmetic: 14.3 us -> 19.7 us
    psum x1 -> x0, waiting for transfers between devices: 64.9 us -> none  [body(): hidden_sum = lax.psum(hidden_term, MP)]
    psum x1, waiting for transfers between devices: 85.4 us -> 33.1 us  [body(): total = lax.psum(packed, MP).astype(f32)]
    ppermute x0 -> x6, waiting for transfers between devices: none -> 43.7 us  [the longest x3 29.3 us: pair_allreduce(): got = lax.ppermute(give.astype(part.dtype), name, pairs)]
    all_gather x2 -> x0, blocking collectives: 24.9 us -> none  [body(): train_rows = lax.all_gather(train_rows, name, axis=0, tiled=True)]
    ppermute x2 -> x5, waiting for transfers between devices: 14.1 us -> 31.3 us  [ring_gather(): from_left = lax.ppermute(from_left, name, ahead)]
    ppermute x0 -> x6, starting transfers between devices: none -> 7.07 us  [the longest x3 6.88 us: pair_allreduce(): got = lax.ppermute(held, name, pairs)]
    convert_element_type x0 -> x5, other arithmetic: none -> 3.36 us  [the longest x3 2.85 us: pair_allreduce(): got = lax.ppermute(give.astype(part.dtype), name, pairs)]
  transfers between devices with their start and end apart: 9 -> 18, of which waited for: 8 -> 14; matrix products, arithmetic and copies ran while one was open for 7% -> 17% of each run, Pallas kernels for 0% -> 0%
where the time goes in v5:
time: 264 us; the launch traced here: 263 us
  waiting for transfers between devices  151 us (57%)
  starting transfers between devices  41 us (16%)
  matrix products  30.1 us (11%)
  other arithmetic  19.7 us (7%)
  between operations  14.5 us (5%)
  local copies, waits for them, and re-layouts  6.78 us (3%)
    psum x1, waiting for transfers between devices, body(): total = lax.psum(packed, MP).astype(f32)  33.1 us
    ppermute x5, waiting for transfers between devices, ring_gather(): from_left = lax.ppermute(from_left, name, ahead)  31.3 us
    ppermute x3, waiting for transfers between devices, pair_allreduce(): got = lax.ppermute(give.astype(part.dtype), name, pairs)  29.3 us
    all_to_all x3, waiting for transfers between devices, staged_scatter(): arrived = lax.all_to_all(held, name, 0, 0, tiled=True)  27.1 us
    all_to_all x1, waiting for transfers between devices, body(): received = lax.all_to_all(outgoing, DP, 0, 0, tiled=True)  15.8 us
    ppermute x3, waiting for transfers between devices, pair_allreduce(): got = lax.ppermute(held, name, pairs)  14.4 us
    all_to_all x3, starting transfers between devices, staged_scatter(): arrived = lax.all_to_all(held, name, 0, 0, tiled=True)  13.2 us
    all_to_all x1, starting transfers between devices, body(): received = lax.all_to_all(outgoing, DP, 0, 0, tiled=True)  13 us
  transfers between devices with their start and end apart: 18, of which 14 were waited for; matrix products, arithmetic and copies ran while one was open for 17% of the time, Pallas kernels for 0%

profile of v5, /device:TPU:32, one launch (start us, length us, event | category | flops | bytes accessed | tf_op | source)
XLA Modules:
  0.0 262.9 jit_solution(6889081427711974138)
XLA Ops:
  7.2 0.9 reshape.103
  8.1 0.8 convert_reduce_fusion
  8.9 0.7 broadcast_add_fusion
  10.0 1.3 convolution_convert_fusion.7
  11.3 0.8 all_to_all.17
  12.1 13.0 %all-to-all-start = ((bf16[32,4,1024]{2,1,0:T(4,128)(2,1)}), bf16[32,4,1024]{2,1,0:T(4,128)(2,1)S(1)}, u32[]{:S(2)}, u32[]{:S(2)}) async-start(bf16[32,4,1024]{2,1,0:T(4,128)(2,1)} %all_to_all.17), calls=%async_computation | async-start | bytes 524288 | tf_op jit(solution)/shard_map/all_to_all | solution.py:115
  25.3 15.8 %all-to-all-done = bf16[32,4,1024]{2,1,0:T(4,128)(2,1)S(1)} async-done(((bf16[32,4,1024]{2,1,0:T(4,128)(2,1)}), bf16[32,4,1024]{2,1,0:T(4,128)(2,1)S(1)}, u32[]{:S(2)}, u32[]{:S(2)}) %all-to-all-start) | async-done | bytes 262176 | tf_op jit(solution)/shard_map/all_to_all | solution.py:115
  41.3 1.0 collective-permute-start.1
  42.3 2.3 collective-permute-start
  44.6 2.2 collective-permute-done.1
  46.9 5.5 %collective-permute-done.2 = bf16[32,1024]{1,0:T(8,128)(2,1)S(1)} collective-permute-done((bf16[32,1024]{1,0:T(8,128)(2,1)S(1)}, bf16[32,1024]{1,0:T(8,128)(2,1)S(1)}, u32[]{:S(2)}, u32[]{:S(2)}) %collective-permute-start.2) | collective-permute-done | bytes 65568 | tf_op jit(solution)/shard_map/ppermute | solution.py:25
  52.5 0.9 collective-permute-start.3
  54.9 9.8 %collective-permute-done.3 = bf16[128,1024]{1,0:T(8,128)(2,1)S(1)} collective-permute-done((bf16[128,1024]{1,0:T(8,128)(2,1)S(1)}, bf16[128,1024]{1,0:T(8,128)(2,1)S(1)}, u32[]{:S(2)}, u32[]{:S(2)}) %collective-permute-start.3) | collective-permute-done | bytes 262176 | tf_op jit(solution)/shard_map/ppermute | solution.py:25
  65.1 0.7 collective-permute-start.5
  65.9 2.7 %collective-permute-start.4 = (bf16[256,1024]{1,0:T(8,128)(2,1)S(1)}, bf16[256,1024]{1,0:T(8,128)(2,1)S(1)}, u32[]{:S(2)}, u32[]{:S(2)}) collective-permute-start(bf16[256,1024]{1,0:T(8,128)(2,1)S(1)} %bitcast.62), channel_id=1, source_target_pairs={{0,192},{64,0},{128,64},{192,128},{1,193},{65,1},{129,65},{193,129... | collective-permute-start | bytes 1572872 | tf_op jit(solution)/shard_map/ppermute | solution.py:28
  68.6 4.9 %fusion.1 = f32[1024,688]{0,1:T(8,128)} fusion(bf16[688,1024]{1,0:T(8,128)(2,1)S(1)} %copy-done, bf16[1024,1024]{1,0:T(8,128)(2,1)} %param.19, f32[1024]{0:T(1024)S(1)} %select_reduce_fusion), kind=kOutput, calls=%fused_computation.19 | convolution fusion | flops 1447395328 | bytes 6328320 | tf_op jit(solution)/shard_map/dot_general | solution.py:139
  73.5 4.6 %collective-permute-done.5 = bf16[256,1024]{1,0:T(8,128)(2,1)S(1)} collective-permute-done((bf16[256,1024]{1,0:T(8,128)(2,1)S(1)}, bf16[256,1024]{1,0:T(8,128)(2,1)S(1)}, u32[]{:S(2)}, u32[]{:S(2)}) %collective-permute-start.5) | collective-permute-done | bytes 524320 | tf_op jit(solution)/shard_map/ppermute | solution.py:25
  78.1 2.8 %select_convert_fusion = bf16[512,688]{0,1:T(8,128)(2,1)} fusion(f32[1024,688]{0,1:T(8,128)} %fusion.1, pred[]{:T(512)S(6)} %ne.35), kind=kLoop, calls=%fused_computation.24 | loop fusion | flops 352256 | bytes 2113537 | tf_op jit(solution)/shard_map/convert_element_type | solution.py:72
  80.9 9.1 %collective-permute-done.6 = bf16[256,1024]{1,0:T(8,128)(2,1)S(1)} collective-permute-done((bf16[256,1024]{1,0:T(8,128)(2,1)S(1)}, bf16[256,1024]{1,0:T(8,128)(2,1)S(1)}, u32[]{:S(2)}, u32[]{:S(2)}) %collective-permute-start.6) | collective-permute-done | bytes 524320 | tf_op jit(solution)/shard_map/ppermute | solution.py:25
  91.4 0.8 copy-done.10
  92.2 1.7 convolution_convert_fusion.5
  94.3 1.6 convolution_convert_fusion.6
  96.4 1.9 pad_maximum_fusion
  98.4 2.4 convert_add_fusion
  100.9 16.5 %collective-permute-done.8 = bf16[256,688]{0,1:T(8,128)(2,1)S(1)} collective-permute-done((bf16[256,688]{0,1:T(8,128)(2,1)S(1)}, bf16[256,688]{0,1:T(8,128)(2,1)S(1)}, u32[]{:S(2)}, u32[]{:S(2)}) %collective-permute-start.8) | collective-permute-done | bytes 352288 | tf_op jit(solution)/shard_map/ppermute | solution.py:72
  117.7 12.7 %collective-permute-done.9 = bf16[128,688]{0,1:T(8,128)(2,1)S(1)} collective-permute-done((bf16[128,688]{0,1:T(8,128)(2,1)S(1)}, bf16[128,688]{0,1:T(8,128)(2,1)S(1)}, u32[]{:S(2)}, u32[]{:S(2)}) %collective-permute-start.9) | collective-permute-done | bytes 176160 | tf_op jit(solution)/shard_map/ppermute | solution.py:72
  130.5 3.8 %collective-permute-start.10 = (bf16[128,688]{0,1:T(8,128)(2,1)S(1)}, bf16[128,688]{0,1:T(8,128)(2,1)S(1)}, u32[]{:S(2)}, u32[]{:S(2)}) collective-permute-start(bf16[128,688]{0,1:T(8,128)(2,1)S(1)} %add_convert_fusion), channel_id=1, source_target_pairs={{0,4},{2,6},{4,0},{6,2},{1,5},{3,7},{5,1},{7,3},{8,12},{10,14},{12... | collective-permute-start | bytes 528392 | tf_op jit(solution)/shard_map/ppermute | solution.py:78
  134.3 9.1 %collective-permute-done.10 = bf16[128,688]{0,1:T(8,128)(2,1)S(1)} collective-permute-done((bf16[128,688]{0,1:T(8,128)(2,1)S(1)}, bf16[128,688]{0,1:T(8,128)(2,1)S(1)}, u32[]{:S(2)}, u32[]{:S(2)}) %collective-permute-start.10) | collective-permute-done | bytes 176160 | tf_op jit(solution)/shard_map/ppermute | solution.py:78
  143.5 3.1 %collective-permute-start.11 = (bf16[256,688]{0,1:T(8,128)(2,1)S(1)}, bf16[256,688]{0,1:T(8,128)(2,1)S(1)}, u32[]{:S(2)}, u32[]{:S(2)}) collective-permute-start(bf16[256,688]{0,1:T(8,128)(2,1)S(1)} %maximum_select_fusion.2), channel_id=1, source_target_pairs={{0,2},{2,0},{4,6},{6,4},{1,3},{3,1},{5,7},{7,5},{8,10},{10,8},{12,... | collective-permute-start | bytes 1056776 | tf_op jit(solution)/shard_map/ppermute | solution.py:78
  146.6 5.3 %collective-permute-done.11 = bf16[256,688]{0,1:T(8,128)(2,1)S(1)} collective-permute-done((bf16[256,688]{0,1:T(8,128)(2,1)S(1)}, bf16[256,688]{0,1:T(8,128)(2,1)S(1)}, u32[]{:S(2)}, u32[]{:S(2)}) %collective-permute-start.11) | collective-permute-done | bytes 352288 | tf_op jit(solution)/shard_map/ppermute | solution.py:78
  151.9 1.1 maximum_select_fusion.1
  153.0 33.1 %all-reduce.2.cloned.1.call-done = bf16[1024,1377]{0,1:T(8,128)(2,1)} async-done(((bf16[1024,1377]{0,1:T(8,128)(2,1)}), bf16[1024,1377]{0,1:T(8,128)(2,1)}) %all-reduce.2.cloned.1.call-update) | async-done | bytes 2820112 | tf_op jit(solution)/shard_map/psum | solution.py:151
  186.1 2.5 convert_element_type.116
  188.6 0.8 multiply_convert_fusion.3
  189.5 1.6 copy-done.1
  191.1 1.8 convolution_convert_fusion
  192.9 1.5 copy.23
  194.4 4.3 %all-to-all-start.1 = ((bf16[4,4,2,32,1024]{4,3,2,1,0:T(8,128)(2,1)}), bf16[4,4,2,32,1024]{4,3,2,1,0:T(8,128)(2,1)S(1)}, u32[]{:S(2)}, u32[]{:S(2)}) async-start(bf16[4,4,2,32,1024]{4,3,2,1,0:T(8,128)(2,1)} %bitcast.60), calls=%async_computation.1 | async-start | bytes 4194304 | tf_op jit(solution)/shard_map/all_to_all | solution.py:51
  198.7 7.6 %convolution_convert_fusion.2 = bf16[1024,688]{0,1:T(8,128)(2,1)} fusion(bf16[1024,1024]{1,0:T(8,128)(2,1)} %copy-done.2, f32[1024,1377]{0,1:T(8,128)} %copy-done.1, f32[1024]{0:T(1024)S(1)} %bitcast.70, bf16[512,688]{0,1:T(8,128)(2,1)} %maximum_select_fusion.1, bf16[512,688]{0,1:T(8,128)(2,1)} %collective-permute-done.12, pred[]{:T(512)S(6)} %ne.35), kind=kOutput, calls=%fused_computation.16 | convolution fusion | flops 1459748864 | bytes 10555393 | tf_op jit(solution)/shard_map/dot_general | solution.py:176
  206.3 19.9 %all-to-all-done.1 = bf16[4,4,2,32,1024]{4,3,2,1,0:T(8,128)(2,1)S(1)} async-done(((bf16[4,4,2,32,1024]{4,3,2,1,0:T(8,128)(2,1)}), bf16[4,4,2,32,1024]{4,3,2,1,0:T(8,128)(2,1)S(1)}, u32[]{:S(2)}, u32[]{:S(2)}) %all-to-all-start.1) | async-done | bytes 2097184 | tf_op jit(solution)/shard_map/all_to_all | solution.py:51
  226.2 1.3 reduce_sum.81
  227.5 4.2 %all-to-all-start.2 = ((bf16[4,2,32,1024]{3,2,1,0:T(8,128)(2,1)}), bf16[4,2,32,1024]{3,2,1,0:T(8,128)(2,1)S(1)}, u32[]{:S(2)}, u32[]{:S(2)}) async-start(bf16[4,2,32,1024]{3,2,1,0:T(8,128)(2,1)} %reduce_sum.81), calls=%async_computation.2 | async-start | bytes 1048576 | tf_op jit(solution)/shard_map/all_to_all | solution.py:51
  231.8 6.5 %convolution_convert_fusion.1 = bf16[1024,688]{0,1:T(8,128)(2,1)} fusion(bf16[1024,1024]{1,0:T(8,128)(2,1)} %copy-done.2, f32[1024,1377]{0,1:T(8,128)} %copy-done.1, f32[1024]{0:T(1024)S(1)} %bitcast.71, bf16[512,688]{0,1:T(8,128)(2,1)} %maximum_select_fusion.1, bf16[512,688]{0,1:T(8,128)(2,1)} %collective-permute-done.12, pred[]{:T(512)S(6)} %ne.35), kind=kOutput, calls=%fused_computation.15 | convolution fusion | flops 1456226304 | bytes 7737345 | tf_op jit(solution)/shard_map/dot_general | solution.py:179
  238.2 3.3 %all-to-all-done.2 = bf16[4,2,32,1024]{3,2,1,0:T(8,128)(2,1)S(1)} async-done(((bf16[4,2,32,1024]{3,2,1,0:T(8,128)(2,1)}), bf16[4,2,32,1024]{3,2,1,0:T(8,128)(2,1)S(1)}, u32[]{:S(2)}, u32[]{:S(2)}) %all-to-all-start.2) | async-done | bytes 524320 | tf_op jit(solution)/shard_map/all_to_all | solution.py:51
  241.5 0.7 reduce_sum.82
  242.3 4.7 %all-to-all-start.3 = ((bf16[2,32,1024]{2,1,0:T(8,128)(2,1)}), bf16[2,32,1024]{2,1,0:T(8,128)(2,1)S(1)}, u32[]{:S(2)}, u32[]{:S(2)}) async-start(bf16[2,32,1024]{2,1,0:T(8,128)(2,1)} %reduce_sum.82), calls=%async_computation.3 | async-start | bytes 262144 | tf_op jit(solution)/shard_map/all_to_all | solution.py:51
  247.0 4.4 %convolution_convert_fusion.3 = bf16[688,1024]{1,0:T(8,128)(2,1)} fusion(bf16[1024,688]{0,1:T(8,128)(2,1)S(1)} %copy-done.4, bf16[1024,1024]{1,0:T(8,128)(2,1)} %param.19, f32[1024]{0:T(1024)S(1)} %select_reduce_fusion), kind=kOutput, calls=%fused_computation.17 | convolution fusion | flops 1446690816 | bytes 4919296 | tf_op jit(solution)/shard_map/dot_general | solution.py:164
  251.4 3.9 %all-to-all-done.3 = bf16[2,32,1024]{2,1,0:T(8,128)(2,1)S(1)} async-done(((bf16[2,32,1024]{2,1,0:T(8,128)(2,1)}), bf16[2,32,1024]{2,1,0:T(8,128)(2,1)S(1)}, u32[]{:S(2)}, u32[]{:S(2)}) %all-to-all-start.3) | async-done | bytes 131104 | tf_op jit(solution)/shard_map/all_to_all | solution.py:51
  (81 shorter events, 6.4 us)
Async XLA Ops:
  7.2 61.4 %copy-start = (bf16[688,1024]{1,0:T(8,128)(2,1)S(1)}, bf16[688,1024]{1,0:T(8,128)(2,1)}, u32[]{:S(2)}) copy-start(bf16[688,1024]{1,0:T(8,128)(2,1)} %param.18) | copy-start | bytes 4227076
  7.2 46.1 %copy-start.9 = (s32[32]{0:T(128)S(1)}, s32[32]{0:T(128)}, u32[]{:S(2)}) copy-start(s32[32]{0:T(128)} %param.14) | copy-start | bytes 388
  7.2 46.7 %copy-start.8 = (s32[32]{0:T(128)S(1)}, s32[32]{0:T(128)}, u32[]{:S(2)}) copy-start(s32[32]{0:T(128)} %param.13) | copy-start | bytes 388
  12.1 28.9 %all-to-all-start = ((bf16[32,4,1024]{2,1,0:T(4,128)(2,1)}), bf16[32,4,1024]{2,1,0:T(4,128)(2,1)S(1)}, u32[]{:S(2)}, u32[]{:S(2)}) async-start(bf16[32,4,1024]{2,1,0:T(4,128)(2,1)} %all_to_all.17), calls=%async_computation | async-start | bytes 524288 | tf_op jit(solution)/shard_map/all_to_all | solution.py:115
  25.2 160.9 %all-reduce.2.cloned.1.call-start = ((), (), s32[]{:S(2)}) async-start(), calls=%async_computation.4 | async-start | bytes 5668864 | tf_op jit(solution)/shard_map/psum | solution.py:151
  41.3 23.4 %copy-start.5 = (bf16[32,1024]{1,0:T(8,128)(2,1)}, bf16[32,1024]{1,0:T(8,128)(2,1)S(1)}, u32[]{:S(2)}) copy-start(bf16[32,1024]{1,0:T(8,128)(2,1)S(1)} %get-tuple-element.5) | copy-start | bytes 196612
  41.3 5.6 %collective-permute-start.1 = (bf16[32,1024]{1,0:T(8,128)(2,1)S(1)}, bf16[32,1024]{1,0:T(8,128)(2,1)S(1)}, u32[]{:S(2)}, u32[]{:S(2)}) collective-permute-start(bf16[32,1024]{1,0:T(8,128)(2,1)S(1)} %get-tuple-element.5), channel_id=1, source_target_pairs={{0,8},{8,16},{16,24},{24,0},{1,9},{9,17},{17,25},{25,1},{2,10},{10... | collective-permute-start | bytes 196616 | tf_op jit(solution)/shard_map/ppermute | solution.py:25
  42.3 4.6 %collective-permute-start = (bf16[32,1024]{1,0:T(8,128)(2,1)S(1)}, bf16[32,1024]{1,0:T(8,128)(2,1)S(1)}, u32[]{:S(2)}, u32[]{:S(2)}) collective-permute-start(bf16[32,1024]{1,0:T(8,128)(2,1)S(1)} %get-tuple-element.5), channel_id=1, source_target_pairs={{0,24},{8,0},{16,8},{24,16},{1,25},{9,1},{17,9},{25,17},{2,26},{10... | collective-permute-start | bytes 196616 | tf_op jit(solution)/shard_map/ppermute | solution.py:28
  46.9 5.5 %collective-permute-start.2 = (bf16[32,1024]{1,0:T(8,128)(2,1)S(1)}, bf16[32,1024]{1,0:T(8,128)(2,1)S(1)}, u32[]{:S(2)}, u32[]{:S(2)}) collective-permute-start(bf16[32,1024]{1,0:T(8,128)(2,1)S(1)} %collective-permute-done.1), channel_id=1, source_target_pairs={{0,8},{8,16},{16,24},{24,0},{1,9},{9,17},{17,25},{25,1},{2,10},{10... | collective-permute-start | bytes 196616 | tf_op jit(solution)/shard_map/ppermute | solution.py:25
  52.5 12.3 %collective-permute-start.3 = (bf16[128,1024]{1,0:T(8,128)(2,1)S(1)}, bf16[128,1024]{1,0:T(8,128)(2,1)S(1)}, u32[]{:S(2)}, u32[]{:S(2)}) collective-permute-start(bf16[128,1024]{1,0:T(8,128)(2,1)S(1)} %bitcast.66), channel_id=1, source_target_pairs={{0,32},{32,0},{1,33},{33,1},{2,34},{34,2},{3,35},{35,3},{4,36},{36... | collective-permute-start | bytes 786440 | tf_op jit(solution)/shard_map/ppermute | solution.py:25
  65.1 13.0 %collective-permute-start.5 = (bf16[256,1024]{1,0:T(8,128)(2,1)S(1)}, bf16[256,1024]{1,0:T(8,128)(2,1)S(1)}, u32[]{:S(2)}, u32[]{:S(2)}) collective-permute-start(bf16[256,1024]{1,0:T(8,128)(2,1)S(1)} %bitcast.61), channel_id=1, source_target_pairs={{0,64},{64,128},{128,192},{192,0},{1,65},{65,129},{129,193},{193,1... | collective-permute-start | bytes 1572872 | tf_op jit(solution)/shard_map/ppermute | solution.py:25
  65.9 14.9 %copy-start.7 = (bf16[1024]{0:T(1024)(128)(2,1)S(1)}, bf16[1024]{0:T(1024)(128)(2,1)}, u32[]{:S(2)}) copy-start(bf16[1024]{0:T(1024)(128)(2,1)} %param.15) | copy-start | bytes 6148
  65.9 15.0 %collective-permute-start.4 = (bf16[256,1024]{1,0:T(8,128)(2,1)S(1)}, bf16[256,1024]{1,0:T(8,128)(2,1)S(1)}, u32[]{:S(2)}, u32[]{:S(2)}) collective-permute-start(bf16[256,1024]{1,0:T(8,128)(2,1)S(1)} %bitcast.62), channel_id=1, source_target_pairs={{0,192},{64,0},{128,64},{192,128},{1,193},{65,1},{129,65},{193,129... | collective-permute-start | bytes 1572872 | tf_op jit(solution)/shard_map/ppermute | solution.py:28
  78.0 12.0 %collective-permute-start.6 = (bf16[256,1024]{1,0:T(8,128)(2,1)S(1)}, bf16[256,1024]{1,0:T(8,128)(2,1)S(1)}, u32[]{:S(2)}, u32[]{:S(2)}) collective-permute-start(bf16[256,1024]{1,0:T(8,128)(2,1)S(1)} %collective-permute-done.5), channel_id=1, source_target_pairs={{0,64},{64,128},{128,192},{192,0},{1,65},{65,129},{129,193},{193,1... | collective-permute-start | bytes 1572872 | tf_op jit(solution)/shard_map/ppermute | solution.py:25
  80.8 17.5 %collective-permute-start.7 = (bf16[512,688]{0,1:T(8,128)(2,1)}, bf16[512,688]{0,1:T(8,128)(2,1)}, u32[]{:S(2)}, u32[]{:S(2)}) collective-permute-start(bf16[512,688]{0,1:T(8,128)(2,1)} %select_convert_fusion), channel_id=1, source_target_pairs={{0,1},{1,0},{2,3},{3,2},{4,5},{5,4},{6,7},{7,6},{8,9},{9,8},{10,11... | collective-permute-start | bytes 2113544 | tf_op jit(solution)/shard_map/ppermute | solution.py:72
  90.8 1.4 copy-start.10
  92.2 1.7 copy-start.2
  92.2 2.1 copy-start.11
  100.8 16.6 %collective-permute-start.8 = (bf16[256,688]{0,1:T(8,128)(2,1)S(1)}, bf16[256,688]{0,1:T(8,128)(2,1)S(1)}, u32[]{:S(2)}, u32[]{:S(2)}) collective-permute-start(bf16[256,688]{0,1:T(8,128)(2,1)S(1)} %select_convert_fusion.1), channel_id=1, source_target_pairs={{0,2},{2,0},{4,6},{6,4},{1,3},{3,1},{5,7},{7,5},{8,10},{10,8},{12,... | collective-permute-start | bytes 1056776 | tf_op jit(solution)/shard_map/ppermute | solution.py:72
  117.6 12.8 %collective-permute-start.9 = (bf16[128,688]{0,1:T(8,128)(2,1)S(1)}, bf16[128,688]{0,1:T(8,128)(2,1)S(1)}, u32[]{:S(2)}, u32[]{:S(2)}) collective-permute-start(bf16[128,688]{0,1:T(8,128)(2,1)S(1)} %select_convert_fusion.2), channel_id=1, source_target_pairs={{0,4},{2,6},{4,0},{6,2},{1,5},{3,7},{5,1},{7,3},{8,12},{10,14},{12... | collective-permute-start | bytes 528392 | tf_op jit(solution)/shard_map/ppermute | solution.py:72
  130.5 12.8 %collective-permute-start.10 = (bf16[128,688]{0,1:T(8,128)(2,1)S(1)}, bf16[128,688]{0,1:T(8,128)(2,1)S(1)}, u32[]{:S(2)}, u32[]{:S(2)}) collective-permute-start(bf16[128,688]{0,1:T(8,128)(2,1)S(1)} %add_convert_fusion), channel_id=1, source_target_pairs={{0,4},{2,6},{4,0},{6,2},{1,5},{3,7},{5,1},{7,3},{8,12},{10,14},{12... | collective-permute-start | bytes 528392 | tf_op jit(solution)/shard_map/ppermute | solution.py:78
  143.5 8.4 %collective-permute-start.11 = (bf16[256,688]{0,1:T(8,128)(2,1)S(1)}, bf16[256,688]{0,1:T(8,128)(2,1)S(1)}, u32[]{:S(2)}, u32[]{:S(2)}) collective-permute-start(bf16[256,688]{0,1:T(8,128)(2,1)S(1)} %maximum_select_fusion.2), channel_id=1, source_target_pairs={{0,2},{2,0},{4,6},{6,4},{1,3},{3,1},{5,7},{7,5},{8,10},{10,8},{12,... | collective-permute-start | bytes 1056776 | tf_op jit(solution)/shard_map/ppermute | solution.py:78
  153.0 45.7 %collective-permute-start.12 = (bf16[512,688]{0,1:T(8,128)(2,1)}, bf16[512,688]{0,1:T(8,128)(2,1)}, u32[]{:S(2)}, u32[]{:S(2)}) collective-permute-start(bf16[512,688]{0,1:T(8,128)(2,1)} %maximum_select_fusion.1), channel_id=1, source_target_pairs={{0,1},{1,0},{2,3},{3,2},{4,5},{5,4},{6,7},{7,6},{8,9},{9,8},{10,11... | collective-permute-start | bytes 2113544 | tf_op jit(solution)/shard_map/ppermute | solution.py:78
  188.6 2.5 copy-start.1
  191.1 1.8 copy-start.3
  194.4 31.8 %all-to-all-start.1 = ((bf16[4,4,2,32,1024]{4,3,2,1,0:T(8,128)(2,1)}), bf16[4,4,2,32,1024]{4,3,2,1,0:T(8,128)(2,1)S(1)}, u32[]{:S(2)}, u32[]{:S(2)}) async-start(bf16[4,4,2,32,1024]{4,3,2,1,0:T(8,128)(2,1)} %bitcast.60), calls=%async_computation.1 | async-start | bytes 4194304 | tf_op jit(solution)/shard_map/all_to_all | solution.py:51
  227.5 14.0 %all-to-all-start.2 = ((bf16[4,2,32,1024]{3,2,1,0:T(8,128)(2,1)}), bf16[4,2,32,1024]{3,2,1,0:T(8,128)(2,1)S(1)}, u32[]{:S(2)}, u32[]{:S(2)}) async-start(bf16[4,2,32,1024]{3,2,1,0:T(8,128)(2,1)} %reduce_sum.81), calls=%async_computation.2 | async-start | bytes 1048576 | tf_op jit(solution)/shard_map/all_to_all | solution.py:51
  231.8 15.2 %copy-start.4 = (bf16[1024,688]{0,1:T(8,128)(2,1)S(1)}, bf16[1024,688]{0,1:T(8,128)(2,1)}, u32[]{:S(2)}) copy-start(bf16[1024,688]{0,1:T(8,128)(2,1)} %copy-done.3) | copy-start | bytes 4227076
  242.3 13.1 %all-to-all-start.3 = ((bf16[2,32,1024]{2,1,0:T(8,128)(2,1)}), bf16[2,32,1024]{2,1,0:T(8,128)(2,1)S(1)}, u32[]{:S(2)}, u32[]{:S(2)}) async-start(bf16[2,32,1024]{2,1,0:T(8,128)(2,1)} %reduce_sum.82), calls=%async_computation.3 | async-start | bytes 262144 | tf_op jit(solution)/shard_map/all_to_all | solution.py:51
  247.0 8.4 %copy-start.6 = (bf16[32,1024]{1,0:T(8,128)(2,1)S(1)}, bf16[32,1024]{1,0:T(8,128)(2,1)}, u32[]{:S(2)}) copy-start(bf16[32,1024]{1,0:T(8,128)(2,1)} %copy-done.5) | copy-start | bytes 196612
Sparse Core Ops, SparseCore 0:
  98.5 87.5 all-reduce.1

commit v6 on v5

--- a/solution.py
+++ b/solution.py
@@ -139,7 +139,8 @@
     hidden_term = lax.dot_general(
         out_grad, w_down, (((1,), (1,)), ((), ())), preferred_element_type=f32
     ).astype(bf16)
-    hidden_sum = pair_allreduce(hidden_term, MP)
+    hidden_sum = lax.psum(hidden_term, MP)
+    hidden_sum, train_rows = lax.optimization_barrier((hidden_sum, train_rows))
     grad_hidden = hidden_sum.astype(f32)
 
     rows_float = train_rows.astype(f32)
@@ -148,7 +149,7 @@
     gate_term = jnp.dot(scaled, w_gate, preferred_element_type=f32)
     up_term = jnp.dot(scaled, w_up, preferred_element_type=f32)
     packed = jnp.concatenate([gate_term, up_term, squares[:, None]], axis=1).astype(bf16)
-    total = lax.psum(packed, MP).astype(f32)
+    total = pair_allreduce(packed, MP).astype(f32)
     gate_total = total[:, :hidden_dev]
     up_total = total[:, hidden_dev : 2 * hidden_dev]
     square_total = total[:, 2 * hidden_dev]

time: 264 us -> 332 us (1.26)
  waiting for transfers between devices: 151 us -> 208 us
  starting transfers between devices: 41 us -> 46.8 us
    psum x1, waiting for transfers between devices: 33.1 us -> 61.9 us  [body(): hidden_sum = lax.psum(hidden_term, MP)]
    ppermute x3, waiting for transfers between devices: 14.4 us -> 33.5 us  [pair_allreduce(): got = lax.ppermute(held, name, pairs)]
    ppermute x3, waiting for transfers between devices: 29.3 us -> 34.8 us  [pair_allreduce(): got = lax.ppermute(give.astype(part.dtype), name, pairs)]
    ppermute x3, starting transfers between devices: 0.19 us -> 5.42 us  [pair_allreduce(): got = lax.ppermute(give.astype(part.dtype), name, pairs)]
    add x2, other arithmetic: 2.47 us -> 6.1 us  [pair_allreduce(): held = keep + got.astype(jnp.float32)]
  transfers between devices with their start and end apart: 18 -> 18, of which waited for: 14 -> 16; matrix products, arithmetic and copies ran while one was open for 17% -> 7% of each run, Pallas kernels for 0% -> 0%
where the time goes in v6:
time: 332 us; the launch traced here: 330 us
  waiting for transfers between devices  208 us (63%)
  starting transfers between devices  46.8 us (14%)
  matrix products  29.4 us (9%)
  other arithmetic  21.7 us (7%)
  between operations  14.5 us (4%)
  local copies, waits for them, and re-layouts  9.84 us (3%)
    psum x1, waiting for transfers between devices, body(): hidden_sum = lax.psum(hidden_term, MP)  61.9 us
    ppermute x3, waiting for transfers between devices, pair_allreduce(): got = lax.ppermute(give.astype(part.dtype), name, pairs)  34.8 us
    ppermute x5, waiting for transfers between devices, ring_gather(): from_left = lax.ppermute(from_left, name, ahead)  34.4 us
    ppermute x3, waiting for transfers between devices, pair_allreduce(): got = lax.ppermute(held, name, pairs)  33.5 us
    all_to_all x3, waiting for transfers between devices, staged_scatter(): arrived = lax.all_to_all(held, name, 0, 0, tiled=True)  27.8 us
    all_to_all x1, waiting for transfers between devices, body(): received = lax.all_to_all(outgoing, DP, 0, 0, tiled=True)  15.8 us
    all_to_all x3, starting transfers between devices, staged_scatter(): arrived = lax.all_to_all(held, name, 0, 0, tiled=True)  13.6 us
    all_to_all x1, starting transfers between devices, body(): received = lax.all_to_all(outgoing, DP, 0, 0, tiled=True)  13 us
  transfers between devices with their start and end apart: 18, of which 16 were waited for; matrix products, arithmetic and copies ran while one was open for 7% of the time, Pallas kernels for 0%

profile of v6, /device:TPU:32, one launch (start us, length us, event | category | flops | bytes accessed | tf_op | source)
XLA Modules:
  0.0 330.5 jit_solution(3913396042761538009)
XLA Ops:
  7.2 0.9 reshape.101
  10.0 1.3 convolution_convert_fusion.7
  12.1 13.0 %all-to-all-start = ((bf16[32,4,1024]{2,1,0:T(4,128)(2,1)}), bf16[32,4,1024]{2,1,0:T(4,128)(2,1)S(1)}, u32[]{:S(2)}, u32[]{:S(2)}) async-start(bf16[32,4,1024]{2,1,0:T(4,128)(2,1)} %all_to_all.17), calls=%async_computation | async-start | bytes 524288 | tf_op jit(solution)/shard_map/all_to_all | solution.py:115
  25.3 15.8 %all-to-all-done = bf16[32,4,1024]{2,1,0:T(4,128)(2,1)S(1)} async-done(((bf16[32,4,1024]{2,1,0:T(4,128)(2,1)}), bf16[32,4,1024]{2,1,0:T(4,128)(2,1)S(1)}, u32[]{:S(2)}, u32[]{:S(2)}) %all-to-all-start) | async-done | bytes 262176 | tf_op jit(solution)/shard_map/all_to_all | solution.py:115
  41.3 1.0 collective-permute-start.1
  42.3 2.3 collective-permute-start
  44.6 2.2 collective-permute-done.1
  46.9 5.5 %collective-permute-done.2 = bf16[32,1024]{1,0:T(8,128)(2,1)S(1)} collective-permute-done((bf16[32,1024]{1,0:T(8,128)(2,1)S(1)}, bf16[32,1024]{1,0:T(8,128)(2,1)S(1)}, u32[]{:S(2)}, u32[]{:S(2)}) %collective-permute-start.2) | collective-permute-done | bytes 65568 | tf_op jit(solution)/shard_map/ppermute | solution.py:25
  52.5 0.9 collective-permute-start.3
  53.3 11.4 %collective-permute-done.3 = bf16[128,1024]{1,0:T(8,128)(2,1)S(1)} collective-permute-done((bf16[128,1024]{1,0:T(8,128)(2,1)S(1)}, bf16[128,1024]{1,0:T(8,128)(2,1)S(1)}, u32[]{:S(2)}, u32[]{:S(2)}) %collective-permute-start.3) | collective-permute-done | bytes 262176 | tf_op jit(solution)/shard_map/ppermute | solution.py:25
  67.4 2.7 collective-permute-start.4
  70.2 7.9 %collective-permute-done.5 = bf16[256,1024]{1,0:T(8,128)(2,1)S(1)} collective-permute-done((bf16[256,1024]{1,0:T(8,128)(2,1)S(1)}, bf16[256,1024]{1,0:T(8,128)(2,1)S(1)}, u32[]{:S(2)}, u32[]{:S(2)}) %collective-permute-start.5) | collective-permute-done | bytes 524320 | tf_op jit(solution)/shard_map/ppermute | solution.py:25
  78.1 4.4 %convolution_convert_fusion.6 = bf16[1024,688]{0,1:T(8,128)(2,1)} fusion(bf16[688,1024]{1,0:T(8,128)(2,1)S(1)} %copy-done, bf16[1024,1024]{1,0:T(8,128)(2,1)} %param.19, f32[1024]{0:T(1024)S(1)} %select_reduce_fusion), kind=kOutput, calls=%fused_computation.24 | convolution fusion | flops 1446690816 | bytes 4919296 | tf_op jit(solution)/shard_map/dot_general | solution.py:139
  82.6 7.4 %collective-permute-done.6 = bf16[256,1024]{1,0:T(8,128)(2,1)S(1)} collective-permute-done((bf16[256,1024]{1,0:T(8,128)(2,1)S(1)}, bf16[256,1024]{1,0:T(8,128)(2,1)S(1)}, u32[]{:S(2)}, u32[]{:S(2)}) %collective-permute-start.6) | collective-permute-done | bytes 524320 | tf_op jit(solution)/shard_map/ppermute | solution.py:25
  90.5 61.9 %all-reduce.2.cloned.1.call-done = bf16[1024,688]{0,1:T(8,128)(2,1)} async-done(((bf16[1024,688]{0,1:T(8,128)(2,1)}), bf16[1024,688]{0,1:T(8,128)(2,1)}) %all-reduce.2.cloned.1.call-update) | async-done | bytes 1409040 | tf_op jit(solution)/shard_map/psum | solution.py:142
  152.9 3.1 convolution_convert_fusion.4
  156.0 1.7 convolution_convert_fusion.5
  158.4 2.5 copy-done.1
  160.9 1.4 select_convert_fusion
  162.3 3.5 %collective-permute-done.7 = bf16[512,1377]{0,1:T(8,128)(2,1)} collective-permute-done((bf16[512,1377]{0,1:T(8,128)(2,1)}, bf16[512,1377]{0,1:T(8,128)(2,1)}, u32[]{:S(2)}, u32[]{:S(2)}) %collective-permute-start.7) | collective-permute-done | bytes 1410080 | tf_op jit(solution)/shard_map/ppermute | solution.py:72
  165.8 3.9 %convert_add_fusion = f32[512,1377]{0,1:T(8,128)S(1)} fusion(bf16[512,1377]{0,1:T(8,128)(2,1)} %collective-permute-done.7, f32[1024,1377]{0,1:T(8,128)} %copy-done.1, pred[]{:T(512)S(6)} %ne.32), kind=kLoop, calls=%fused_computation.8 | loop fusion | flops 2115072 | bytes 9870337 | tf_op jit(solution)/shard_map/add | solution.py:73
  169.7 1.5 copy-done.3
  171.2 1.0 select_convert_fusion.1
  172.2 3.1 collective-permute-start.8
  175.3 16.5 %collective-permute-done.8 = bf16[256,1377]{0,1:T(8,128)(2,1)} collective-permute-done((bf16[256,1377]{0,1:T(8,128)(2,1)}, bf16[256,1377]{0,1:T(8,128)(2,1)}, u32[]{:S(2)}, u32[]{:S(2)}) %collective-permute-start.8) | collective-permute-done | bytes 705056 | tf_op jit(solution)/shard_map/ppermute | solution.py:72
  191.8 2.2 convert_add_fusion.1
  194.1 2.3 collective-permute-start.9
  196.4 14.8 %collective-permute-done.9 = bf16[128,1377]{0,1:T(8,128)(2,1)S(1)} collective-permute-done((bf16[128,1377]{0,1:T(8,128)(2,1)S(1)}, bf16[128,1377]{0,1:T(8,128)(2,1)S(1)}, u32[]{:S(2)}, u32[]{:S(2)}) %collective-permute-start.9) | collective-permute-done | bytes 352544 | tf_op jit(solution)/shard_map/ppermute | solution.py:72
  211.4 3.5 %collective-permute-start.10 = (bf16[128,1377]{0,1:T(8,128)(2,1)S(1)}, bf16[128,1377]{0,1:T(8,128)(2,1)S(1)}, u32[]{:S(2)}, u32[]{:S(2)}) collective-permute-start(bf16[128,1377]{0,1:T(8,128)(2,1)S(1)} %add_convert_fusion), channel_id=1, source_target_pairs={{0,4},{2,6},{4,0},{6,2},{1,5},{3,7},{5,1},{7,3},{8,12},{10,14},{12... | collective-permute-start | bytes 1057544 | tf_op jit(solution)/shard_map/ppermute | solution.py:78
  214.8 14.3 %collective-permute-done.10 = bf16[128,1377]{0,1:T(8,128)(2,1)S(1)} collective-permute-done((bf16[128,1377]{0,1:T(8,128)(2,1)S(1)}, bf16[128,1377]{0,1:T(8,128)(2,1)S(1)}, u32[]{:S(2)}, u32[]{:S(2)}) %collective-permute-start.10) | collective-permute-done | bytes 352544 | tf_op jit(solution)/shard_map/ppermute | solution.py:78
  229.4 3.3 %collective-permute-start.11 = (bf16[256,1377]{0,1:T(8,128)(2,1)S(1)}, bf16[256,1377]{0,1:T(8,128)(2,1)S(1)}, u32[]{:S(2)}, u32[]{:S(2)}) collective-permute-start(bf16[256,1377]{0,1:T(8,128)(2,1)S(1)} %maximum_select_fusion.2), channel_id=1, source_target_pairs={{0,2},{2,0},{4,6},{6,4},{1,3},{3,1},{5,7},{7,5},{8,10},{10,8},{12,... | collective-permute-start | bytes 2115080 | tf_op jit(solution)/shard_map/ppermute | solution.py:78
  232.7 16.1 %collective-permute-done.11 = bf16[256,1377]{0,1:T(8,128)(2,1)S(1)} collective-permute-done((bf16[256,1377]{0,1:T(8,128)(2,1)S(1)}, bf16[256,1377]{0,1:T(8,128)(2,1)S(1)}, u32[]{:S(2)}, u32[]{:S(2)}) %collective-permute-start.11) | collective-permute-done | bytes 705056 | tf_op jit(solution)/shard_map/ppermute | solution.py:78
  249.4 3.2 collective-permute-done.12
  252.6 1.4 fusion.2
  254.9 1.6 copy-done.2
  256.5 1.8 convolution_convert_fusion
  258.4 1.6 copy.22
  260.0 4.5 %all-to-all-start.1 = ((bf16[4,4,2,32,1024]{4,3,2,1,0:T(8,128)(2,1)}), bf16[4,4,2,32,1024]{4,3,2,1,0:T(8,128)(2,1)}, u32[]{:S(2)}, u32[]{:S(2)}) async-start(bf16[4,4,2,32,1024]{4,3,2,1,0:T(8,128)(2,1)} %bitcast.52), calls=%async_computation.1 | async-start | bytes 4194304 | tf_op jit(solution)/shard_map/all_to_all | solution.py:51
  264.4 6.7 %convolution_convert_fusion.2 = bf16[1024,688]{0,1:T(8,128)(2,1)} fusion(bf16[1024,688]{0,1:T(8,128)(2,1)} %all-reduce.2.cloned.1.call-done, f32[1024,1377]{0,1:T(8,128)} %copy-done.2, f32[1024]{0:T(1024)S(1)} %bitcast.62, bf16[1024,1024]{1,0:T(8,128)(2,1)S(1)} %bitcast.50, f32[1024]{0:T(1024)S(1)} %convert_element_type.111), kind=kOutput, calls=%fused_computation.20 | convolution fusion | flops 1456553984 | bytes 10559488 | tf_op jit(solution)/shard_map/dot_general | solution.py:177
  271.1 20.3 %all-to-all-done.1 = bf16[4,4,2,32,1024]{4,3,2,1,0:T(8,128)(2,1)} async-done(((bf16[4,4,2,32,1024]{4,3,2,1,0:T(8,128)(2,1)}), bf16[4,4,2,32,1024]{4,3,2,1,0:T(8,128)(2,1)}, u32[]{:S(2)}, u32[]{:S(2)}) %all-to-all-start.1) | async-done | bytes 2097184 | tf_op jit(solution)/shard_map/all_to_all | solution.py:51
  291.4 2.9 reduce_sum.83
  294.3 4.1 %all-to-all-start.2 = ((bf16[4,2,32,1024]{3,2,1,0:T(8,128)(2,1)}), bf16[4,2,32,1024]{3,2,1,0:T(8,128)(2,1)}, u32[]{:S(2)}, u32[]{:S(2)}) async-start(bf16[4,2,32,1024]{3,2,1,0:T(8,128)(2,1)} %reduce_sum.83), calls=%async_computation.2 | async-start | bytes 1048576 | tf_op jit(solution)/shard_map/all_to_all | solution.py:51
  298.5 5.3 %convolution_convert_fusion.1 = bf16[1024,688]{0,1:T(8,128)(2,1)} fusion(bf16[1024,688]{0,1:T(8,128)(2,1)} %all-reduce.2.cloned.1.call-done, f32[1024,1377]{0,1:T(8,128)} %copy-done.2, f32[1024]{0:T(1024)S(1)} %bitcast.63, bf16[1024,1024]{1,0:T(8,128)(2,1)S(1)} %bitcast.51, f32[1024]{0:T(1024)S(1)} %convert_element_type.111), kind=kOutput, calls=%fused_computation.19 | convolution fusion | flops 1453031424 | bytes 7741440 | tf_op jit(solution)/shard_map/dot_general | solution.py:180
  303.8 4.0 %all-to-all-done.2 = bf16[4,2,32,1024]{3,2,1,0:T(8,128)(2,1)} async-done(((bf16[4,2,32,1024]{3,2,1,0:T(8,128)(2,1)}), bf16[4,2,32,1024]{3,2,1,0:T(8,128)(2,1)}, u32[]{:S(2)}, u32[]{:S(2)}) %all-to-all-start.2) | async-done | bytes 524320 | tf_op jit(solution)/shard_map/all_to_all | solution.py:51
  307.7 1.8 reduce_sum.84
  309.5 5.0 %all-to-all-start.3 = ((bf16[2,32,1024]{2,1,0:T(8,128)(2,1)}), bf16[2,32,1024]{2,1,0:T(8,128)(2,1)S(1)}, u32[]{:S(2)}, u32[]{:S(2)}) async-start(bf16[2,32,1024]{2,1,0:T(8,128)(2,1)} %reduce_sum.84), calls=%async_computation.3 | async-start | bytes 262144 | tf_op jit(solution)/shard_map/all_to_all | solution.py:51
  314.6 4.9 %convolution_convert_fusion.3 = bf16[688,1024]{1,0:T(8,128)(2,1)} fusion(bf16[1024,688]{0,1:T(8,128)(2,1)} %copy-done.4, bf16[1024,1024]{1,0:T(8,128)(2,1)} %param.19, f32[1024]{0:T(1024)S(1)} %select_reduce_fusion), kind=kOutput, calls=%fused_computation.21 | convolution fusion | flops 1446690816 | bytes 4919296 | tf_op jit(solution)/shard_map/dot_general | solution.py:165
  319.4 3.5 %all-to-all-done.3 = bf16[2,32,1024]{2,1,0:T(8,128)(2,1)S(1)} async-done(((bf16[2,32,1024]{2,1,0:T(8,128)(2,1)}), bf16[2,32,1024]{2,1,0:T(8,128)(2,1)S(1)}, u32[]{:S(2)}, u32[]{:S(2)}) %all-to-all-start.3) | async-done | bytes 131104 | tf_op jit(solution)/shard_map/all_to_all | solution.py:51
  (78 shorter events, 10.2 us)
Async XLA Ops:
  7.2 70.9 %copy-start = (bf16[688,1024]{1,0:T(8,128)(2,1)S(1)}, bf16[688,1024]{1,0:T(8,128)(2,1)}, u32[]{:S(2)}) copy-start(bf16[688,1024]{1,0:T(8,128)(2,1)} %param.18) | copy-start | bytes 4227076
  7.2 58.6 %copy-start.8 = (s32[32]{0:T(128)S(1)}, s32[32]{0:T(128)}, u32[]{:S(2)}) copy-start(s32[32]{0:T(128)} %param.13) | copy-start | bytes 388
  7.2 58.9 %copy-start.9 = (s32[32]{0:T(128)S(1)}, s32[32]{0:T(128)}, u32[]{:S(2)}) copy-start(s32[32]{0:T(128)} %param.14) | copy-start | bytes 388
  12.1 28.9 %all-to-all-start = ((bf16[32,4,1024]{2,1,0:T(4,128)(2,1)}), bf16[32,4,1024]{2,1,0:T(4,128)(2,1)S(1)}, u32[]{:S(2)}, u32[]{:S(2)}) async-start(bf16[32,4,1024]{2,1,0:T(4,128)(2,1)} %all_to_all.17), calls=%async_computation | async-start | bytes 524288 | tf_op jit(solution)/shard_map/all_to_all | solution.py:115
  25.2 127.2 %all-reduce.2.cloned.1.call-start = ((), (), s32[]{:S(2)}) async-start(), calls=%async_computation.4 | async-start | bytes 2818048 | tf_op jit(solution)/shard_map/psum | solution.py:142
  41.3 23.4 %copy-start.5 = (bf16[32,1024]{1,0:T(8,128)(2,1)}, bf16[32,1024]{1,0:T(8,128)(2,1)S(1)}, u32[]{:S(2)}) copy-start(bf16[32,1024]{1,0:T(8,128)(2,1)S(1)} %get-tuple-element.9) | copy-start | bytes 196612
  41.3 5.6 %collective-permute-start.1 = (bf16[32,1024]{1,0:T(8,128)(2,1)S(1)}, bf16[32,1024]{1,0:T(8,128)(2,1)S(1)}, u32[]{:S(2)}, u32[]{:S(2)}) collective-permute-start(bf16[32,1024]{1,0:T(8,128)(2,1)S(1)} %get-tuple-element.9), channel_id=1, source_target_pairs={{0,8},{8,16},{16,24},{24,0},{1,9},{9,17},{17,25},{25,1},{2,10},{10... | collective-permute-start | bytes 196616 | tf_op jit(solution)/shard_map/ppermute | solution.py:25
  42.3 4.6 %collective-permute-start = (bf16[32,1024]{1,0:T(8,128)(2,1)S(1)}, bf16[32,1024]{1,0:T(8,128)(2,1)S(1)}, u32[]{:S(2)}, u32[]{:S(2)}) collective-permute-start(bf16[32,1024]{1,0:T(8,128)(2,1)S(1)} %get-tuple-element.9), channel_id=1, source_target_pairs={{0,24},{8,0},{16,8},{24,16},{1,25},{9,1},{17,9},{25,17},{2,26},{10... | collective-permute-start | bytes 196616 | tf_op jit(solution)/shard_map/ppermute | solution.py:28
  46.9 5.5 %collective-permute-start.2 = (bf16[32,1024]{1,0:T(8,128)(2,1)S(1)}, bf16[32,1024]{1,0:T(8,128)(2,1)S(1)}, u32[]{:S(2)}, u32[]{:S(2)}) collective-permute-start(bf16[32,1024]{1,0:T(8,128)(2,1)S(1)} %collective-permute-done.1), channel_id=1, source_target_pairs={{0,8},{8,16},{16,24},{24,0},{1,9},{9,17},{17,25},{25,1},{2,10},{10... | collective-permute-start | bytes 196616 | tf_op jit(solution)/shard_map/ppermute | solution.py:25
  52.5 12.3 %collective-permute-start.3 = (bf16[128,1024]{1,0:T(8,128)(2,1)S(1)}, bf16[128,1024]{1,0:T(8,128)(2,1)S(1)}, u32[]{:S(2)}, u32[]{:S(2)}) collective-permute-start(bf16[128,1024]{1,0:T(8,128)(2,1)S(1)} %bitcast.58), channel_id=1, source_target_pairs={{0,32},{32,0},{1,33},{33,1},{2,34},{34,2},{3,35},{35,3},{4,36},{36... | collective-permute-start | bytes 786440 | tf_op jit(solution)/shard_map/ppermute | solution.py:25
  65.1 13.0 %collective-permute-start.5 = (bf16[256,1024]{1,0:T(8,128)(2,1)S(1)}, bf16[256,1024]{1,0:T(8,128)(2,1)S(1)}, u32[]{:S(2)}, u32[]{:S(2)}) collective-permute-start(bf16[256,1024]{1,0:T(8,128)(2,1)S(1)} %bitcast.53), channel_id=1, source_target_pairs={{0,64},{64,128},{128,192},{192,0},{1,65},{65,129},{129,193},{193,1... | collective-permute-start | bytes 1572872 | tf_op jit(solution)/shard_map/ppermute | solution.py:25
  67.4 15.1 %copy-start.7 = (bf16[1024]{0:T(1024)(128)(2,1)S(1)}, bf16[1024]{0:T(1024)(128)(2,1)}, u32[]{:S(2)}) copy-start(bf16[1024]{0:T(1024)(128)(2,1)} %param.15) | copy-start | bytes 6148
  67.4 15.2 %collective-permute-start.4 = (bf16[256,1024]{1,0:T(8,128)(2,1)S(1)}, bf16[256,1024]{1,0:T(8,128)(2,1)S(1)}, u32[]{:S(2)}, u32[]{:S(2)}) collective-permute-start(bf16[256,1024]{1,0:T(8,128)(2,1)S(1)} %bitcast.54), channel_id=1, source_target_pairs={{0,192},{64,0},{128,64},{192,128},{1,193},{65,1},{129,65},{193,129... | collective-permute-start | bytes 1572872 | tf_op jit(solution)/shard_map/ppermute | solution.py:28
  78.0 12.0 %collective-permute-start.6 = (bf16[256,1024]{1,0:T(8,128)(2,1)S(1)}, bf16[256,1024]{1,0:T(8,128)(2,1)S(1)}, u32[]{:S(2)}, u32[]{:S(2)}) collective-permute-start(bf16[256,1024]{1,0:T(8,128)(2,1)S(1)} %collective-permute-done.5), channel_id=1, source_target_pairs={{0,64},{64,128},{128,192},{192,0},{1,65},{65,129},{129,193},{193,1... | collective-permute-start | bytes 1572872 | tf_op jit(solution)/shard_map/ppermute | solution.py:25
  152.9 3.1 copy-start.10
  158.4 2.5 copy-start.1
  162.3 3.5 %collective-permute-start.7 = (bf16[512,1377]{0,1:T(8,128)(2,1)}, bf16[512,1377]{0,1:T(8,128)(2,1)}, u32[]{:S(2)}, u32[]{:S(2)}) collective-permute-start(bf16[512,1377]{0,1:T(8,128)(2,1)} %select_convert_fusion), channel_id=1, source_target_pairs={{0,1},{1,0},{2,3},{3,2},{4,5},{5,4},{6,7},{7,6},{8,9},{9,8},{10,11... | collective-permute-start | bytes 4230152 | tf_op jit(solution)/shard_map/ppermute | solution.py:72
  169.7 1.6 copy-start.3
  172.2 19.6 %collective-permute-start.8 = (bf16[256,1377]{0,1:T(8,128)(2,1)}, bf16[256,1377]{0,1:T(8,128)(2,1)}, u32[]{:S(2)}, u32[]{:S(2)}) collective-permute-start(bf16[256,1377]{0,1:T(8,128)(2,1)} %select_convert_fusion.1), channel_id=1, source_target_pairs={{0,2},{2,0},{4,6},{6,4},{1,3},{3,1},{5,7},{7,5},{8,10},{10,8},{12,... | collective-permute-start | bytes 2115080 | tf_op jit(solution)/shard_map/ppermute | solution.py:72
  194.1 17.2 %collective-permute-start.9 = (bf16[128,1377]{0,1:T(8,128)(2,1)S(1)}, bf16[128,1377]{0,1:T(8,128)(2,1)S(1)}, u32[]{:S(2)}, u32[]{:S(2)}) collective-permute-start(bf16[128,1377]{0,1:T(8,128)(2,1)S(1)} %select_convert_fusion.2), channel_id=1, source_target_pairs={{0,4},{2,6},{4,0},{6,2},{1,5},{3,7},{5,1},{7,3},{8,12},{10,14},{12... | collective-permute-start | bytes 1057544 | tf_op jit(solution)/shard_map/ppermute | solution.py:72
  211.4 17.8 %collective-permute-start.10 = (bf16[128,1377]{0,1:T(8,128)(2,1)S(1)}, bf16[128,1377]{0,1:T(8,128)(2,1)S(1)}, u32[]{:S(2)}, u32[]{:S(2)}) collective-permute-start(bf16[128,1377]{0,1:T(8,128)(2,1)S(1)} %add_convert_fusion), channel_id=1, source_target_pairs={{0,4},{2,6},{4,0},{6,2},{1,5},{3,7},{5,1},{7,3},{8,12},{10,14},{12... | collective-permute-start | bytes 1057544 | tf_op jit(solution)/shard_map/ppermute | solution.py:78
  229.4 19.4 %collective-permute-start.11 = (bf16[256,1377]{0,1:T(8,128)(2,1)S(1)}, bf16[256,1377]{0,1:T(8,128)(2,1)S(1)}, u32[]{:S(2)}, u32[]{:S(2)}) collective-permute-start(bf16[256,1377]{0,1:T(8,128)(2,1)S(1)} %maximum_select_fusion.2), channel_id=1, source_target_pairs={{0,2},{2,0},{4,6},{6,4},{1,3},{3,1},{5,7},{7,5},{8,10},{10,8},{12,... | collective-permute-start | bytes 2115080 | tf_op jit(solution)/shard_map/ppermute | solution.py:78
  249.1 3.5 %collective-permute-start.12 = (bf16[512,1377]{0,1:T(8,128)(2,1)S(1)}, bf16[512,1377]{0,1:T(8,128)(2,1)S(1)}, u32[]{:S(2)}, u32[]{:S(2)}) collective-permute-start(bf16[512,1377]{0,1:T(8,128)(2,1)S(1)} %maximum_select_fusion.1), channel_id=1, source_target_pairs={{0,1},{1,0},{2,3},{3,2},{4,5},{5,4},{6,7},{7,6},{8,9},{9,8},{10,11... | collective-permute-start | bytes 4230152 | tf_op jit(solution)/shard_map/ppermute | solution.py:78
  254.1 2.5 copy-start.2
  256.5 1.8 copy-start.4
  260.0 31.4 %all-to-all-start.1 = ((bf16[4,4,2,32,1024]{4,3,2,1,0:T(8,128)(2,1)}), bf16[4,4,2,32,1024]{4,3,2,1,0:T(8,128)(2,1)}, u32[]{:S(2)}, u32[]{:S(2)}) async-start(bf16[4,4,2,32,1024]{4,3,2,1,0:T(8,128)(2,1)} %bitcast.52), calls=%async_computation.1 | async-start | bytes 4194304 | tf_op jit(solution)/shard_map/all_to_all | solution.py:51
  294.3 13.4 %all-to-all-start.2 = ((bf16[4,2,32,1024]{3,2,1,0:T(8,128)(2,1)}), bf16[4,2,32,1024]{3,2,1,0:T(8,128)(2,1)}, u32[]{:S(2)}, u32[]{:S(2)}) async-start(bf16[4,2,32,1024]{3,2,1,0:T(8,128)(2,1)} %reduce_sum.83), calls=%async_computation.2 | async-start | bytes 1048576 | tf_op jit(solution)/shard_map/all_to_all | solution.py:51
  309.5 13.4 %all-to-all-start.3 = ((bf16[2,32,1024]{2,1,0:T(8,128)(2,1)}), bf16[2,32,1024]{2,1,0:T(8,128)(2,1)S(1)}, u32[]{:S(2)}, u32[]{:S(2)}) async-start(bf16[2,32,1024]{2,1,0:T(8,128)(2,1)} %reduce_sum.84), calls=%async_computation.3 | async-start | bytes 262144 | tf_op jit(solution)/shard_map/all_to_all | solution.py:51
  314.6 8.4 %copy-start.6 = (bf16[32,1024]{1,0:T(8,128)(2,1)S(1)}, bf16[32,1024]{1,0:T(8,128)(2,1)}, u32[]{:S(2)}) copy-start(bf16[32,1024]{1,0:T(8,128)(2,1)} %copy-done.5) | copy-start | bytes 196612
Sparse Core Ops, SparseCore 0:
  82.6 69.7 all-reduce.1

commit v7 on v6

--- a/solution.py
+++ b/solution.py
@@ -82,6 +82,11 @@
     return held
 
 
+def halves(rows, blocks):
+    shaped = rows.reshape((blocks, 2, rows.shape[0] // (2 * blocks)) + rows.shape[1:])
+    return jnp.swapaxes(shaped, 0, 1).reshape(rows.shape)
+
+
 def body(
     store_rows, source_shard, source_row, state_len, visits, gain, w_gate, w_up, w_down, upstream
 ):
@@ -135,11 +140,12 @@
     importance = jnp.log1p(visits.astype(f32))
     per_state = total_rows * importance / (state_len.astype(f32) * jnp.sum(importance))
     row_weight = jnp.sum(member * per_state[None, :], axis=1)
-    out_grad = (upstream.astype(f32) * row_weight[:, None]).astype(bf16)
+    out_grad = halves((upstream.astype(f32) * row_weight[:, None]).astype(bf16), count_dp)
     hidden_term = lax.dot_general(
         out_grad, w_down, (((1,), (1,)), ((), ())), preferred_element_type=f32
     ).astype(bf16)
     hidden_sum = lax.psum(hidden_term, MP)
+    train_rows = halves(train_rows, count_dp)
     hidden_sum, train_rows = lax.optimization_barrier((hidden_sum, train_rows))
     grad_hidden = hidden_sum.astype(f32)
 
@@ -149,17 +155,26 @@
     gate_term = jnp.dot(scaled, w_gate, preferred_element_type=f32)
     up_term = jnp.dot(scaled, w_up, preferred_element_type=f32)
     packed = jnp.concatenate([gate_term, up_term, squares[:, None]], axis=1).astype(bf16)
-    total = pair_allreduce(packed, MP).astype(f32)
-    gate_total = total[:, :hidden_dev]
-    up_total = total[:, hidden_dev : 2 * hidden_dev]
-    square_total = total[:, 2 * hidden_dev]
-    inverse = lax.rsqrt(square_total / D + epsilon)
-    gate_all = inverse[:, None] * gate_total
-    up_all = inverse[:, None] * up_total
-    hidden_all = (jax.nn.silu(gate_all) * up_all).astype(bf16)
-
-    down_part = jnp.dot(hidden_all, w_down, preferred_element_type=f32).astype(bf16)
-    down_block = staged_scatter(down_part, block_rows)
+    chunk = total_rows // 2
+    pieces = []
+    later = packed[chunk:]
+    for first in (0, chunk):
+        reduced = pair_allreduce(packed[:chunk] if first == 0 else later, MP)
+        if first == 0:
+            reduced, later = lax.optimization_barrier((reduced, later))
+        part_total = reduced.astype(f32)
+        part_inverse = lax.rsqrt(part_total[:, 2 * hidden_dev] / D + epsilon)
+        part_gate = part_inverse[:, None] * part_total[:, :hidden_dev]
+        part_up = part_inverse[:, None] * part_total[:, hidden_dev : 2 * hidden_dev]
+        part_hidden = (jax.nn.silu(part_gate) * part_up).astype(bf16)
+        down_part = jnp.dot(part_hidden, w_down, preferred_element_type=f32).astype(bf16)
+        down_rows = staged_scatter(down_part, block_rows // 2)
+        pieces.append((part_inverse, part_gate, part_up, part_hidden, down_rows))
+    inverse = jnp.concatenate([p[0] for p in pieces], axis=0)
+    gate_all = jnp.concatenate([p[1] for p in pieces], axis=0)
+    up_all = jnp.concatenate([p[2] for p in pieces], axis=0)
+    hidden_all = jnp.concatenate([p[3] for p in pieces], axis=0)
+    down_block = jnp.concatenate([p[4] for p in pieces], axis=0)
     layer_out = (own_rows.astype(f32) + down_block).astype(bf16)
 
     grad_down = lax.dot_general(

time: 332 us -> 380 us (1.14)
  blocking collectives: 0 us -> 23.5 us
  waiting for transfers between devices: 208 us -> 221 us
  starting transfers between devices: 46.8 us -> 59.7 us
  other arithmetic: 21.7 us -> 26.5 us
    all_to_all x0 -> x2, blocking collectives: none -> 23.5 us  [staged_scatter(): arrived = lax.all_to_all(held, name, 0, 0, tiled=True)]
    ppermute x3 -> x6, waiting for transfers between devices: 34.8 us -> 50.1 us  [pair_allreduce(): got = lax.ppermute(give.astype(part.dtype), name, pairs)]
    all_to_all x3 -> x4, waiting for transfers between devices: 27.8 us -> 21 us  [staged_scatter(): arrived = lax.all_to_all(held, name, 0, 0, tiled=True)]
    ppermute x3 -> x6, waiting for transfers between devices: 33.5 us -> 39.9 us  [pair_allreduce(): got = lax.ppermute(held, name, pairs)]
    ppermute x3 -> x6, starting transfers between devices: 7.09 us -> 13.2 us  [pair_allreduce(): got = lax.ppermute(held, name, pairs)]
    convert_element_type x2 -> x5, other arithmetic: 2.26 us -> 8.32 us  [the longest x2 4.18 us: body(): part_hidden = (jax.nn.silu(part_gate) * part_up).astype(bf16)]
    ppermute x3 -> x6, starting transfers between devices: 5.42 us -> 9.83 us  [pair_allreduce(): got = lax.ppermute(give.astype(part.dtype), name, pairs)]
    all_to_all x3 -> x4, starting transfers between devices: 13.6 us -> 15.9 us  [staged_scatter(): arrived = lax.all_to_all(held, name, 0, 0, tiled=True)]
  transfers between devices with their start and end apart: 18 -> 25, of which waited for: 16 -> 22; matrix products, arithmetic and copies ran while one was open for 7% -> 8% of each run, Pallas kernels for 0% -> 0%
where the time goes in v7:
time: 380 us; the launch traced here: 379 us
  waiting for transfers between devices  221 us (58%)
  starting transfers between devices  59.7 us (16%)
  other arithmetic  26.5 us (7%)
  matrix products  26 us (7%)
  blocking collectives  23.5 us (6%)
  between operations  14.7 us (4%)
  local copies, waits for them, and re-layouts  7.77 us (2%)
    psum x1, waiting for transfers between devices, body(): hidden_sum = lax.psum(hidden_term, MP)  60.2 us
    ppermute x6, waiting for transfers between devices, pair_allreduce(): got = lax.ppermute(give.astype(part.dtype), name, pairs)  50.1 us
    ppermute x6, waiting for transfers between devices, pair_allreduce(): got = lax.ppermute(held, name, pairs)  39.9 us
    ppermute x5, waiting for transfers between devices, ring_gather(): from_left = lax.ppermute(from_left, name, ahead)  33.8 us
    all_to_all x2, blocking collectives, staged_scatter(): arrived = lax.all_to_all(held, name, 0, 0, tiled=True)  23.5 us
    all_to_all x4, waiting for transfers between devices, staged_scatter(): arrived = lax.all_to_all(held, name, 0, 0, tiled=True)  21 us
    all_to_all x4, starting transfers between devices, staged_scatter(): arrived = lax.all_to_all(held, name, 0, 0, tiled=True)  15.9 us
    all_to_all x1, waiting for transfers between devices, body(): received = lax.all_to_all(outgoing, DP, 0, 0, tiled=True)  15.8 us
  transfers between devices with their start and end apart: 25, of which 22 were waited for; matrix products, arithmetic and copies ran while one was open for 8% of the time, Pallas kernels for 0%

profile of v7, /device:TPU:32, one launch (start us, length us, event | category | flops | bytes accessed | tf_op | source)
XLA Modules:
  0.0 378.9 jit_solution(15598469755401491306)
XLA Ops:
  12.1 13.2 %all-to-all-start = ((bf16[32,4,1024]{2,1,0:T(4,128)(2,1)}), bf16[32,4,1024]{2,1,0:T(4,128)(2,1)S(1)}, u32[]{:S(2)}, u32[]{:S(2)}) async-start(bf16[32,4,1024]{2,1,0:T(4,128)(2,1)} %all_to_all.26), calls=%async_computation | async-start | bytes 524288 | tf_op jit(solution)/shard_map/all_to_all | solution.py:120
  25.4 15.8 %all-to-all-done = bf16[32,4,1024]{2,1,0:T(4,128)(2,1)S(1)} async-done(((bf16[32,4,1024]{2,1,0:T(4,128)(2,1)}), bf16[32,4,1024]{2,1,0:T(4,128)(2,1)S(1)}, u32[]{:S(2)}, u32[]{:S(2)}) %all-to-all-start) | async-done | bytes 262176 | tf_op jit(solution)/shard_map/all_to_all | solution.py:120
  42.4 2.3 collective-permute-start
  44.8 2.2 collective-permute-done.1
  47.0 5.5 %collective-permute-done.2 = bf16[32,1024]{1,0:T(8,128)(2,1)S(1)} collective-permute-done((bf16[32,1024]{1,0:T(8,128)(2,1)S(1)}, bf16[32,1024]{1,0:T(8,128)(2,1)S(1)}, u32[]{:S(2)}, u32[]{:S(2)}) %collective-permute-start.2) | collective-permute-done | bytes 65568 | tf_op jit(solution)/shard_map/ppermute | solution.py:25
  54.1 10.8 %collective-permute-done.3 = bf16[128,1024]{1,0:T(8,128)(2,1)S(1)} collective-permute-done((bf16[128,1024]{1,0:T(8,128)(2,1)S(1)}, bf16[128,1024]{1,0:T(8,128)(2,1)S(1)}, u32[]{:S(2)}, u32[]{:S(2)}) %collective-permute-start.3) | collective-permute-done | bytes 262176 | tf_op jit(solution)/shard_map/ppermute | solution.py:25
  66.9 2.0 multiply_convert_fusion
  69.3 2.7 collective-permute-start.4
  72.0 6.2 %collective-permute-done.5 = bf16[256,1024]{1,0:T(8,128)(2,1)S(1)} collective-permute-done((bf16[256,1024]{1,0:T(8,128)(2,1)S(1)}, bf16[256,1024]{1,0:T(8,128)(2,1)S(1)}, u32[]{:S(2)}, u32[]{:S(2)}) %collective-permute-start.5) | collective-permute-done | bytes 524320 | tf_op jit(solution)/shard_map/ppermute | solution.py:25
  78.2 2.8 convolution_convert_fusion.5
  81.1 9.1 %collective-permute-done.6 = bf16[256,1024]{1,0:T(8,128)(2,1)S(1)} collective-permute-done((bf16[256,1024]{1,0:T(8,128)(2,1)S(1)}, bf16[256,1024]{1,0:T(8,128)(2,1)S(1)}, u32[]{:S(2)}, u32[]{:S(2)}) %collective-permute-start.6) | collective-permute-done | bytes 524320 | tf_op jit(solution)/shard_map/ppermute | solution.py:25
  90.8 60.2 %all-reduce.2.cloned.1.call-done = bf16[1024,688]{0,1:T(8,128)(2,1)} async-done(((bf16[1024,688]{0,1:T(8,128)(2,1)}), bf16[1024,688]{0,1:T(8,128)(2,1)}) %all-reduce.2.cloned.1.call-update) | async-done | bytes 1409040 | tf_op jit(solution)/shard_map/psum | solution.py:147
  159.4 2.2 collective-permute-done.7
  161.6 2.1 convert_add_fusion.1
  163.7 3.2 collective-permute-start.8
  166.9 8.6 %collective-permute-done.8 = bf16[128,1377]{0,1:T(8,128)(2,1)S(1)} collective-permute-done((bf16[128,1377]{0,1:T(8,128)(2,1)S(1)}, bf16[128,1377]{0,1:T(8,128)(2,1)S(1)}, u32[]{:S(2)}, u32[]{:S(2)}) %collective-permute-start.8) | collective-permute-done | bytes 352544 | tf_op jit(solution)/shard_map/ppermute | solution.py:72
  175.7 2.3 collective-permute-start.9
  178.1 14.8 %collective-permute-done.9 = bf16[64,1377]{0,1:T(8,128)(2,1)S(1)} collective-permute-done((bf16[64,1377]{0,1:T(8,128)(2,1)S(1)}, bf16[64,1377]{0,1:T(8,128)(2,1)S(1)}, u32[]{:S(2)}, u32[]{:S(2)}) %collective-permute-start.9) | collective-permute-done | bytes 176288 | tf_op jit(solution)/shard_map/ppermute | solution.py:72
  193.2 3.5 collective-permute-start.10
  196.6 14.3 %collective-permute-done.10 = bf16[64,1377]{0,1:T(8,128)(2,1)S(1)} collective-permute-done((bf16[64,1377]{0,1:T(8,128)(2,1)S(1)}, bf16[64,1377]{0,1:T(8,128)(2,1)S(1)}, u32[]{:S(2)}, u32[]{:S(2)}) %collective-permute-start.10) | collective-permute-done | bytes 176288 | tf_op jit(solution)/shard_map/ppermute | solution.py:78
  211.3 3.3 collective-permute-start.11
  214.6 8.5 %collective-permute-done.11 = bf16[128,1377]{0,1:T(8,128)(2,1)S(1)} collective-permute-done((bf16[128,1377]{0,1:T(8,128)(2,1)S(1)}, bf16[128,1377]{0,1:T(8,128)(2,1)S(1)}, u32[]{:S(2)}, u32[]{:S(2)}) %collective-permute-start.11) | collective-permute-done | bytes 352544 | tf_op jit(solution)/shard_map/ppermute | solution.py:78
  223.5 2.2 collective-permute-done.12
  227.0 2.0 collective-permute-done.13
  229.4 1.8 collective-permute-start.14
  231.6 8.2 %collective-permute-done.14 = bf16[128,1377]{0,1:T(8,128)(2,1)S(1)} collective-permute-done((bf16[128,1377]{0,1:T(8,128)(2,1)S(1)}, bf16[128,1377]{0,1:T(8,128)(2,1)S(1)}, u32[]{:S(2)}, u32[]{:S(2)}) %collective-permute-start.14) | collective-permute-done | bytes 352544 | tf_op jit(solution)/shard_map/ppermute | solution.py:72
  240.1 2.0 collective-permute-start.15
  242.1 14.3 %collective-permute-done.15 = bf16[64,1377]{0,1:T(8,128)(2,1)S(1)} collective-permute-done((bf16[64,1377]{0,1:T(8,128)(2,1)S(1)}, bf16[64,1377]{0,1:T(8,128)(2,1)S(1)}, u32[]{:S(2)}, u32[]{:S(2)}) %collective-permute-start.15) | collective-permute-done | bytes 176288 | tf_op jit(solution)/shard_map/ppermute | solution.py:72
  256.7 3.5 collective-permute-start.16
  260.1 2.1 multiply_convert_fusion.3
  262.3 12.8 %collective-permute-done.16 = bf16[64,1377]{0,1:T(8,128)(2,1)S(1)} collective-permute-done((bf16[64,1377]{0,1:T(8,128)(2,1)S(1)}, bf16[64,1377]{0,1:T(8,128)(2,1)S(1)}, u32[]{:S(2)}, u32[]{:S(2)}) %collective-permute-start.16) | collective-permute-done | bytes 176288 | tf_op jit(solution)/shard_map/ppermute | solution.py:78
  275.4 2.7 collective-permute-start.17
  280.2 4.3 %all-to-all-start.1 = ((bf16[4,4,2,16,1024]{4,3,2,1,0:T(8,128)(2,1)}), bf16[4,4,2,16,1024]{4,3,2,1,0:T(8,128)(2,1)S(1)}, u32[]{:S(2)}, u32[]{:S(2)}) async-start(bf16[4,4,2,16,1024]{4,3,2,1,0:T(8,128)(2,1)} %bitcast.59), calls=%async_computation.1 | async-start | bytes 2097152 | tf_op jit(solution)/shard_map/all_to_all | solution.py:51
  284.5 2.2 collective-permute-done.17
  288.1 11.4 %all-to-all-done.1 = bf16[4,4,2,16,1024]{4,3,2,1,0:T(8,128)(2,1)S(1)} async-done(((bf16[4,4,2,16,1024]{4,3,2,1,0:T(8,128)(2,1)}), bf16[4,4,2,16,1024]{4,3,2,1,0:T(8,128)(2,1)S(1)}, u32[]{:S(2)}, u32[]{:S(2)}) %all-to-all-start.1) | async-done | bytes 1048608 | tf_op jit(solution)/shard_map/all_to_all | solution.py:51
  299.7 10.7 %all_to_all.42 = bf16[4,2,16,1024]{3,2,1,0:T(8,128)(2,1)S(1)} all-to-all(bf16[4,2,16,1024]{3,2,1,0:T(8,128)(2,1)S(1)} %reduce_sum.116), channel_id=1, replica_groups=mesh['x'=4,'zh'=2,'y'=4,'zl'=4,'c'=2] {'x'}, dimensions={0} | all-to-all | bytes 524288 | tf_op jit(solution)/shard_map/all_to_all | solution.py:51
  310.5 12.8 %all_to_all.43 = bf16[2,16,1024]{2,1,0:T(8,128)(2,1)S(1)} all-to-all(bf16[2,16,1024]{2,1,0:T(8,128)(2,1)S(1)} %reduce_sum.117), channel_id=1, replica_groups=mesh['x'=4,'zh'=2,'y'=4,'zl'=4,'c'=2] {'zh'}, dimensions={0} | all-to-all | bytes 131072 | tf_op jit(solution)/shard_map/all_to_all | solution.py:51
  323.9 1.8 fusion.5
  325.7 2.1 multiply_convert_fusion.2
  329.8 4.2 %all-to-all-start.4 = ((bf16[4,4,2,16,1024]{4,3,2,1,0:T(8,128)(2,1)}), bf16[4,4,2,16,1024]{4,3,2,1,0:T(8,128)(2,1)}, u32[]{:S(2)}, u32[]{:S(2)}) async-start(bf16[4,4,2,16,1024]{4,3,2,1,0:T(8,128)(2,1)} %bitcast.73), calls=%async_computation.4 | async-start | bytes 2097152 | tf_op jit(solution)/shard_map/all_to_all | solution.py:51
  334.1 6.5 %convolution_convert_fusion.1 = bf16[1024,688]{0,1:T(8,128)(2,1)} fusion(f32[512,688]{0,1:T(8,128)} %get-tuple-element.17, f32[512,688]{0,1:T(8,128)} %get-tuple-element.14, bf16[1024,688]{0,1:T(8,128)(2,1)} %all-reduce.2.cloned.1.call-done, f32[512,688]{0,1:T(8,128)} %get-tuple-element.16, f32[512,688]{0,1:T(8,128)} %get-tuple-element.13, ...), kind=kOutput, calls=%fused_computation.15 | convolution fusion | flops 1456553984 | bytes 10559488 | tf_op jit(solution)/shard_map/dot_general | solution.py:192
  340.5 4.9 %all-to-all-done.4 = bf16[4,4,2,16,1024]{4,3,2,1,0:T(8,128)(2,1)} async-done(((bf16[4,4,2,16,1024]{4,3,2,1,0:T(8,128)(2,1)}), bf16[4,4,2,16,1024]{4,3,2,1,0:T(8,128)(2,1)}, u32[]{:S(2)}, u32[]{:S(2)}) %all-to-all-start.4) | async-done | bytes 1048608 | tf_op jit(solution)/shard_map/all_to_all | solution.py:51
  345.4 2.2 reduce_sum.119
  347.6 4.0 %all-to-all-start.5 = ((bf16[4,2,16,1024]{3,2,1,0:T(8,128)(2,1)}), bf16[4,2,16,1024]{3,2,1,0:T(8,128)(2,1)}, u32[]{:S(2)}, u32[]{:S(2)}) async-start(bf16[4,2,16,1024]{3,2,1,0:T(8,128)(2,1)} %reduce_sum.119), calls=%async_computation.5 | async-start | bytes 524288 | tf_op jit(solution)/shard_map/all_to_all | solution.py:51
  351.7 5.2 %convolution_convert_fusion = bf16[1024,688]{0,1:T(8,128)(2,1)} fusion(bf16[1024,688]{0,1:T(8,128)(2,1)} %all-reduce.2.cloned.1.call-done, f32[512,688]{0,1:T(8,128)} %get-tuple-element.16, f32[512,688]{0,1:T(8,128)} %get-tuple-element.13, f32[1024]{0:T(1024)S(1)} %pad_maximum_fusion.2, bf16[1024,1024]{1,0:T(8,128)(2,1)S(1)} %bitcast.67, ...), kind=kOutput, calls=%fused_computation.14 | convolution fusion | flops 1453031424 | bytes 7741440 | tf_op jit(solution)/shard_map/dot_general | solution.py:195
  360.0 3.3 all-to-all-start.6
  363.4 4.8 %convolution_convert_fusion.2 = bf16[688,1024]{1,0:T(8,128)(2,1)} fusion(bf16[1024,1024]{1,0:T(8,128)(2,1)} %bitcast.75, bf16[512,688]{0,1:T(8,128)(2,1)} %copy-done.7, bf16[512,688]{0,1:T(8,128)(2,1)} %copy-done.6), kind=kOutput, calls=%fused_computation.16 | convolution fusion | flops 1446363136 | bytes 4915200 | tf_op jit(solution)/shard_map/dot_general | solution.py:180
  368.1 3.2 all-to-all-done.6
  (127 shorter events, 33.7 us)
Async XLA Ops:
  7.2 71.0 %copy-start = (bf16[688,1024]{1,0:T(8,128)(2,1)S(1)}, bf16[688,1024]{1,0:T(8,128)(2,1)}, u32[]{:S(2)}) copy-start(bf16[688,1024]{1,0:T(8,128)(2,1)} %param.18) | copy-start | bytes 4227076
  10.0 43.5 %copy-start.13 = (s32[32]{0:T(128)S(1)}, s32[32]{0:T(128)}, u32[]{:S(2)}) copy-start(s32[32]{0:T(128)} %param.14) | copy-start | bytes 388
  12.1 53.8 %copy-start.12 = (s32[32]{0:T(128)S(1)}, s32[32]{0:T(128)}, u32[]{:S(2)}) copy-start(s32[32]{0:T(128)} %param.13) | copy-start | bytes 388
  12.1 29.0 %all-to-all-start = ((bf16[32,4,1024]{2,1,0:T(4,128)(2,1)}), bf16[32,4,1024]{2,1,0:T(4,128)(2,1)S(1)}, u32[]{:S(2)}, u32[]{:S(2)}) async-start(bf16[32,4,1024]{2,1,0:T(4,128)(2,1)} %all_to_all.26), calls=%async_computation | async-start | bytes 524288 | tf_op jit(solution)/shard_map/all_to_all | solution.py:120
  25.3 125.7 %all-reduce.2.cloned.1.call-start = ((), (), s32[]{:S(2)}) async-start(), calls=%async_computation.7 | async-start | bytes 2818048 | tf_op jit(solution)/shard_map/psum | solution.py:147
  41.4 23.4 %copy-start.8 = (bf16[32,1024]{1,0:T(8,128)(2,1)}, bf16[32,1024]{1,0:T(8,128)(2,1)S(1)}, u32[]{:S(2)}) copy-start(bf16[32,1024]{1,0:T(8,128)(2,1)S(1)} %get-tuple-element.21) | copy-start | bytes 196612
  41.5 5.6 %collective-permute-start.1 = (bf16[32,1024]{1,0:T(8,128)(2,1)S(1)}, bf16[32,1024]{1,0:T(8,128)(2,1)S(1)}, u32[]{:S(2)}, u32[]{:S(2)}) collective-permute-start(bf16[32,1024]{1,0:T(8,128)(2,1)S(1)} %get-tuple-element.21), channel_id=1, source_target_pairs={{0,8},{8,16},{16,24},{24,0},{1,9},{9,17},{17,25},{25,1},{2,10},{10... | collective-permute-start | bytes 196616 | tf_op jit(solution)/shard_map/ppermute | solution.py:25
  42.4 4.6 %collective-permute-start = (bf16[32,1024]{1,0:T(8,128)(2,1)S(1)}, bf16[32,1024]{1,0:T(8,128)(2,1)S(1)}, u32[]{:S(2)}, u32[]{:S(2)}) collective-permute-start(bf16[32,1024]{1,0:T(8,128)(2,1)S(1)} %get-tuple-element.21), channel_id=1, source_target_pairs={{0,24},{8,0},{16,8},{24,16},{1,25},{9,1},{17,9},{25,17},{2,26},{10... | collective-permute-start | bytes 196616 | tf_op jit(solution)/shard_map/ppermute | solution.py:28
  47.0 5.5 %collective-permute-start.2 = (bf16[32,1024]{1,0:T(8,128)(2,1)S(1)}, bf16[32,1024]{1,0:T(8,128)(2,1)S(1)}, u32[]{:S(2)}, u32[]{:S(2)}) collective-permute-start(bf16[32,1024]{1,0:T(8,128)(2,1)S(1)} %collective-permute-done.1), channel_id=1, source_target_pairs={{0,8},{8,16},{16,24},{24,0},{1,9},{9,17},{17,25},{25,1},{2,10},{10... | collective-permute-start | bytes 196616 | tf_op jit(solution)/shard_map/ppermute | solution.py:25
  52.6 12.3 %collective-permute-start.3 = (bf16[128,1024]{1,0:T(8,128)(2,1)S(1)}, bf16[128,1024]{1,0:T(8,128)(2,1)S(1)}, u32[]{:S(2)}, u32[]{:S(2)}) collective-permute-start(bf16[128,1024]{1,0:T(8,128)(2,1)S(1)} %bitcast.78), channel_id=1, source_target_pairs={{0,32},{32,0},{1,33},{33,1},{2,34},{34,2},{3,35},{35,3},{4,36},{36... | collective-permute-start | bytes 786440 | tf_op jit(solution)/shard_map/ppermute | solution.py:25
  65.2 12.9 %collective-permute-start.5 = (bf16[256,1024]{1,0:T(8,128)(2,1)S(1)}, bf16[256,1024]{1,0:T(8,128)(2,1)S(1)}, u32[]{:S(2)}, u32[]{:S(2)}) collective-permute-start(bf16[256,1024]{1,0:T(8,128)(2,1)S(1)} %bitcast.69), channel_id=1, source_target_pairs={{0,64},{64,128},{128,192},{192,0},{1,65},{65,129},{129,193},{193,1... | collective-permute-start | bytes 1572872 | tf_op jit(solution)/shard_map/ppermute | solution.py:25
  69.3 8.9 %copy-start.5 = (bf16[2,32,16,1024]{3,2,1,0:T(8,128)(2,1)}, bf16[2,32,16,1024]{3,2,1,0:T(8,128)(2,1)S(1)}, u32[]{:S(2)}) copy-start(bf16[2,32,16,1024]{3,2,1,0:T(8,128)(2,1)S(1)} %copy.26) | copy-start | bytes 6291460
  69.3 11.8 %collective-permute-start.4 = (bf16[256,1024]{1,0:T(8,128)(2,1)S(1)}, bf16[256,1024]{1,0:T(8,128)(2,1)S(1)}, u32[]{:S(2)}, u32[]{:S(2)}) collective-permute-start(bf16[256,1024]{1,0:T(8,128)(2,1)S(1)} %bitcast.70), channel_id=1, source_target_pairs={{0,192},{64,0},{128,64},{192,128},{1,193},{65,1},{129,65},{193,129... | collective-permute-start | bytes 1572872 | tf_op jit(solution)/shard_map/ppermute | solution.py:28
  78.2 12.0 %collective-permute-start.6 = (bf16[256,1024]{1,0:T(8,128)(2,1)S(1)}, bf16[256,1024]{1,0:T(8,128)(2,1)S(1)}, u32[]{:S(2)}, u32[]{:S(2)}) collective-permute-start(bf16[256,1024]{1,0:T(8,128)(2,1)S(1)} %collective-permute-done.5), channel_id=1, source_target_pairs={{0,64},{64,128},{128,192},{192,0},{1,65},{65,129},{129,193},{193,1... | collective-permute-start | bytes 1572872 | tf_op jit(solution)/shard_map/ppermute | solution.py:25
  78.2 2.8 copy-start.11
  90.8 63.2 %copy-start.2 = (bf16[2,32,16,1024]{3,2,1,0:T(8,128)(2,1)}, bf16[2,32,16,1024]{3,2,1,0:T(8,128)(2,1)S(1)}, u32[]{:S(2)}) copy-start(bf16[2,32,16,1024]{3,2,1,0:T(8,128)(2,1)S(1)} %copy.27) | copy-start | bytes 6291460
  151.0 1.4 copy-start.14
  152.4 1.7 copy-start.15
  157.5 1.6 copy-start.1
  159.3 2.3 collective-permute-start.7
  163.7 11.7 %collective-permute-start.8 = (bf16[128,1377]{0,1:T(8,128)(2,1)S(1)}, bf16[128,1377]{0,1:T(8,128)(2,1)S(1)}, u32[]{:S(2)}, u32[]{:S(2)}) collective-permute-start(bf16[128,1377]{0,1:T(8,128)(2,1)S(1)} %select_convert_fusion.5), channel_id=1, source_target_pairs={{0,2},{2,0},{4,6},{6,4},{1,3},{3,1},{5,7},{7,5},{8,10},{10,8},{12,... | collective-permute-start | bytes 1057544 | tf_op jit(solution)/shard_map/ppermute | solution.py:72
  175.7 17.2 %collective-permute-start.9 = (bf16[64,1377]{0,1:T(8,128)(2,1)S(1)}, bf16[64,1377]{0,1:T(8,128)(2,1)S(1)}, u32[]{:S(2)}, u32[]{:S(2)}) collective-permute-start(bf16[64,1377]{0,1:T(8,128)(2,1)S(1)} %select_convert_fusion.4), channel_id=1, source_target_pairs={{0,4},{2,6},{4,0},{6,2},{1,5},{3,7},{5,1},{7,3},{8,12},{10,14},{12... | collective-permute-start | bytes 528776 | tf_op jit(solution)/shard_map/ppermute | solution.py:72
  193.2 17.8 %collective-permute-start.10 = (bf16[64,1377]{0,1:T(8,128)(2,1)S(1)}, bf16[64,1377]{0,1:T(8,128)(2,1)S(1)}, u32[]{:S(2)}, u32[]{:S(2)}) collective-permute-start(bf16[64,1377]{0,1:T(8,128)(2,1)S(1)} %add_convert_fusion.1), channel_id=1, source_target_pairs={{0,4},{2,6},{4,0},{6,2},{1,5},{3,7},{5,1},{7,3},{8,12},{10,14},{12... | collective-permute-start | bytes 528776 | tf_op jit(solution)/shard_map/ppermute | solution.py:78
  211.3 14.7 %copy-start.4 = (bf16[512,1377]{0,1:T(8,128)(2,1)S(1)}, bf16[512,1377]{0,1:T(8,128)(2,1)}, u32[]{:S(2)}) copy-start(bf16[512,1377]{0,1:T(8,128)(2,1)} %get-tuple-element.10) | copy-start | bytes 4230148
  211.3 11.8 %collective-permute-start.11 = (bf16[128,1377]{0,1:T(8,128)(2,1)S(1)}, bf16[128,1377]{0,1:T(8,128)(2,1)S(1)}, u32[]{:S(2)}, u32[]{:S(2)}) collective-permute-start(bf16[128,1377]{0,1:T(8,128)(2,1)S(1)} %maximum_select_fusion.4), channel_id=1, source_target_pairs={{0,2},{2,0},{4,6},{6,4},{1,3},{3,1},{5,7},{7,5},{8,10},{10,8},{12,... | collective-permute-start | bytes 1057544 | tf_op jit(solution)/shard_map/ppermute | solution.py:78
  223.4 2.3 collective-permute-start.12
  226.5 2.5 collective-permute-start.13
  229.4 10.4 %collective-permute-start.14 = (bf16[128,1377]{0,1:T(8,128)(2,1)S(1)}, bf16[128,1377]{0,1:T(8,128)(2,1)S(1)}, u32[]{:S(2)}, u32[]{:S(2)}) collective-permute-start(bf16[128,1377]{0,1:T(8,128)(2,1)S(1)} %select_convert_fusion.3), channel_id=1, source_target_pairs={{0,2},{2,0},{4,6},{6,4},{1,3},{3,1},{5,7},{7,5},{8,10},{10,8},{12,... | collective-permute-start | bytes 1057544 | tf_op jit(solution)/shard_map/ppermute | solution.py:72
  240.1 16.3 %collective-permute-start.15 = (bf16[64,1377]{0,1:T(8,128)(2,1)S(1)}, bf16[64,1377]{0,1:T(8,128)(2,1)S(1)}, u32[]{:S(2)}, u32[]{:S(2)}) collective-permute-start(bf16[64,1377]{0,1:T(8,128)(2,1)S(1)} %select_convert_fusion.2), channel_id=1, source_target_pairs={{0,4},{2,6},{4,0},{6,2},{1,5},{3,7},{5,1},{7,3},{8,12},{10,14},{12... | collective-permute-start | bytes 528776 | tf_op jit(solution)/shard_map/ppermute | solution.py:72
  256.7 18.4 %collective-permute-start.16 = (bf16[64,1377]{0,1:T(8,128)(2,1)S(1)}, bf16[64,1377]{0,1:T(8,128)(2,1)S(1)}, u32[]{:S(2)}, u32[]{:S(2)}) collective-permute-start(bf16[64,1377]{0,1:T(8,128)(2,1)S(1)} %add_convert_fusion), channel_id=1, source_target_pairs={{0,4},{2,6},{4,0},{6,2},{1,5},{3,7},{5,1},{7,3},{8,12},{10,14},{12... | collective-permute-start | bytes 528776 | tf_op jit(solution)/shard_map/ppermute | solution.py:78
  262.3 16.9 %copy-start.6 = (bf16[512,688]{0,1:T(8,128)(2,1)}, bf16[512,688]{0,1:T(8,128)(2,1)S(1)}, u32[]{:S(2)}) copy-start(bf16[512,688]{0,1:T(8,128)(2,1)S(1)} %get-tuple-element.12) | copy-start | bytes 2113540
  275.4 11.3 %collective-permute-start.17 = (bf16[128,1377]{0,1:T(8,128)(2,1)S(1)}, bf16[128,1377]{0,1:T(8,128)(2,1)}, u32[]{:S(2)}, u32[]{:S(2)}) collective-permute-start(bf16[128,1377]{0,1:T(8,128)(2,1)S(1)} %maximum_select_fusion.5), channel_id=1, source_target_pairs={{0,2},{2,0},{4,6},{6,4},{1,3},{3,1},{5,7},{7,5},{8,10},{10,8},{12,... | collective-permute-start | bytes 1057544 | tf_op jit(solution)/shard_map/ppermute | solution.py:78
  280.2 19.3 %all-to-all-start.1 = ((bf16[4,4,2,16,1024]{4,3,2,1,0:T(8,128)(2,1)}), bf16[4,4,2,16,1024]{4,3,2,1,0:T(8,128)(2,1)S(1)}, u32[]{:S(2)}, u32[]{:S(2)}) async-start(bf16[4,4,2,16,1024]{4,3,2,1,0:T(8,128)(2,1)} %bitcast.59), calls=%async_computation.1 | async-start | bytes 2097152 | tf_op jit(solution)/shard_map/all_to_all | solution.py:51
  288.0 35.9 %collective-permute-start.18 = (bf16[256,1377]{0,1:T(8,128)(2,1)S(1)}, bf16[256,1377]{0,1:T(8,128)(2,1)}, u32[]{:S(2)}, u32[]{:S(2)}) collective-permute-start(bf16[256,1377]{0,1:T(8,128)(2,1)S(1)} %maximum_select_fusion.3), channel_id=1, source_target_pairs={{0,1},{1,0},{2,3},{3,2},{4,5},{5,4},{6,7},{7,6},{8,9},{9,8},{10,11... | collective-permute-start | bytes 2115080 | tf_op jit(solution)/shard_map/ppermute | solution.py:78
  327.7 1.0 copy-start.7
  328.8 5.3 %copy-start.3 = (bf16[2,32,16,1024]{3,2,1,0:T(8,128)(2,1)S(1)}, bf16[2,32,16,1024]{3,2,1,0:T(8,128)(2,1)}, u32[]{:S(2)}) copy-start(bf16[2,32,16,1024]{3,2,1,0:T(8,128)(2,1)} %copy-done.2) | copy-start | bytes 6291460
  329.8 15.6 %all-to-all-start.4 = ((bf16[4,4,2,16,1024]{4,3,2,1,0:T(8,128)(2,1)}), bf16[4,4,2,16,1024]{4,3,2,1,0:T(8,128)(2,1)}, u32[]{:S(2)}, u32[]{:S(2)}) async-start(bf16[4,4,2,16,1024]{4,3,2,1,0:T(8,128)(2,1)} %bitcast.73), calls=%async_computation.4 | async-start | bytes 2097152 | tf_op jit(solution)/shard_map/all_to_all | solution.py:51
  347.6 10.8 %all-to-all-start.5 = ((bf16[4,2,16,1024]{3,2,1,0:T(8,128)(2,1)}), bf16[4,2,16,1024]{3,2,1,0:T(8,128)(2,1)}, u32[]{:S(2)}, u32[]{:S(2)}) async-start(bf16[4,2,16,1024]{3,2,1,0:T(8,128)(2,1)} %reduce_sum.119), calls=%async_computation.5 | async-start | bytes 524288 | tf_op jit(solution)/shard_map/all_to_all | solution.py:51
  360.0 11.3 %all-to-all-start.6 = ((bf16[2,16,1024]{2,1,0:T(8,128)(2,1)}), bf16[2,16,1024]{2,1,0:T(8,128)(2,1)S(1)}, u32[]{:S(2)}, u32[]{:S(2)}) async-start(bf16[2,16,1024]{2,1,0:T(8,128)(2,1)} %reduce_sum.120), calls=%async_computation.6 | async-start | bytes 131072 | tf_op jit(solution)/shard_map/all_to_all | solution.py:51
  363.3 8.0 %copy-start.9 = (bf16[32,1024]{1,0:T(8,128)(2,1)S(1)}, bf16[32,1024]{1,0:T(8,128)(2,1)}, u32[]{:S(2)}) copy-start(bf16[32,1024]{1,0:T(8,128)(2,1)} %copy-done.8) | copy-start | bytes 196612
  363.3 8.0 %copy-start.10 = (f32[16,1024]{1,0:T(8,128)S(1)}, f32[16,1024]{1,0:T(8,128)}, u32[]{:S(2)}) copy-start(f32[16,1024]{1,0:T(8,128)} %convert_reduce_fusion.2) | copy-start | bytes 196612
Sparse Core Ops, SparseCore 0:
  81.1 69.8 all-reduce.1

commit v8 on v4

--- a/solution.py
+++ b/solution.py
@@ -54,6 +54,20 @@
     return total.reshape(block_rows, features)
 
 
+def core_split_sum(part):
+    core, chips = MP[1], MP[0]
+    upper = lax.axis_index(core) != 0
+    swap = [(0, 1), (1, 0)]
+    low, high = jnp.split(part, 2, axis=0)
+    got = lax.ppermute(jnp.where(upper, low, high), core, swap)
+    half = (jnp.where(upper, high, low).astype(jnp.float32) + got.astype(jnp.float32)).astype(part.dtype)
+    half = lax.psum(half, chips)
+    other = lax.ppermute(half, core, swap)
+    return jnp.where(
+        upper, jnp.concatenate([other, half], axis=0), jnp.concatenate([half, other], axis=0)
+    )
+
+
 def body(
     store_rows, source_shard, source_row, state_len, visits, gain, w_gate, w_up, w_down, upstream
 ):
@@ -95,9 +109,8 @@
     own_rows = jnp.dot(pick_in, received, preferred_element_type=f32).astype(bf16)
 
     train_rows = own_rows
-    for name in reversed(DP[1:]):
-        train_rows = lax.all_gather(train_rows, name, axis=0, tiled=True)
-    train_rows = ring_gather(train_rows, DP[0])
+    for name in reversed(DP):
+        train_rows = ring_gather(train_rows, name)
 
     row_ids = jnp.arange(total_rows, dtype=jnp.int32)
     ends = jnp.cumsum(state_len)
@@ -122,7 +135,7 @@
     gate_term = jnp.dot(scaled, w_gate, preferred_element_type=f32)
     up_term = jnp.dot(scaled, w_up, preferred_element_type=f32)
     packed = jnp.concatenate([gate_term, up_term, squares[:, None]], axis=1).astype(bf16)
-    total = lax.psum(packed, MP).astype(f32)
+    total = core_split_sum(packed).astype(f32)
     gate_total = total[:, :hidden_dev]
     up_total = total[:, hidden_dev : 2 * hidden_dev]
     square_total = total[:, 2 * hidden_dev]

time: 329 us -> 324 us (0.985)
  blocking collectives: 24.9 us -> 0 us
  waiting for transfers between devices: 209 us -> 223 us
  starting transfers between devices: 30.7 us -> 35.7 us
    all_gather x2 -> x0, blocking collectives: 24.9 us -> none  [body(): train_rows = lax.all_gather(train_rows, name, axis=0, tiled=True)]
    ppermute x2 -> x5, waiting for transfers between devices: 14.1 us -> 34.2 us  [ring_gather(): from_left = lax.ppermute(from_left, name, ahead)]
    psum x1, waiting for transfers between devices: 85.4 us -> 76.6 us  [core_split_sum(): half = lax.psum(half, chips)]
    ppermute x0 -> x2, waiting for transfers between devices: none -> 6.57 us  [the longest x1 3.4 us: core_split_sum(): other = lax.ppermute(half, core, swap)]
  transfers between devices with their start and end apart: 9 -> 15, of which waited for: 8 -> 13; matrix products, arithmetic and copies ran while one was open for 7% -> 7% of each run, Pallas kernels for 0% -> 0%
where the time goes in v8:
time: 324 us
  waiting for transfers between devices  223 us (69%)
  starting transfers between devices  35.7 us (11%)
  matrix products  29.4 us (9%)
  other arithmetic  15.5 us (5%)
  between operations  14.5 us (4%)
  local copies, waits for them, and re-layouts  5.87 us (2%)
    psum x1, waiting for transfers between devices, core_split_sum(): half = lax.psum(half, chips)  76.6 us
    psum x1, waiting for transfers between devices, body(): hidden_sum = lax.psum(hidden_term, MP)  61.8 us
    ppermute x5, waiting for transfers between devices, ring_gather(): from_left = lax.ppermute(from_left, name, ahead)  34.2 us
    all_to_all x3, waiting for transfers between devices, staged_scatter(): arrived = lax.all_to_all(held, name, 0, 0, tiled=True)  27.6 us
    all_to_all x1, waiting for transfers between devices, body(): received = lax.all_to_all(outgoing, DP, 0, 0, tiled=True)  15.8 us
    all_to_all x3, starting transfers between devices, staged_scatter(): arrived = lax.all_to_all(held, name, 0, 0, tiled=True)  14.7 us
    all_to_all x1, starting transfers between devices, body(): received = lax.all_to_all(outgoing, DP, 0, 0, tiled=True)  13 us
    dot_general x1, matrix products, body(): lax.dot_general(scaled, gate_delta, (((0,), (0,)), ((), ())), preferred_e...  6.69 us
  transfers between devices with their start and end apart: 15, of which 13 were waited for; matrix products, arithmetic and copies ran while one was open for 7% of the time, Pallas kernels for 0%

profile of v8, /device:TPU:32, one launch (start us, length us, event | category | flops | bytes accessed | tf_op | source)
XLA Modules:
  0.0 323.6 jit_solution(15501637994254532802)
XLA Ops:
  7.2 0.9 reshape.101
  8.1 0.8 convert_reduce_fusion
  8.9 0.7 broadcast_add_fusion
  10.0 1.3 convolution_convert_fusion.7
  11.3 0.8 all_to_all.17
  12.1 13.0 %all-to-all-start = ((bf16[32,4,1024]{2,1,0:T(4,128)(2,1)}), bf16[32,4,1024]{2,1,0:T(4,128)(2,1)S(1)}, u32[]{:S(2)}, u32[]{:S(2)}) async-start(bf16[32,4,1024]{2,1,0:T(4,128)(2,1)} %all_to_all.17), calls=%async_computation | async-start | bytes 524288 | tf_op jit(solution)/shard_map/all_to_all | solution.py:101
  25.3 15.8 %all-to-all-done = bf16[32,4,1024]{2,1,0:T(4,128)(2,1)S(1)} async-done(((bf16[32,4,1024]{2,1,0:T(4,128)(2,1)}), bf16[32,4,1024]{2,1,0:T(4,128)(2,1)S(1)}, u32[]{:S(2)}, u32[]{:S(2)}) %all-to-all-start) | async-done | bytes 262176 | tf_op jit(solution)/shard_map/all_to_all | solution.py:101
  41.3 1.0 collective-permute-start.1
  42.3 2.3 collective-permute-start
  44.6 2.2 collective-permute-done.1
  46.9 5.5 %collective-permute-done.2 = bf16[32,1024]{1,0:T(8,128)(2,1)S(1)} collective-permute-done((bf16[32,1024]{1,0:T(8,128)(2,1)S(1)}, bf16[32,1024]{1,0:T(8,128)(2,1)S(1)}, u32[]{:S(2)}, u32[]{:S(2)}) %collective-permute-start.2) | collective-permute-done | bytes 65568 | tf_op jit(solution)/shard_map/ppermute | solution.py:25
  52.5 0.9 collective-permute-start.3
  53.3 11.4 %collective-permute-done.3 = bf16[128,1024]{1,0:T(8,128)(2,1)S(1)} collective-permute-done((bf16[128,1024]{1,0:T(8,128)(2,1)S(1)}, bf16[128,1024]{1,0:T(8,128)(2,1)S(1)}, u32[]{:S(2)}, u32[]{:S(2)}) %collective-permute-start.3) | collective-permute-done | bytes 262176 | tf_op jit(solution)/shard_map/ppermute | solution.py:25
  64.7 0.4 fusion.9
  65.1 0.7 collective-permute-start.5
  66.1 0.6 fusion.19
  66.7 0.7 multiply_divide_fusion
  67.4 2.7 collective-permute-start.4
  70.2 7.9 %collective-permute-done.5 = bf16[256,1024]{1,0:T(8,128)(2,1)S(1)} collective-permute-done((bf16[256,1024]{1,0:T(8,128)(2,1)S(1)}, bf16[256,1024]{1,0:T(8,128)(2,1)S(1)}, u32[]{:S(2)}, u32[]{:S(2)}) %collective-permute-start.5) | collective-permute-done | bytes 524320 | tf_op jit(solution)/shard_map/ppermute | solution.py:25
  78.1 4.4 %convolution_convert_fusion.6 = bf16[1024,688]{0,1:T(8,128)(2,1)} fusion(bf16[688,1024]{1,0:T(8,128)(2,1)S(1)} %copy-done, bf16[1024,1024]{1,0:T(8,128)(2,1)} %param.19, f32[1024]{0:T(1024)S(1)} %select_reduce_fusion), kind=kOutput, calls=%fused_computation.23 | convolution fusion | flops 1446690816 | bytes 4919296 | tf_op jit(solution)/shard_map/dot_general | solution.py:125
  82.5 0.2 all-reduce.5.cloned.1.call-start
  82.9 7.2 %collective-permute-done.6 = bf16[256,1024]{1,0:T(8,128)(2,1)S(1)} collective-permute-done((bf16[256,1024]{1,0:T(8,128)(2,1)S(1)}, bf16[256,1024]{1,0:T(8,128)(2,1)S(1)}, u32[]{:S(2)}, u32[]{:S(2)}) %collective-permute-start.6) | collective-permute-done | bytes 524320 | tf_op jit(solution)/shard_map/ppermute | solution.py:25
  90.5 61.8 %all-reduce.3.cloned.1.call-done = bf16[1024,688]{0,1:T(8,128)(2,1)} async-done(((bf16[1024,688]{0,1:T(8,128)(2,1)}), bf16[1024,688]{0,1:T(8,128)(2,1)}) %all-reduce.3.cloned.1.call-update) | async-done | bytes 1409040 | tf_op jit(solution)/shard_map/psum | solution.py:128
  152.4 0.5 fusion.1
  152.8 3.1 convolution_convert_fusion.4
  156.0 1.7 convolution_convert_fusion.5
  157.7 0.3 pad_maximum_fusion
  158.2 3.2 collective-permute-done.7
  161.4 1.7 add_convert_fusion
  163.1 76.6 %all-reduce.5.cloned.1.call-done = bf16[512,1377]{0,1:T(8,128)(2,1)} async-done(((bf16[512,1377]{0,1:T(8,128)(2,1)}), bf16[512,1377]{0,1:T(8,128)(2,1)}) %all-reduce.5.cloned.1.call-update) | async-done | bytes 1410064 | tf_op jit(solution)/shard_map/psum | solution.py:64
  239.7 3.4 %collective-permute-done.8 = bf16[512,1377]{0,1:T(8,128)(2,1)S(1)} collective-permute-done((bf16[512,1377]{0,1:T(8,128)(2,1)}, bf16[512,1377]{0,1:T(8,128)(2,1)S(1)}, u32[]{:S(2)}, u32[]{:S(2)}) %collective-permute-start.8) | collective-permute-done | bytes 1410080 | tf_op jit(solution)/shard_map/ppermute | solution.py:65
  243.1 3.1 fusion.2
  246.2 0.8 multiply_convert_fusion.3
  247.1 1.6 copy-done.1
  248.7 1.8 convolution_convert_fusion
  250.5 1.6 copy.22
  252.1 4.7 %all-to-all-start.1 = ((bf16[4,4,2,32,1024]{4,3,2,1,0:T(8,128)(2,1)}), bf16[4,4,2,32,1024]{4,3,2,1,0:T(8,128)(2,1)}, u32[]{:S(2)}, u32[]{:S(2)}) async-start(bf16[4,4,2,32,1024]{4,3,2,1,0:T(8,128)(2,1)} %bitcast.52), calls=%async_computation.1 | async-start | bytes 4194304 | tf_op jit(solution)/shard_map/all_to_all | solution.py:51
  256.8 6.7 %convolution_convert_fusion.2 = bf16[1024,688]{0,1:T(8,128)(2,1)} fusion(bf16[1024,688]{0,1:T(8,128)(2,1)} %all-reduce.3.cloned.1.call-done, f32[1024,1377]{0,1:T(8,128)} %copy-done.1, f32[1024]{0:T(1024)S(1)} %bitcast.62, bf16[1024,1024]{1,0:T(8,128)(2,1)S(1)} %bitcast.50, f32[1024]{0:T(1024)S(1)} %convert_element_type.96), kind=kOutput, calls=%fused_computation.19 | convolution fusion | flops 1456553984 | bytes 10559488 | tf_op jit(solution)/shard_map/dot_general | solution.py:163
  263.5 20.1 %all-to-all-done.1 = bf16[4,4,2,32,1024]{4,3,2,1,0:T(8,128)(2,1)} async-done(((bf16[4,4,2,32,1024]{4,3,2,1,0:T(8,128)(2,1)}), bf16[4,4,2,32,1024]{4,3,2,1,0:T(8,128)(2,1)}, u32[]{:S(2)}, u32[]{:S(2)}) %all-to-all-start.1) | async-done | bytes 2097184 | tf_op jit(solution)/shard_map/all_to_all | solution.py:51
  283.5 2.9 reduce_sum.83
  286.5 4.2 %all-to-all-start.2 = ((bf16[4,2,32,1024]{3,2,1,0:T(8,128)(2,1)}), bf16[4,2,32,1024]{3,2,1,0:T(8,128)(2,1)}, u32[]{:S(2)}, u32[]{:S(2)}) async-start(bf16[4,2,32,1024]{3,2,1,0:T(8,128)(2,1)} %reduce_sum.83), calls=%async_computation.2 | async-start | bytes 1048576 | tf_op jit(solution)/shard_map/all_to_all | solution.py:51
  290.7 5.3 %convolution_convert_fusion.1 = bf16[1024,688]{0,1:T(8,128)(2,1)} fusion(bf16[1024,688]{0,1:T(8,128)(2,1)} %all-reduce.3.cloned.1.call-done, f32[1024,1377]{0,1:T(8,128)} %copy-done.1, f32[1024]{0:T(1024)S(1)} %bitcast.63, bf16[1024,1024]{1,0:T(8,128)(2,1)S(1)} %bitcast.51, f32[1024]{0:T(1024)S(1)} %convert_element_type.96), kind=kOutput, calls=%fused_computation.18 | convolution fusion | flops 1453031424 | bytes 7741440 | tf_op jit(solution)/shard_map/dot_general | solution.py:166
  296.0 3.9 %all-to-all-done.2 = bf16[4,2,32,1024]{3,2,1,0:T(8,128)(2,1)} async-done(((bf16[4,2,32,1024]{3,2,1,0:T(8,128)(2,1)}), bf16[4,2,32,1024]{3,2,1,0:T(8,128)(2,1)}, u32[]{:S(2)}, u32[]{:S(2)}) %all-to-all-start.2) | async-done | bytes 524320 | tf_op jit(solution)/shard_map/all_to_all | solution.py:51
  299.9 1.8 reduce_sum.84
  301.7 5.8 %all-to-all-start.3 = ((bf16[2,32,1024]{2,1,0:T(8,128)(2,1)}), bf16[2,32,1024]{2,1,0:T(8,128)(2,1)S(1)}, u32[]{:S(2)}, u32[]{:S(2)}) async-start(bf16[2,32,1024]{2,1,0:T(8,128)(2,1)} %reduce_sum.84), calls=%async_computation.3 | async-start | bytes 262144 | tf_op jit(solution)/shard_map/all_to_all | solution.py:51
  307.5 4.9 %convolution_convert_fusion.3 = bf16[688,1024]{1,0:T(8,128)(2,1)} fusion(bf16[1024,688]{0,1:T(8,128)(2,1)} %copy-done.2, bf16[1024,1024]{1,0:T(8,128)(2,1)} %param.19, f32[1024]{0:T(1024)S(1)} %select_reduce_fusion), kind=kOutput, calls=%fused_computation.20 | convolution fusion | flops 1446690816 | bytes 4919296 | tf_op jit(solution)/shard_map/dot_general | solution.py:151
  312.4 3.7 %all-to-all-done.3 = bf16[2,32,1024]{2,1,0:T(8,128)(2,1)S(1)} async-done(((bf16[2,32,1024]{2,1,0:T(8,128)(2,1)}), bf16[2,32,1024]{2,1,0:T(8,128)(2,1)S(1)}, u32[]{:S(2)}, u32[]{:S(2)}) %all-to-all-start.3) | async-done | bytes 131104 | tf_op jit(solution)/shard_map/all_to_all | solution.py:51
  316.1 0.7 add_convert_fusion.1
  (63 shorter events, 2.0 us)
Async XLA Ops:
  7.2 70.9 %copy-start = (bf16[688,1024]{1,0:T(8,128)(2,1)S(1)}, bf16[688,1024]{1,0:T(8,128)(2,1)}, u32[]{:S(2)}) copy-start(bf16[688,1024]{1,0:T(8,128)(2,1)} %param.18) | copy-start | bytes 4227076
  7.2 58.6 %copy-start.6 = (s32[32]{0:T(128)S(1)}, s32[32]{0:T(128)}, u32[]{:S(2)}) copy-start(s32[32]{0:T(128)} %param.13) | copy-start | bytes 388
  7.2 58.9 %copy-start.7 = (s32[32]{0:T(128)S(1)}, s32[32]{0:T(128)}, u32[]{:S(2)}) copy-start(s32[32]{0:T(128)} %param.14) | copy-start | bytes 388
  12.1 28.9 %all-to-all-start = ((bf16[32,4,1024]{2,1,0:T(4,128)(2,1)}), bf16[32,4,1024]{2,1,0:T(4,128)(2,1)S(1)}, u32[]{:S(2)}, u32[]{:S(2)}) async-start(bf16[32,4,1024]{2,1,0:T(4,128)(2,1)} %all_to_all.17), calls=%async_computation | async-start | bytes 524288 | tf_op jit(solution)/shard_map/all_to_all | solution.py:101
  25.2 127.2 %all-reduce.3.cloned.1.call-start = ((), (), s32[]{:S(2)}) async-start(), calls=%async_computation.4 | async-start | bytes 2818048 | tf_op jit(solution)/shard_map/psum | solution.py:128
  41.3 11.1 %copy-start.3 = (bf16[32,1024]{1,0:T(8,128)(2,1)}, bf16[32,1024]{1,0:T(8,128)(2,1)S(1)}, u32[]{:S(2)}) copy-start(bf16[32,1024]{1,0:T(8,128)(2,1)S(1)} %get-tuple-element.9) | copy-start | bytes 196612
  41.3 5.6 %collective-permute-start.1 = (bf16[32,1024]{1,0:T(8,128)(2,1)S(1)}, bf16[32,1024]{1,0:T(8,128)(2,1)S(1)}, u32[]{:S(2)}, u32[]{:S(2)}) collective-permute-start(bf16[32,1024]{1,0:T(8,128)(2,1)S(1)} %get-tuple-element.9), channel_id=1, source_target_pairs={{0,8},{8,16},{16,24},{24,0},{1,9},{9,17},{17,25},{25,1},{2,10},{10... | collective-permute-start | bytes 196616 | tf_op jit(solution)/shard_map/ppermute | solution.py:25
  42.3 4.6 %collective-permute-start = (bf16[32,1024]{1,0:T(8,128)(2,1)S(1)}, bf16[32,1024]{1,0:T(8,128)(2,1)S(1)}, u32[]{:S(2)}, u32[]{:S(2)}) collective-permute-start(bf16[32,1024]{1,0:T(8,128)(2,1)S(1)} %get-tuple-element.9), channel_id=1, source_target_pairs={{0,24},{8,0},{16,8},{24,16},{1,25},{9,1},{17,9},{25,17},{2,26},{10... | collective-permute-start | bytes 196616 | tf_op jit(solution)/shard_map/ppermute | solution.py:28
  46.9 5.5 %collective-permute-start.2 = (bf16[32,1024]{1,0:T(8,128)(2,1)S(1)}, bf16[32,1024]{1,0:T(8,128)(2,1)S(1)}, u32[]{:S(2)}, u32[]{:S(2)}) collective-permute-start(bf16[32,1024]{1,0:T(8,128)(2,1)S(1)} %collective-permute-done.1), channel_id=1, source_target_pairs={{0,8},{8,16},{16,24},{24,0},{1,9},{9,17},{17,25},{25,1},{2,10},{10... | collective-permute-start | bytes 196616 | tf_op jit(solution)/shard_map/ppermute | solution.py:25
  52.5 12.3 %collective-permute-start.3 = (bf16[128,1024]{1,0:T(8,128)(2,1)S(1)}, bf16[128,1024]{1,0:T(8,128)(2,1)S(1)}, u32[]{:S(2)}, u32[]{:S(2)}) collective-permute-start(bf16[128,1024]{1,0:T(8,128)(2,1)S(1)} %bitcast.58), channel_id=1, source_target_pairs={{0,32},{32,0},{1,33},{33,1},{2,34},{34,2},{3,35},{35,3},{4,36},{36... | collective-permute-start | bytes 786440 | tf_op jit(solution)/shard_map/ppermute | solution.py:25
  65.1 13.0 %collective-permute-start.5 = (bf16[256,1024]{1,0:T(8,128)(2,1)S(1)}, bf16[256,1024]{1,0:T(8,128)(2,1)S(1)}, u32[]{:S(2)}, u32[]{:S(2)}) collective-permute-start(bf16[256,1024]{1,0:T(8,128)(2,1)S(1)} %bitcast.53), channel_id=1, source_target_pairs={{0,64},{64,128},{128,192},{192,0},{1,65},{65,129},{129,193},{193,1... | collective-permute-start | bytes 1572872 | tf_op jit(solution)/shard_map/ppermute | solution.py:25
  67.4 15.3 %copy-start.5 = (bf16[1024]{0:T(1024)(128)(2,1)S(1)}, bf16[1024]{0:T(1024)(128)(2,1)}, u32[]{:S(2)}) copy-start(bf16[1024]{0:T(1024)(128)(2,1)} %param.15) | copy-start | bytes 6148
  67.4 15.4 %collective-permute-start.4 = (bf16[256,1024]{1,0:T(8,128)(2,1)S(1)}, bf16[256,1024]{1,0:T(8,128)(2,1)S(1)}, u32[]{:S(2)}, u32[]{:S(2)}) collective-permute-start(bf16[256,1024]{1,0:T(8,128)(2,1)S(1)} %bitcast.54), channel_id=1, source_target_pairs={{0,192},{64,0},{128,64},{192,128},{1,193},{65,1},{129,65},{193,129... | collective-permute-start | bytes 1572872 | tf_op jit(solution)/shard_map/ppermute | solution.py:28
  78.1 12.0 %collective-permute-start.6 = (bf16[256,1024]{1,0:T(8,128)(2,1)S(1)}, bf16[256,1024]{1,0:T(8,128)(2,1)S(1)}, u32[]{:S(2)}, u32[]{:S(2)}) collective-permute-start(bf16[256,1024]{1,0:T(8,128)(2,1)S(1)} %collective-permute-done.5), channel_id=1, source_target_pairs={{0,64},{64,128},{128,192},{192,0},{1,65},{65,129},{129,193},{193,1... | collective-permute-start | bytes 1572872 | tf_op jit(solution)/shard_map/ppermute | solution.py:25
  82.5 157.2 %all-reduce.5.cloned.1.call-start = ((), (), s32[]{:S(2)}) async-start(), calls=%async_computation.5 | async-start | bytes 2834432 | tf_op jit(solution)/shard_map/psum | solution.py:64
  152.8 3.1 copy-start.8
  158.1 3.3 %collective-permute-start.7 = (bf16[512,1377]{0,1:T(8,128)(2,1)S(1)}, bf16[512,1377]{0,1:T(8,128)(2,1)S(1)}, u32[]{:S(2)}, u32[]{:S(2)}) collective-permute-start(bf16[512,1377]{0,1:T(8,128)(2,1)S(1)} %broadcast_select_fusion), channel_id=1, source_target_pairs={{0,1},{1,0},{2,3},{3,2},{4,5},{5,4},{6,7},{7,6},{8,9},{9,8},{10,11... | collective-permute-start | bytes 4230152 | tf_op jit(solution)/shard_map/ppermute | solution.py:62
  239.7 3.4 %collective-permute-start.8 = (bf16[512,1377]{0,1:T(8,128)(2,1)}, bf16[512,1377]{0,1:T(8,128)(2,1)S(1)}, u32[]{:S(2)}, u32[]{:S(2)}) collective-permute-start(bf16[512,1377]{0,1:T(8,128)(2,1)} %all-reduce.5.cloned.1.call-done), channel_id=1, source_target_pairs={{0,1},{1,0},{2,3},{3,2},{4,5},{5,4},{6,7},{7,6},{8,9},{9,8},{10,11... | collective-permute-start | bytes 4230152 | tf_op jit(solution)/shard_map/ppermute | solution.py:65
  246.2 2.5 copy-start.1
  248.7 1.8 copy-start.2
  252.1 31.4 %all-to-all-start.1 = ((bf16[4,4,2,32,1024]{4,3,2,1,0:T(8,128)(2,1)}), bf16[4,4,2,32,1024]{4,3,2,1,0:T(8,128)(2,1)}, u32[]{:S(2)}, u32[]{:S(2)}) async-start(bf16[4,4,2,32,1024]{4,3,2,1,0:T(8,128)(2,1)} %bitcast.52), calls=%async_computation.1 | async-start | bytes 4194304 | tf_op jit(solution)/shard_map/all_to_all | solution.py:51
  286.5 13.4 %all-to-all-start.2 = ((bf16[4,2,32,1024]{3,2,1,0:T(8,128)(2,1)}), bf16[4,2,32,1024]{3,2,1,0:T(8,128)(2,1)}, u32[]{:S(2)}, u32[]{:S(2)}) async-start(bf16[4,2,32,1024]{3,2,1,0:T(8,128)(2,1)} %reduce_sum.83), calls=%async_computation.2 | async-start | bytes 1048576 | tf_op jit(solution)/shard_map/all_to_all | solution.py:51
  301.7 14.4 %all-to-all-start.3 = ((bf16[2,32,1024]{2,1,0:T(8,128)(2,1)}), bf16[2,32,1024]{2,1,0:T(8,128)(2,1)S(1)}, u32[]{:S(2)}, u32[]{:S(2)}) async-start(bf16[2,32,1024]{2,1,0:T(8,128)(2,1)} %reduce_sum.84), calls=%async_computation.3 | async-start | bytes 262144 | tf_op jit(solution)/shard_map/all_to_all | solution.py:51
  307.5 8.6 %copy-start.4 = (bf16[32,1024]{1,0:T(8,128)(2,1)S(1)}, bf16[32,1024]{1,0:T(8,128)(2,1)}, u32[]{:S(2)}) copy-start(bf16[32,1024]{1,0:T(8,128)(2,1)} %copy-done.3) | copy-start | bytes 196612
Sparse Core Ops, SparseCore 0:
  82.6 69.6 all-reduce.2
  163.2 76.4 all-reduce.4

commit v9 on v8

--- a/solution.py
+++ b/solution.py
@@ -56,16 +56,16 @@
 
 def core_split_sum(part):
     core, chips = MP[1], MP[0]
-    upper = lax.axis_index(core) != 0
+    here = lax.axis_index(core)
     swap = [(0, 1), (1, 0)]
-    low, high = jnp.split(part, 2, axis=0)
-    got = lax.ppermute(jnp.where(upper, low, high), core, swap)
-    half = (jnp.where(upper, high, low).astype(jnp.float32) + got.astype(jnp.float32)).astype(part.dtype)
+    rows = part.shape[0] // 2
+    got = lax.ppermute(lax.dynamic_slice_in_dim(part, (1 - here) * rows, rows, 0), core, swap)
+    keep = lax.dynamic_slice_in_dim(part, here * rows, rows, 0)
+    half = (keep.astype(jnp.float32) + got.astype(jnp.float32)).astype(part.dtype)
     half = lax.psum(half, chips)
     other = lax.ppermute(half, core, swap)
-    return jnp.where(
-        upper, jnp.concatenate([other, half], axis=0), jnp.concatenate([half, other], axis=0)
-    )
+    whole = lax.dynamic_update_slice_in_dim(jnp.zeros_like(part), half, here * rows, 0)
+    return lax.dynamic_update_slice_in_dim(whole, other, (1 - here) * rows, 0)
 
 
 def body(

time: 324 us -> 327 us (level)
  local copies, waits for them, and re-layouts: 5.87 us -> 10.5 us
where the time goes in v9:
time: 327 us; the launch traced here: 326 us
  waiting for transfers between devices  221 us (68%)
  starting transfers between devices  35.6 us (11%)
  matrix products  29.4 us (9%)
  other arithmetic  14.6 us (4%)
  between operations  14.5 us (4%)
  local copies, waits for them, and re-layouts  10.5 us (3%)
    psum x1, waiting for transfers between devices, core_split_sum(): half = lax.psum(half, chips)  76.6 us
    psum x1, waiting for transfers between devices, body(): hidden_sum = lax.psum(hidden_term, MP)  61.8 us
    ppermute x5, waiting for transfers between devices, ring_gather(): from_left = lax.ppermute(from_left, name, ahead)  34.2 us
    all_to_all x3, waiting for transfers between devices, staged_scatter(): arrived = lax.all_to_all(held, name, 0, 0, tiled=True)  27.6 us
    all_to_all x1, waiting for transfers between devices, body(): received = lax.all_to_all(outgoing, DP, 0, 0, tiled=True)  15.8 us
    all_to_all x3, starting transfers between devices, staged_scatter(): arrived = lax.all_to_all(held, name, 0, 0, tiled=True)  14.7 us
    all_to_all x1, starting transfers between devices, body(): received = lax.all_to_all(outgoing, DP, 0, 0, tiled=True)  13 us
    dot_general x1, matrix products, body(): lax.dot_general(scaled, gate_delta, (((0,), (0,)), ((), ())), preferred_e...  6.69 us
  transfers between devices with their start and end apart: 15, of which 13 were waited for; matrix products, arithmetic and copies ran while one was open for 7% of the time, Pallas kernels for 0%

profile of v9, /device:TPU:32, one launch (start us, length us, event | category | flops | bytes accessed | tf_op | source)
XLA Modules:
  0.0 326.0 jit_solution(8100898521966040456)
XLA Ops:
  7.2 0.9 reshape.101
  8.1 0.8 convert_reduce_fusion
  8.9 0.7 broadcast_add_fusion
  10.0 1.3 convolution_convert_fusion.7
  11.3 0.8 all_to_all.17
  12.1 13.0 %all-to-all-start = ((bf16[32,4,1024]{2,1,0:T(4,128)(2,1)}), bf16[32,4,1024]{2,1,0:T(4,128)(2,1)S(1)}, u32[]{:S(2)}, u32[]{:S(2)}) async-start(bf16[32,4,1024]{2,1,0:T(4,128)(2,1)} %all_to_all.17), calls=%async_computation | async-start | bytes 524288 | tf_op jit(solution)/shard_map/all_to_all | solution.py:101
  25.3 15.8 %all-to-all-done = bf16[32,4,1024]{2,1,0:T(4,128)(2,1)S(1)} async-done(((bf16[32,4,1024]{2,1,0:T(4,128)(2,1)}), bf16[32,4,1024]{2,1,0:T(4,128)(2,1)S(1)}, u32[]{:S(2)}, u32[]{:S(2)}) %all-to-all-start) | async-done | bytes 262176 | tf_op jit(solution)/shard_map/all_to_all | solution.py:101
  41.3 1.0 collective-permute-start.1
  42.3 2.3 collective-permute-start
  44.6 2.2 collective-permute-done.1
  46.9 5.5 %collective-permute-done.2 = bf16[32,1024]{1,0:T(8,128)(2,1)S(1)} collective-permute-done((bf16[32,1024]{1,0:T(8,128)(2,1)S(1)}, bf16[32,1024]{1,0:T(8,128)(2,1)S(1)}, u32[]{:S(2)}, u32[]{:S(2)}) %collective-permute-start.2) | collective-permute-done | bytes 65568 | tf_op jit(solution)/shard_map/ppermute | solution.py:25
  52.5 0.9 collective-permute-start.3
  53.3 11.4 %collective-permute-done.3 = bf16[128,1024]{1,0:T(8,128)(2,1)S(1)} collective-permute-done((bf16[128,1024]{1,0:T(8,128)(2,1)S(1)}, bf16[128,1024]{1,0:T(8,128)(2,1)S(1)}, u32[]{:S(2)}, u32[]{:S(2)}) %collective-permute-start.3) | collective-permute-done | bytes 262176 | tf_op jit(solution)/shard_map/ppermute | solution.py:25
  65.1 0.7 collective-permute-start.5
  66.1 0.6 fusion.18
  66.7 0.7 multiply_divide_fusion
  67.4 2.7 collective-permute-start.4
  70.2 7.9 %collective-permute-done.5 = bf16[256,1024]{1,0:T(8,128)(2,1)S(1)} collective-permute-done((bf16[256,1024]{1,0:T(8,128)(2,1)S(1)}, bf16[256,1024]{1,0:T(8,128)(2,1)S(1)}, u32[]{:S(2)}, u32[]{:S(2)}) %collective-permute-start.5) | collective-permute-done | bytes 524320 | tf_op jit(solution)/shard_map/ppermute | solution.py:25
  78.1 4.4 %convolution_convert_fusion.6 = bf16[1024,688]{0,1:T(8,128)(2,1)} fusion(bf16[688,1024]{1,0:T(8,128)(2,1)S(1)} %copy-done, bf16[1024,1024]{1,0:T(8,128)(2,1)} %param.19, f32[1024]{0:T(1024)S(1)} %select_reduce_fusion), kind=kOutput, calls=%fused_computation.21 | convolution fusion | flops 1446690816 | bytes 4919296 | tf_op jit(solution)/shard_map/dot_general | solution.py:125
  82.9 7.2 %collective-permute-done.6 = bf16[256,1024]{1,0:T(8,128)(2,1)S(1)} collective-permute-done((bf16[256,1024]{1,0:T(8,128)(2,1)S(1)}, bf16[256,1024]{1,0:T(8,128)(2,1)S(1)}, u32[]{:S(2)}, u32[]{:S(2)}) %collective-permute-start.6) | collective-permute-done | bytes 524320 | tf_op jit(solution)/shard_map/ppermute | solution.py:25
  90.5 61.8 %all-reduce.3.cloned.1.call-done = bf16[1024,688]{0,1:T(8,128)(2,1)} async-done(((bf16[1024,688]{0,1:T(8,128)(2,1)}), bf16[1024,688]{0,1:T(8,128)(2,1)}) %all-reduce.3.cloned.1.call-update) | async-done | bytes 1409040 | tf_op jit(solution)/shard_map/psum | solution.py:128
  152.4 0.5 fusion.1
  152.8 3.1 convolution_convert_fusion.4
  156.0 1.7 convolution_convert_fusion.5
  158.0 1.6 copy-done.2
  159.5 1.3 constant_dynamic-slice_fusion
  160.8 3.5 %collective-permute-done.7 = bf16[512,1377]{0,1:T(8,128)(2,1)} collective-permute-done((bf16[512,1377]{0,1:T(8,128)(2,1)}, bf16[512,1377]{0,1:T(8,128)(2,1)}, u32[]{:S(2)}, u32[]{:S(2)}) %collective-permute-start.7) | collective-permute-done | bytes 1410080 | tf_op jit(solution)/shard_map/ppermute | solution.py:62
  164.3 3.3 %add_convert_fusion = bf16[512,1377]{0,1:T(8,128)(2,1)} fusion(bf16[512,1377]{0,1:T(8,128)(2,1)} %collective-permute-done.7, bf16[1024,1377]{0,1:T(8,128)(2,1)} %copy-done.2, s32[]{:T(128)S(6)} %select_n.58), kind=kLoop, calls=%fused_computation.6 | loop fusion | flops 2820096 | bytes 4230148 | tf_op jit(solution)/shard_map/convert_element_type | solution.py:64
  167.6 76.6 %all-reduce.5.cloned.1.call-done = bf16[512,1377]{0,1:T(8,128)(2,1)} async-done(((bf16[512,1377]{0,1:T(8,128)(2,1)}), bf16[512,1377]{0,1:T(8,128)(2,1)}) %all-reduce.5.cloned.1.call-update) | async-done | bytes 1410064 | tf_op jit(solution)/shard_map/psum | solution.py:65
  244.6 1.0 copy-done.3
  245.8 1.8 collective-permute-done.8
  247.8 0.7 convert_element_type.101
  248.6 0.8 multiply_convert_fusion.3
  249.4 1.6 copy-done.1
  251.0 1.8 convolution_convert_fusion
  252.9 1.6 copy.22
  254.5 4.7 %all-to-all-start.1 = ((bf16[4,4,2,32,1024]{4,3,2,1,0:T(8,128)(2,1)}), bf16[4,4,2,32,1024]{4,3,2,1,0:T(8,128)(2,1)}, u32[]{:S(2)}, u32[]{:S(2)}) async-start(bf16[4,4,2,32,1024]{4,3,2,1,0:T(8,128)(2,1)} %bitcast.52), calls=%async_computation.1 | async-start | bytes 4194304 | tf_op jit(solution)/shard_map/all_to_all | solution.py:51
  259.1 6.7 %convolution_convert_fusion.2 = bf16[1024,688]{0,1:T(8,128)(2,1)} fusion(bf16[1024,688]{0,1:T(8,128)(2,1)} %all-reduce.3.cloned.1.call-done, f32[1024,1377]{0,1:T(8,128)} %copy-done.1, f32[1024]{0:T(1024)S(1)} %bitcast.62, bf16[1024,1024]{1,0:T(8,128)(2,1)S(1)} %bitcast.50, f32[1024]{0:T(1024)S(1)} %convert_element_type.96), kind=kOutput, calls=%fused_computation.17 | convolution fusion | flops 1456553984 | bytes 10559488 | tf_op jit(solution)/shard_map/dot_general | solution.py:163
  265.8 20.1 %all-to-all-done.1 = bf16[4,4,2,32,1024]{4,3,2,1,0:T(8,128)(2,1)} async-done(((bf16[4,4,2,32,1024]{4,3,2,1,0:T(8,128)(2,1)}), bf16[4,4,2,32,1024]{4,3,2,1,0:T(8,128)(2,1)}, u32[]{:S(2)}, u32[]{:S(2)}) %all-to-all-start.1) | async-done | bytes 2097184 | tf_op jit(solution)/shard_map/all_to_all | solution.py:51
  285.9 2.9 reduce_sum.83
  288.8 4.2 %all-to-all-start.2 = ((bf16[4,2,32,1024]{3,2,1,0:T(8,128)(2,1)}), bf16[4,2,32,1024]{3,2,1,0:T(8,128)(2,1)}, u32[]{:S(2)}, u32[]{:S(2)}) async-start(bf16[4,2,32,1024]{3,2,1,0:T(8,128)(2,1)} %reduce_sum.83), calls=%async_computation.2 | async-start | bytes 1048576 | tf_op jit(solution)/shard_map/all_to_all | solution.py:51
  293.1 5.3 %convolution_convert_fusion.1 = bf16[1024,688]{0,1:T(8,128)(2,1)} fusion(bf16[1024,688]{0,1:T(8,128)(2,1)} %all-reduce.3.cloned.1.call-done, f32[1024,1377]{0,1:T(8,128)} %copy-done.1, f32[1024]{0:T(1024)S(1)} %bitcast.63, bf16[1024,1024]{1,0:T(8,128)(2,1)S(1)} %bitcast.51, f32[1024]{0:T(1024)S(1)} %convert_element_type.96), kind=kOutput, calls=%fused_computation.16 | convolution fusion | flops 1453031424 | bytes 7741440 | tf_op jit(solution)/shard_map/dot_general | solution.py:166
  298.4 3.9 %all-to-all-done.2 = bf16[4,2,32,1024]{3,2,1,0:T(8,128)(2,1)} async-done(((bf16[4,2,32,1024]{3,2,1,0:T(8,128)(2,1)}), bf16[4,2,32,1024]{3,2,1,0:T(8,128)(2,1)}, u32[]{:S(2)}, u32[]{:S(2)}) %all-to-all-start.2) | async-done | bytes 524320 | tf_op jit(solution)/shard_map/all_to_all | solution.py:51
  302.3 1.8 reduce_sum.84
  304.1 5.8 %all-to-all-start.3 = ((bf16[2,32,1024]{2,1,0:T(8,128)(2,1)}), bf16[2,32,1024]{2,1,0:T(8,128)(2,1)S(1)}, u32[]{:S(2)}, u32[]{:S(2)}) async-start(bf16[2,32,1024]{2,1,0:T(8,128)(2,1)} %reduce_sum.84), calls=%async_computation.3 | async-start | bytes 262144 | tf_op jit(solution)/shard_map/all_to_all | solution.py:51
  309.9 4.9 %convolution_convert_fusion.3 = bf16[688,1024]{1,0:T(8,128)(2,1)} fusion(bf16[1024,688]{0,1:T(8,128)(2,1)} %copy-done.4, bf16[1024,1024]{1,0:T(8,128)(2,1)} %param.19, f32[1024]{0:T(1024)S(1)} %select_reduce_fusion), kind=kOutput, calls=%fused_computation.18 | convolution fusion | flops 1446690816 | bytes 4919296 | tf_op jit(solution)/shard_map/dot_general | solution.py:151
  314.7 3.7 %all-to-all-done.3 = bf16[2,32,1024]{2,1,0:T(8,128)(2,1)S(1)} async-done(((bf16[2,32,1024]{2,1,0:T(8,128)(2,1)}), bf16[2,32,1024]{2,1,0:T(8,128)(2,1)S(1)}, u32[]{:S(2)}, u32[]{:S(2)}) %all-to-all-start.3) | async-done | bytes 131104 | tf_op jit(solution)/shard_map/all_to_all | solution.py:51
  318.5 0.7 add_convert_fusion.1
  (70 shorter events, 3.4 us)
Async XLA Ops:
  7.2 70.9 %copy-start = (bf16[688,1024]{1,0:T(8,128)(2,1)S(1)}, bf16[688,1024]{1,0:T(8,128)(2,1)}, u32[]{:S(2)}) copy-start(bf16[688,1024]{1,0:T(8,128)(2,1)} %param.18) | copy-start | bytes 4227076
  7.2 58.6 %copy-start.8 = (s32[32]{0:T(128)S(1)}, s32[32]{0:T(128)}, u32[]{:S(2)}) copy-start(s32[32]{0:T(128)} %param.13) | copy-start | bytes 388
  7.2 58.9 %copy-start.9 = (s32[32]{0:T(128)S(1)}, s32[32]{0:T(128)}, u32[]{:S(2)}) copy-start(s32[32]{0:T(128)} %param.14) | copy-start | bytes 388
  12.1 28.9 %all-to-all-start = ((bf16[32,4,1024]{2,1,0:T(4,128)(2,1)}), bf16[32,4,1024]{2,1,0:T(4,128)(2,1)S(1)}, u32[]{:S(2)}, u32[]{:S(2)}) async-start(bf16[32,4,1024]{2,1,0:T(4,128)(2,1)} %all_to_all.17), calls=%async_computation | async-start | bytes 524288 | tf_op jit(solution)/shard_map/all_to_all | solution.py:101
  25.2 127.2 %all-reduce.3.cloned.1.call-start = ((), (), s32[]{:S(2)}) async-start(), calls=%async_computation.4 | async-start | bytes 2818048 | tf_op jit(solution)/shard_map/psum | solution.py:128
  41.3 11.1 %copy-start.5 = (bf16[32,1024]{1,0:T(8,128)(2,1)}, bf16[32,1024]{1,0:T(8,128)(2,1)S(1)}, u32[]{:S(2)}) copy-start(bf16[32,1024]{1,0:T(8,128)(2,1)S(1)} %get-tuple-element.9) | copy-start | bytes 196612
  41.3 5.6 %collective-permute-start.1 = (bf16[32,1024]{1,0:T(8,128)(2,1)S(1)}, bf16[32,1024]{1,0:T(8,128)(2,1)S(1)}, u32[]{:S(2)}, u32[]{:S(2)}) collective-permute-start(bf16[32,1024]{1,0:T(8,128)(2,1)S(1)} %get-tuple-element.9), channel_id=1, source_target_pairs={{0,8},{8,16},{16,24},{24,0},{1,9},{9,17},{17,25},{25,1},{2,10},{10... | collective-permute-start | bytes 196616 | tf_op jit(solution)/shard_map/ppermute | solution.py:25
  42.3 4.6 %collective-permute-start = (bf16[32,1024]{1,0:T(8,128)(2,1)S(1)}, bf16[32,1024]{1,0:T(8,128)(2,1)S(1)}, u32[]{:S(2)}, u32[]{:S(2)}) collective-permute-start(bf16[32,1024]{1,0:T(8,128)(2,1)S(1)} %get-tuple-element.9), channel_id=1, source_target_pairs={{0,24},{8,0},{16,8},{24,16},{1,25},{9,1},{17,9},{25,17},{2,26},{10... | collective-permute-start | bytes 196616 | tf_op jit(solution)/shard_map/ppermute | solution.py:28
  46.9 5.5 %collective-permute-start.2 = (bf16[32,1024]{1,0:T(8,128)(2,1)S(1)}, bf16[32,1024]{1,0:T(8,128)(2,1)S(1)}, u32[]{:S(2)}, u32[]{:S(2)}) collective-permute-start(bf16[32,1024]{1,0:T(8,128)(2,1)S(1)} %collective-permute-done.1), channel_id=1, source_target_pairs={{0,8},{8,16},{16,24},{24,0},{1,9},{9,17},{17,25},{25,1},{2,10},{10... | collective-permute-start | bytes 196616 | tf_op jit(solution)/shard_map/ppermute | solution.py:25
  52.5 12.3 %collective-permute-start.3 = (bf16[128,1024]{1,0:T(8,128)(2,1)S(1)}, bf16[128,1024]{1,0:T(8,128)(2,1)S(1)}, u32[]{:S(2)}, u32[]{:S(2)}) collective-permute-start(bf16[128,1024]{1,0:T(8,128)(2,1)S(1)} %bitcast.58), channel_id=1, source_target_pairs={{0,32},{32,0},{1,33},{33,1},{2,34},{34,2},{3,35},{35,3},{4,36},{36... | collective-permute-start | bytes 786440 | tf_op jit(solution)/shard_map/ppermute | solution.py:25
  65.1 13.0 %collective-permute-start.5 = (bf16[256,1024]{1,0:T(8,128)(2,1)S(1)}, bf16[256,1024]{1,0:T(8,128)(2,1)S(1)}, u32[]{:S(2)}, u32[]{:S(2)}) collective-permute-start(bf16[256,1024]{1,0:T(8,128)(2,1)S(1)} %bitcast.53), channel_id=1, source_target_pairs={{0,64},{64,128},{128,192},{192,0},{1,65},{65,129},{129,193},{193,1... | collective-permute-start | bytes 1572872 | tf_op jit(solution)/shard_map/ppermute | solution.py:25
  67.4 15.3 %copy-start.7 = (bf16[1024]{0:T(1024)(128)(2,1)S(1)}, bf16[1024]{0:T(1024)(128)(2,1)}, u32[]{:S(2)}) copy-start(bf16[1024]{0:T(1024)(128)(2,1)} %param.15) | copy-start | bytes 6148
  67.4 15.4 %collective-permute-start.4 = (bf16[256,1024]{1,0:T(8,128)(2,1)S(1)}, bf16[256,1024]{1,0:T(8,128)(2,1)S(1)}, u32[]{:S(2)}, u32[]{:S(2)}) collective-permute-start(bf16[256,1024]{1,0:T(8,128)(2,1)S(1)} %bitcast.54), channel_id=1, source_target_pairs={{0,192},{64,0},{128,64},{192,128},{1,193},{65,1},{129,65},{193,129... | collective-permute-start | bytes 1572872 | tf_op jit(solution)/shard_map/ppermute | solution.py:28
  78.1 12.0 %collective-permute-start.6 = (bf16[256,1024]{1,0:T(8,128)(2,1)S(1)}, bf16[256,1024]{1,0:T(8,128)(2,1)S(1)}, u32[]{:S(2)}, u32[]{:S(2)}) collective-permute-start(bf16[256,1024]{1,0:T(8,128)(2,1)S(1)} %collective-permute-done.5), channel_id=1, source_target_pairs={{0,64},{64,128},{128,192},{192,0},{1,65},{65,129},{129,193},{193,1... | collective-permute-start | bytes 1572872 | tf_op jit(solution)/shard_map/ppermute | solution.py:25
  82.5 161.7 %all-reduce.5.cloned.1.call-start = ((), (), s32[]{:S(2)}) async-start(), calls=%async_computation.5 | async-start | bytes 2834432 | tf_op jit(solution)/shard_map/psum | solution.py:65
  152.8 3.1 copy-start.10
  157.9 1.6 copy-start.2
  160.8 3.5 %collective-permute-start.7 = (bf16[512,1377]{0,1:T(8,128)(2,1)}, bf16[512,1377]{0,1:T(8,128)(2,1)}, u32[]{:S(2)}, u32[]{:S(2)}) collective-permute-start(bf16[512,1377]{0,1:T(8,128)(2,1)} %constant_dynamic-slice_fusion), channel_id=1, source_target_pairs={{0,1},{1,0},{2,3},{3,2},{4,5},{5,4},{6,7},{7,6},{8,9},{9,8},{10,11... | collective-permute-start | bytes 4230152 | tf_op jit(solution)/shard_map/ppermute | solution.py:62
  244.2 1.4 copy-start.3
  244.2 3.4 %collective-permute-start.8 = (bf16[512,1377]{0,1:T(8,128)(2,1)}, bf16[512,1377]{0,1:T(8,128)(2,1)S(1)}, u32[]{:S(2)}, u32[]{:S(2)}) collective-permute-start(bf16[512,1377]{0,1:T(8,128)(2,1)} %all-reduce.5.cloned.1.call-done), channel_id=1, source_target_pairs={{0,1},{1,0},{2,3},{3,2},{4,5},{5,4},{6,7},{7,6},{8,9},{9,8},{10,11... | collective-permute-start | bytes 4230152 | tf_op jit(solution)/shard_map/ppermute | solution.py:66
  248.6 2.5 copy-start.1
  251.0 1.8 copy-start.4
  254.5 31.4 %all-to-all-start.1 = ((bf16[4,4,2,32,1024]{4,3,2,1,0:T(8,128)(2,1)}), bf16[4,4,2,32,1024]{4,3,2,1,0:T(8,128)(2,1)}, u32[]{:S(2)}, u32[]{:S(2)}) async-start(bf16[4,4,2,32,1024]{4,3,2,1,0:T(8,128)(2,1)} %bitcast.52), calls=%async_computation.1 | async-start | bytes 4194304 | tf_op jit(solution)/shard_map/all_to_all | solution.py:51
  288.8 13.4 %all-to-all-start.2 = ((bf16[4,2,32,1024]{3,2,1,0:T(8,128)(2,1)}), bf16[4,2,32,1024]{3,2,1,0:T(8,128)(2,1)}, u32[]{:S(2)}, u32[]{:S(2)}) async-start(bf16[4,2,32,1024]{3,2,1,0:T(8,128)(2,1)} %reduce_sum.83), calls=%async_computation.2 | async-start | bytes 1048576 | tf_op jit(solution)/shard_map/all_to_all | solution.py:51
  304.1 14.4 %all-to-all-start.3 = ((bf16[2,32,1024]{2,1,0:T(8,128)(2,1)}), bf16[2,32,1024]{2,1,0:T(8,128)(2,1)S(1)}, u32[]{:S(2)}, u32[]{:S(2)}) async-start(bf16[2,32,1024]{2,1,0:T(8,128)(2,1)} %reduce_sum.84), calls=%async_computation.3 | async-start | bytes 262144 | tf_op jit(solution)/shard_map/all_to_all | solution.py:51
  309.9 8.6 %copy-start.6 = (bf16[32,1024]{1,0:T(8,128)(2,1)S(1)}, bf16[32,1024]{1,0:T(8,128)(2,1)}, u32[]{:S(2)}) copy-start(bf16[32,1024]{1,0:T(8,128)(2,1)} %copy-done.5) | copy-start | bytes 196612
Sparse Core Ops, SparseCore 0:
  82.6 69.6 all-reduce.2
  167.7 76.4 all-reduce.4
